TPU v7x, 256 devices: a whole 4x4x8 slice. The times are simulated.
256 devices in a mesh: req: 8 (over z), exp: 8 (over y, core), hid: 4 (over x).
Axes of the slice: x: 4, y: 4, z: 8, core: 2. Of those that a mesh axis runs over, the one named last changes fastest.
Arguments:
- layer_input_rows: bfloat16 [16384, 1536], P(('req', 'exp')), may hold values from -6 to 6
- attention_norm_gain: float32 [1536], replicated
- query_weight: bfloat16 [1536, 1536], P(None, 'hid'), may hold values from -1 to 1
- key_weight: bfloat16 [1536, 512], P(None, 'hid'), may hold values from -1 to 1
- value_weight: bfloat16 [1536, 512], P(None, 'hid'), may hold values from -0.15625 to 0.15625
- attention_output_weight: bfloat16 [1536, 1536], P('hid'), may hold values from -0.15625 to 0.15625
- query_down_factor: bfloat16 [64, 1536, 16], P(('req', 'exp')), may hold values from -0.15625 to 0.15625
- query_up_factor: bfloat16 [64, 16, 1536], P(('req', 'exp')), may hold values from -1.5 to 1.5
- value_down_factor: bfloat16 [64, 1536, 16], P(('req', 'exp')), may hold values from -0.15625 to 0.15625
- value_up_factor: bfloat16 [64, 16, 512], P(('req', 'exp')), may hold values from -1.5 to 1.5
- lengths: int32 [8, 4], P('req'), may hold values from 1 to 1024, 2048 in all within a row
- request_adapter: int32 [8, 4], replicated, may hold values from 0 to 63
- adapter_home_row: int32 [64], replicated, may hold values from 0 to 63, each once
- expert_norm_gain: float32 [1536], replicated, may hold values from 0.4 to 1.6
- routes: int32 [16384, 8], P(('req', 'exp', 'hid')), may hold values from 0 to 39, all different within a row; in each aligned block of 64 rows (0 to 63, 64 to 127, ...) at most 16 rows name the same one
- router_expert_weight: float32 [16384, 8], P(('req', 'exp', 'hid')), may hold values from 0.1 to 0.5
- expert_gate_weight: bfloat16 [40, 1536, 512], P('exp', None, 'hid'), may hold values from -0.15625 to 0.15625
- expert_up_weight: bfloat16 [40, 1536, 512], P('exp', None, 'hid'), may hold values from -0.15625 to 0.15625
- expert_down_weight: bfloat16 [40, 512, 1536], P('exp', 'hid'), may hold values from -0.25 to 0.25
Outputs:
- attn_out: bfloat16 [16384, 1536], P(('req', 'exp', 'hid'))
- expert_out: bfloat16 [16384, 1536], P(('req', 'exp', 'hid'))
Inputs may be any that keep to these rules, and one draw needn't show every extreme that they name: `lengths`: each row sums to 2048; its largest entry is exactly 1024. `adapter_home_row`: each adapter row appears once. `routes`: A row names 8 different experts. In the rows of one device (64 consecutive rows, aligned) no expert is named more than 16 times, a bound that some block reaches in some of them.
All inputs are finite; a program needn't handle non-finite values.
Results may differ from a plain program's by a relative error of at most 0.029.
The roundings to bfloat16 on the way count: a program that leaves them out, or rounds other values in their place, can miss the bound.
Values may be sent and summed in bfloat16 or wider, within the bound.
No kernel may reach another device: no remote copies, remote signals or barrier semaphores. Data moves between devices by JAX's collectives and lax.ppermute only.
A program may use at most 128 MiB of HBM per device.

v0:
```python
import jax
import jax.numpy as jnp
from jax import lax
from jax.sharding import PartitionSpec as P

HEAD_WIDTH = 64


scale_attn = 0.015625
residual_mult = 0.22
norm_eps = 1e-06
rope_base = 10000.0
neg_large = -1e30


def rms_norm(values, norm_gain):
    widened = values.astype(jnp.float32)
    mean_sq = jnp.mean(widened * widened, axis=-1, keepdims=True)
    return (widened * lax.rsqrt(mean_sq + norm_eps) * norm_gain).astype(jnp.bfloat16)


def rotary(heads_in, position):
    half_size = heads_in.shape[-1] // 2
    frequency = rope_base ** (-2.0 * jnp.arange(half_size, dtype=jnp.float32) / heads_in.shape[-1])
    angles = position.astype(jnp.float32)[:, None] * frequency[None, :]
    cosine = jnp.cos(angles)[:, None, :]
    sine_part = jnp.sin(angles)[:, None, :]
    first_half = heads_in[..., :half_size]
    second_half = heads_in[..., half_size:]
    return jnp.concatenate(
        [
            first_half * cosine - second_half * sine_part,
            second_half * cosine + first_half * sine_part,
        ],
        axis=-1,
    )


def request_of(row_ids, group_len):
    request_end = jnp.cumsum(group_len)
    return jnp.sum((row_ids[:, None] >= request_end[None, :]).astype(jnp.int32), axis=1)


def locate(row_ids, group_len):
    request_end = jnp.cumsum(group_len)
    request_start = request_end - group_len
    request = request_of(row_ids, group_len)
    member = request[:, None] == jnp.arange(group_len.shape[0], dtype=jnp.int32)[None, :]
    position = row_ids - jnp.sum(jnp.where(member, request_start[None, :], 0), axis=1)
    return (request, member, position)


def expert_rows(rows_in, expert_gate_weight, expert_up_weight, expert_down_weight):
    gate_act = jnp.einsum(
        "red,edf->ref", rows_in, expert_gate_weight, preferred_element_type=jnp.float32
    )
    upper = jnp.einsum(
        "red,edf->ref", rows_in, expert_up_weight, preferred_element_type=jnp.float32
    )
    hidden = (jax.nn.silu(gate_act) * upper).astype(jnp.bfloat16)
    return jnp.einsum(
        "ref,efd->red", hidden, expert_down_weight, preferred_element_type=jnp.float32
    )


def per_device(
    layer_input_rows,
    attention_norm_gain,
    query_weight,
    key_weight,
    value_weight,
    attention_output_weight,
    query_down_factor,
    query_up_factor,
    value_down_factor,
    value_up_factor,
    lengths,
    request_adapter,
    adapter_home_row,
    expert_norm_gain,
    routes,
    router_expert_weight,
    expert_gate_weight,
    expert_up_weight,
    expert_down_weight,
):
    exp_count = lax.axis_size("exp")
    hid_count = lax.axis_size("hid")
    exp_index = lax.axis_index("exp")
    hid_index = lax.axis_index("hid")
    req_index = lax.axis_index("req")
    query_rows = layer_input_rows.shape[0]
    width = layer_input_rows.shape[1]
    kv_local = key_weight.shape[1] // HEAD_WIDTH
    q_local = query_weight.shape[1] // HEAD_WIDTH
    group_share = q_local // kv_local
    adapter_rank_size = query_down_factor.shape[2]
    requests = lengths.shape[1]
    group_len = lengths[0]
    row_ids = exp_index * query_rows + jnp.arange(query_rows, dtype=jnp.int32)
    request, member, position = locate(row_ids, group_len)
    wanted = lax.dynamic_index_in_dim(request_adapter, req_index, 0, keepdims=False)
    slot_ids = jnp.arange(adapter_home_row.shape[0], dtype=jnp.int32)
    home_of = jnp.sum(
        jnp.where(wanted[:, None] == slot_ids[None, :], adapter_home_row[None, :], 0), axis=1
    )
    pieces = (
        lax.all_gather(query_down_factor, ("req", "exp"), axis=0, tiled=True),
        lax.all_gather(query_up_factor, ("req", "exp"), axis=0, tiled=True),
        lax.all_gather(value_down_factor, ("req", "exp"), axis=0, tiled=True),
        lax.all_gather(value_up_factor, ("req", "exp"), axis=0, tiled=True),
    )
    adapter_bank_rows = jnp.arange(pieces[0].shape[0], dtype=jnp.int32)
    selector = (home_of[:, None] == adapter_bank_rows[None, :]).astype(jnp.bfloat16)
    picked_now = tuple(
        (
            jnp.einsum("jn,nab->jab", selector, piece_in, preferred_element_type=jnp.float32)
            for piece_in in pieces
        )
    )
    chosen = tuple((fresh for fresh in picked_now))
    qa_sel, qb_sel, va_sel, vb_sel = [member_in.astype(jnp.bfloat16) for member_in in chosen]
    normed_rows = rms_norm(layer_input_rows, attention_norm_gain)

    def low_rank_term(a_sel, b_sel, width_cols, offset):
        inner_terms = jnp.einsum(
            "td,jdr->tjr", normed_rows, a_sel, preferred_element_type=jnp.float32
        )
        inner_terms = (
            jnp.where(member[:, :, None], inner_terms, 0.0)
            .reshape(query_rows, requests * adapter_rank_size)
            .astype(jnp.bfloat16)
        )
        right_factor = lax.dynamic_slice_in_dim(b_sel, offset, width_cols, 2).reshape(
            requests * adapter_rank_size, width_cols
        )
        return jnp.dot(inner_terms, right_factor, preferred_element_type=jnp.float32)

    query_cols = q_local * HEAD_WIDTH
    kv_cols = kv_local * HEAD_WIDTH
    query_matrix = jnp.dot(
        normed_rows, query_weight, preferred_element_type=jnp.float32
    ) + low_rank_term(qa_sel, qb_sel, query_cols, hid_index * query_cols)
    query_matrix = rotary(query_matrix.reshape(query_rows, q_local, HEAD_WIDTH), position).astype(
        jnp.bfloat16
    )
    query_matrix = query_matrix.reshape(query_rows, kv_local, group_share, HEAD_WIDTH)
    keys_own = jnp.dot(normed_rows, key_weight, preferred_element_type=jnp.float32)
    keys_own = (
        rotary(keys_own.reshape(query_rows, kv_local, HEAD_WIDTH), position)
        .astype(jnp.bfloat16)
        .reshape(query_rows, kv_cols)
    )
    values_own = jnp.dot(
        normed_rows, value_weight, preferred_element_type=jnp.float32
    ) + low_rank_term(va_sel, vb_sel, kv_cols, hid_index * kv_cols)
    values_own = values_own.astype(jnp.bfloat16)
    running_max = jnp.full((kv_local, group_share, query_rows), neg_large, jnp.float32)
    key_piece = lax.all_gather(keys_own, "exp", axis=0, tiled=True)
    value_piece = lax.all_gather(values_own, "exp", axis=0, tiled=True)
    piece_len = key_piece.shape[0]
    key_ids = jnp.arange(piece_len, dtype=jnp.int32)
    key_request = request_of(key_ids, group_len)
    allowed = (request[:, None] == key_request[None, :]) & (key_ids[None, :] <= row_ids[:, None])
    key_heads = key_piece.reshape(piece_len, kv_local, HEAD_WIDTH)
    value_heads = value_piece.reshape(piece_len, kv_local, HEAD_WIDTH)
    scores = (
        jnp.einsum("qkgh,nkh->kgqn", query_matrix, key_heads, preferred_element_type=jnp.float32)
        * scale_attn
    )
    scores = jnp.where(allowed[None, None], scores, neg_large)
    new_max = jnp.maximum(running_max, jnp.max(scores, axis=-1))
    weights = jnp.where(allowed[None, None], jnp.exp(scores - new_max[..., None]), 0.0)
    running_sum = jnp.sum(weights, axis=-1)
    running_out = jnp.einsum(
        "kgqn,nkh->kgqh",
        weights.astype(jnp.bfloat16),
        value_heads,
        preferred_element_type=jnp.float32,
    )
    running_max, running_sum, running_out = (new_max, running_sum, running_out)
    attended = (running_out / running_sum[..., None]).astype(jnp.bfloat16)
    attended = jnp.transpose(attended, (2, 0, 1, 3)).reshape(query_rows, query_cols)
    tok_rows = query_rows // hid_count
    attn_out = lax.psum_scatter(
        jnp.dot(attended, attention_output_weight, preferred_element_type=jnp.float32).astype(
            jnp.bfloat16
        ),
        "hid",
        scatter_dimension=0,
        tiled=True,
    )
    own_rows = lax.dynamic_slice_in_dim(layer_input_rows, hid_index * tok_rows, tok_rows, 0)
    mixed_rows = own_rows.astype(jnp.float32) + residual_mult * attn_out.astype(jnp.float32)
    normed_moe = rms_norm(mixed_rows, expert_norm_gain)
    local_exp = expert_gate_weight.shape[0]
    expert_count = local_exp * exp_count
    top_count = routes.shape[1]
    capacity = max(2, tok_rows // 4)
    flat_route = routes.reshape(tok_rows * top_count)
    route_hits = (flat_route[:, None] == jnp.arange(expert_count, dtype=jnp.int32)[None, :]).astype(
        jnp.int32
    )
    earlier = jnp.cumsum(route_hits, axis=0) - route_hits
    slot_pos = jnp.sum(earlier * route_hits, axis=1)
    slots = slot_pos * expert_count + flat_route
    slot_table = jnp.arange(capacity * expert_count, dtype=jnp.int32)
    placed = jnp.any(
        slot_table[:, None, None] == slots.reshape(tok_rows, top_count)[None], axis=2
    ).astype(jnp.bfloat16)
    outgoing = jnp.dot(placed, normed_moe, preferred_element_type=jnp.float32).astype(jnp.bfloat16)
    outgoing = outgoing.reshape(capacity, expert_count, width)
    copies = jnp.broadcast_to(
        outgoing.reshape(capacity, exp_count, 1, local_exp, width),
        (capacity, exp_count, hid_count, local_exp, width),
    )
    copies = copies.reshape(capacity, exp_count * hid_count * local_exp, width)
    arrived = lax.all_to_all(copies, ("exp", "hid"), split_axis=1, concat_axis=0, tiled=True)
    partials = expert_rows(
        arrived, expert_gate_weight, expert_up_weight, expert_down_weight
    ).astype(jnp.bfloat16)
    returned = lax.all_to_all(partials, ("exp", "hid"), split_axis=0, concat_axis=1, tiled=True)
    returned = returned.reshape(capacity, exp_count, hid_count, local_exp, width)
    results = jnp.sum(returned.astype(jnp.float32), axis=2).astype(jnp.bfloat16)
    results = results.reshape(capacity * expert_count, width)
    picked = jnp.take(results, slots, axis=0).reshape(tok_rows, top_count, width)
    expert_out = jnp.sum(
        router_expert_weight[:, :, None] * picked.astype(jnp.float32), axis=1
    ).astype(jnp.bfloat16)
    return (attn_out, expert_out)


def solution(mesh):
    in_specs = (
        P(("req", "exp"), None),
        P(),
        P(None, "hid"),
        P(None, "hid"),
        P(None, "hid"),
        P("hid", None),
        P(("req", "exp"), None, None),
        P(("req", "exp"), None, None),
        P(("req", "exp"), None, None),
        P(("req", "exp"), None, None),
        P("req", None),
        P(),
        P(),
        P(),
        P(("req", "exp", "hid"), None),
        P(("req", "exp", "hid"), None),
        P("exp", None, "hid"),
        P("exp", None, "hid"),
        P("exp", "hid", None),
    )
    out_specs = (P(("req", "exp", "hid"), None), P(("req", "exp", "hid"), None))
    return jax.shard_map(
        per_device, mesh=mesh, in_specs=in_specs, out_specs=out_specs, check_vma=False
    )
```

profile of v0, /device:TPU:3, one launch (start us, length us, event | category | flops | bytes accessed | tf_op | source)
XLA Modules:
  0.0 724.9 jit_solution(7659078790844080535)
XLA Ops:
  7.2 0.7 all-gather.11.cloned.1.call-update
  8.0 0.7 all-gather.5.cloned.1.call-update
  8.7 0.7 all-gather.7.cloned.1.call-update
  9.4 0.5 all-gather.9.cloned.1.call-update
  10.0 0.8 reduce-window.10
  10.9 0.9 dynamic-slice_reduce_fusion
  11.7 0.1 convert_reduce_fusion
  11.8 0.8 select_reduce_fusion.1
  12.8 0.7 fusion.63
  13.5 1.4 fusion.19
  14.9 0.2 multiply_cosine_fusion
  15.1 1.7 fusion.82
  16.9 0.5 iota_compare_fusion.5
  17.4 15.2 %all_gather.18 = bf16[2048,128]{0,1:T(8,128)(2,1)} all-gather(bf16[256,128]{0,1:T(8,128)(2,1)S(1)} %bitcast.138), channel_id=1, replica_groups=mesh['req'=8,'exp'=8,'hid'=4] {'exp'}, dimensions={0}, use_global_device_ids=true | all-gather | bytes 589824 | tf_op jit(solution)/shard_map/all_gather | solution.py:159
  32.7 0.5 fusion.18
  33.2 57.8 %all-gather.11.cloned.1.call-done = bf16[64,16,512]{2,1,0:T(8,128)(2,1)} async-done(((bf16[1,16,512]{2,1,0:T(8,128)(2,1)}), bf16[64,16,512]{2,1,0:T(8,128)(2,1)}) %all-gather.11.cloned.1.call-update) | async-done | bytes 1048592 | tf_op jit(solution)/shard_map/all_gather | solution.py:111
  91.0 2.4 fusion.34
  93.4 76.1 %all-gather.5.cloned.1.call-done = bf16[64,1536,16]{1,2,0:T(8,128)(2,1)} async-done(((bf16[1,1536,16]{1,2,0:T(8,128)(2,1)}), bf16[64,1536,16]{1,2,0:T(8,128)(2,1)}) %all-gather.5.cloned.1.call-update) | async-done | bytes 3145744 | tf_op jit(solution)/shard_map/all_gather | solution.py:108
  169.5 5.3 fusion.12
  174.8 72.9 %all-gather.7.cloned.1.call-done = bf16[64,16,1536]{2,1,0:T(8,128)(2,1)} async-done(((bf16[1,16,1536]{2,1,0:T(8,128)(2,1)}), bf16[64,16,1536]{2,1,0:T(8,128)(2,1)}) %all-gather.7.cloned.1.call-update) | async-done | bytes 3145744 | tf_op jit(solution)/shard_map/all_gather | solution.py:109
  247.7 5.4 fusion.8
  253.1 0.4 fusion.79
  253.6 0.2 convolution_bitcast_fusion.2
  253.8 1.4 convolution_add_fusion
  255.2 1.9 copy.89
  257.1 1.1 subtract_convert_fusion
  258.2 7.7 %fusion = (f32[2,3,256]{2,1,0:T(4,128)S(1)}, f32[2,2048,256,3]{2,1,3,0:T(8,128)}) fusion(pred[256,2048]{0,1:T(8,128)(4,1)S(1)} %fusion.18, bf16[2048,2,64,1]{0,2,3,1:T(8,128)(2,1)} %bitcast.136, bf16[256,2,3,32]{0,3,2,1:T(8,128)(2,1)S(1)} %bitcast.144, bf16[256,2,3,32]{0,3,2,1:T(8,128)(2,1)S(1)} %bitcast.143), kind=kOutput, calls=%fused_computation.3 | convolution fusion | flops 412482048 | bytes 13834240 | tf_op jit(solution)/shard_map/qkgh,nkh->kgqn/dot_general | solution.py:168
  265.9 0.6 broadcast_maximum_fusion
  266.5 59.3 %all-gather.9.cloned.1.call-done = bf16[64,1536,16]{1,2,0:T(8,128)(2,1)} async-done(((bf16[1,1536,16]{1,2,0:T(8,128)(2,1)}), bf16[64,1536,16]{1,2,0:T(8,128)(2,1)}) %all-gather.9.cloned.1.call-update) | async-done | bytes 3145744 | tf_op jit(solution)/shard_map/all_gather | solution.py:110
  325.8 5.8 fusion.15
  331.6 0.4 fusion.76
  332.1 0.2 convolution_bitcast_fusion.3
  332.3 0.4 fusion.33
  332.7 13.2 %all_gather.23 = bf16[2048,128]{1,0:T(8,128)(2,1)S(1)} all-gather(bf16[256,128]{1,0:T(8,128)(2,1)S(1)} %fusion.33), channel_id=1, replica_groups=mesh['req'=8,'exp'=8,'hid'=4] {'exp'}, dimensions={0}, use_global_device_ids=true | all-gather | bytes 589824 | tf_op jit(solution)/shard_map/all_gather | solution.py:160
  345.9 0.2 copy.94
  346.2 7.5 %fusion.1 = f32[2,3,256]{2,1,0:T(4,128)S(1)} fusion(f32[2,2048,256,3]{2,1,3,0:T(8,128)} %get-tuple-element.11, f32[2,3,256]{2,1,0:T(4,128)} %broadcast_maximum_fusion, pred[256,2048]{0,1:T(8,128)(4,1)S(1)} %fusion.18), kind=kLoop, calls=%fused_computation.4 | loop fusion | flops 15727104 | bytes 13119488 | tf_op jit(solution)/shard_map/reduce_sum | solution.py:174
  353.7 0.7 copy-done.2
  354.4 3.6 fusion.39
  358.1 1.5 convolution_convert_fusion.1
  359.6 0.1 eq.117
  359.8 1.2 reduce-window.11
  361.0 0.2 slice_reduce_fusion
  361.3 0.1 fusion.53
  361.7 0.5 fusion.29
  362.1 15.8 %reduce-scatter.2.cloned.1.call-done = bf16[64,1536]{1,0:T(8,128)(2,1)} async-done(((bf16[256,1536]{1,0:T(8,128)(2,1)}), bf16[64,1536]{1,0:T(8,128)(2,1)}) %reduce-scatter.2.cloned.1.call-update) | async-done | bytes 196624 | tf_op jit(solution)/shard_map/reduce_scatter | solution.py:185
  378.0 1.1 multiply_reduce_fusion.1
  379.1 3.0 convolution_convert_fusion
  382.1 4.3 broadcast_in_dim.129
  386.4 3.2 copy.103
  389.5 1.0 broadcast_in_dim.130
  390.5 98.9 %all_to_all.33 = bf16[16,160,1536]{2,0,1:T(8,128)(2,1)S(1)} all-to-all(bf16[16,160,1536]{2,0,1:T(8,128)(2,1)S(1)} %bitcast.131), channel_id=1, replica_groups=mesh['req'=8,'exp'=8,'hid'=4] {'exp','hid'}, dimensions={1} | all-to-all | bytes 15728640 | tf_op jit(solution)/shard_map/all_to_all | solution.py:218
  489.4 3.9 copy.104
  493.3 6.0 convolution_bitcast_fusion.1
  499.2 12.2 %convert_bitcast_fusion = bf16[512,5,1536]{2,0,1:T(8,128)(2,1)} fusion(bf16[5,128,1536]{2,1,0:T(8,128)(2,1)S(1)} %copy-done, bf16[512,5,1536]{2,0,1:T(8,128)(2,1)} %bitcast.134, bf16[5,1536,128]{2,1,0:T(8,128)(2,1)} %param.36, f32[512,5,128]{2,0,1:T(8,128)S(1)} %convolution_bitcast_fusion.1), kind=kOutput, calls=%fused_computation.6 | convolution fusion | flops 2019164160 | bytes 20971520 | tf_op jit(solution)/shard_map/ref,efd->red/dot_general | solution.py:61
  511.4 12.0 %copy.105 = bf16[512,5,1536]{2,1,0:T(8,128)(2,1)} copy(bf16[512,5,1536]{2,0,1:T(8,128)(2,1)} %convert_bitcast_fusion) | data formatting | bytes 15728640 | tf_op jit(solution)/shard_map/convert_element_type | solution.py:221
  523.4 6.7 all-to-all-start.1
  530.1 0.1 copy.101
  530.3 0.7 copy.96
  531.0 160.5 %all-to-all-done.1 = bf16[512,5,1536]{2,1,0:T(8,128)(2,1)} async-done(((bf16[512,5,1536]{2,1,0:T(8,128)(2,1)}), bf16[512,5,1536]{2,1,0:T(8,128)(2,1)}, u32[]{:S(2)}, u32[]{:S(2)}) %all-to-all-start.1) | async-done | bytes 7864352 | tf_op jit(solution)/shard_map/all_to_all | solution.py:222
  691.5 10.2 %reduce.1 = bf16[16,8,5,1536]{3,2,0,1:T(8,128)(2,1)} reduce(bf16[16,8,4,5,1536]{4,3,0,2,1:T(8,128)(2,1)} %bitcast.39, bf16[]{:T(256)} %constant.89.clone.1), dimensions={2}, to_apply=%region_14.15 | reduce | flops 2949120 | bytes 9830402 | tf_op jit(solution)/shard_map/reduce_sum | solution.py:224
  701.7 3.9 copy.107
  705.6 4.3 reshape.289
  709.9 5.5 gather_fusion
  715.4 2.8 multiply_reduce_fusion
  (73 shorter events, 1.2 us)
Async XLA Ops:
  7.2 492.1 %copy-start = (bf16[5,128,1536]{2,1,0:T(8,128)(2,1)S(1)}, bf16[5,128,1536]{2,1,0:T(8,128)(2,1)}, u32[]{:S(2)}) copy-start(bf16[5,128,1536]{2,1,0:T(8,128)(2,1)} %param.37) | copy-start | bytes 5898244
  7.2 83.8 %all-gather.11.cloned.1.call-start = ((), (), s32[]{:S(2)}) async-start(), calls=%async_computation.6 | async-start | bytes 1064960 | tf_op jit(solution)/shard_map/all_gather | solution.py:111
  7.9 161.5 %all-gather.5.cloned.1.call-start = ((), (), s32[]{:S(2)}) async-start(), calls=%async_computation.3 | async-start | bytes 3194880 | tf_op jit(solution)/shard_map/all_gather | solution.py:108
  8.7 239.0 %all-gather.7.cloned.1.call-start = ((), (), s32[]{:S(2)}) async-start(), calls=%async_computation.4 | async-start | bytes 3194880 | tf_op jit(solution)/shard_map/all_gather | solution.py:109
  9.4 316.4 %all-gather.9.cloned.1.call-start = ((), (), s32[]{:S(2)}) async-start(), calls=%async_computation.5 | async-start | bytes 3194880 | tf_op jit(solution)/shard_map/all_gather | solution.py:110
  10.0 368.0 %reduce-scatter.2.cloned.1.call-start = ((), (), s32[]{:S(2)}) async-start(), calls=%async_computation.7 | async-start | bytes 983040 | tf_op jit(solution)/shard_map/reduce_scatter | solution.py:185
  12.7 156.8 %copy-start.9 = (s32[4]{0:T(128)}, s32[4]{0:T(128)S(1)}, u32[]{:S(2)}) copy-start(s32[4]{0:T(128)S(1)} %select_reduce_fusion.1) | copy-start | bytes 52
  14.9 18.3 %copy-start.14 = (f32[256]{0:T(256)}, f32[256]{0:T(256)S(1)}, u32[]{:S(2)}) copy-start(f32[256]{0:T(256)S(1)} %add_rsqrt_fusion) | copy-start | bytes 3076
  174.8 78.3 %copy-start.3 = (bf16[256,1536]{1,0:T(8,128)(2,1)S(1)}, bf16[256,1536]{1,0:T(8,128)(2,1)}, u32[]{:S(2)}) copy-start(bf16[256,1536]{1,0:T(8,128)(2,1)} %param.19) | copy-start | bytes 2359300
  247.7 5.4 copy-start.15
  247.7 5.5 copy-start.19
  247.7 5.9 copy-start.11
  247.7 6.1 copy-start.17
  258.2 67.5 %copy-start.10 = (s32[4]{0:T(128)S(1)}, s32[4]{0:T(128)}, u32[]{:S(2)}) copy-start(s32[4]{0:T(128)} %copy-done.9) | copy-start | bytes 52
  265.9 65.7 %copy-start.16 = (f32[256]{0:T(256)S(1)}, f32[256]{0:T(256)}, u32[]{:S(2)}) copy-start(f32[256]{0:T(256)} %copy-done.14) | copy-start | bytes 3076
  265.9 65.7 %copy-start.20 = (f32[1536]{0:T(1024)S(1)}, f32[1536]{0:T(1024)}, u32[]{:S(2)}) copy-start(f32[1536]{0:T(1024)} %param.20) | copy-start | bytes 18436
  266.5 65.6 %copy-start.12 = (pred[256,4]{0,1:T(4,128)(4,1)S(1)}, pred[256,4]{0,1:T(4,128)(4,1)}, u32[]{:S(2)}) copy-start(pred[256,4]{0,1:T(4,128)(4,1)} %iota_compare_fusion.5) | copy-start | bytes 3076
  325.8 6.5 copy-start.18
  346.2 8.2 %copy-start.2 = (f32[2,2048,256,3]{2,1,3,0:T(8,128)S(1)}, f32[2,2048,256,3]{2,1,3,0:T(8,128)}, u32[]{:S(2)}) copy-start(f32[2,2048,256,3]{2,1,3,0:T(8,128)} %get-tuple-element.11) | copy-start | bytes 37748740
  346.2 8.2 %copy-start.6 = (f32[2,3,256]{2,1,0:T(4,128)S(1)}, f32[2,3,256]{2,1,0:T(4,128)}, u32[]{:S(2)}) copy-start(f32[2,3,256]{2,1,0:T(4,128)} %broadcast_maximum_fusion) | copy-start | bytes 18436
  354.4 3.6 copy-start.5
  358.0 1.5 copy-start.7
  358.0 20.0 %copy-start.4 = (bf16[256,1536]{1,0:T(8,128)(2,1)S(1)}, bf16[256,1536]{1,0:T(8,128)(2,1)}, u32[]{:S(2)}) copy-start(bf16[256,1536]{1,0:T(8,128)(2,1)} %param.19) | copy-start | bytes 2359300
  358.0 21.1 %copy-start.8 = (f32[1536]{0:T(1024)S(1)}, f32[1536]{0:T(1024)}, u32[]{:S(2)}) copy-start(f32[1536]{0:T(1024)} %param.32) | copy-start | bytes 18436
  523.4 6.9 copy-start.13
  523.4 168.1 %all-to-all-start.1 = ((bf16[512,5,1536]{2,1,0:T(8,128)(2,1)}), bf16[512,5,1536]{2,1,0:T(8,128)(2,1)}, u32[]{:S(2)}, u32[]{:S(2)}) async-start(bf16[512,5,1536]{2,1,0:T(8,128)(2,1)} %copy.105), calls=%async_computation.2 | async-start | bytes 25165824 | tf_op jit(solution)/shard_map/all_to_all | solution.py:222
  709.9 8.3 %copy-start.1 = (bf16[5,128,1536]{2,1,0:T(8,128)(2,1)S(1)}, bf16[5,128,1536]{2,1,0:T(8,128)(2,1)}, u32[]{:S(2)}) copy-start(bf16[5,128,1536]{2,1,0:T(8,128)(2,1)} %param.37) | copy-start | bytes 5898244
Sparse Core Ops, SparseCore 0:
  10.8 80.1 all-gather.10
  93.7 75.7 all-gather.4
  172.2 75.4 all-gather.6
  250.3 75.4 all-gather.8
  359.7 18.2 reduce-scatter.1
where the time goes:
time: 739 us; the launch traced here: 725 us
  waiting for transfers between devices  445 us (60%)
  blocking collectives  127 us (17%)
  matrix products  57.6 us (8%)
  local copies, waits for them, and re-layouts  43.5 us (6%)
  other arithmetic  30.3 us (4%)
  between operations  14.4 us (2%)
    all_to_all x1, waiting for transfers between devices, per_device(): lax.all_to_all(partials, ('exp', 'hid'), split_axis=0, concat_axis=1, til...  161 us
    all_to_all x1, blocking collectives, per_device(): lax.all_to_all(copies, ('exp', 'hid'), split_axis=1, concat_axis=0, tiled...  98.9 us
    all_gather x1, waiting for transfers between devices, per_device(): lax.all_gather(query_down_factor, ('req', 'exp'), axis=0, tiled=True)  76.1 us
    all_gather x1, waiting for transfers between devices, per_device(): lax.all_gather(query_up_factor, ('req', 'exp'), axis=0, tiled=True)  72.9 us
    all_gather x1, waiting for transfers between devices, per_device(): lax.all_gather(value_down_factor, ('req', 'exp'), axis=0, tiled=True)  59.3 us
    all_gather x1, waiting for transfers between devices, per_device(): lax.all_gather(value_up_factor, ('req', 'exp'), axis=0, tiled=True)  57.8 us
    dot_general x4, matrix products, per_device(): jnp.einsum('jn,nab->jab', selector, piece_in, preferred_element_type=jnp....  18.9 us
    reduce_scatter x1, waiting for transfers between devices, per_device(): lax.psum_scatter(jnp.dot(attended, attention_output_weight, preferred_ele...  15.8 us
  transfers between devices with their start and end apart: 6, of which 6 were waited for; matrix products, arithmetic and copies ran while one was open for 5% of the time, Pallas kernels for 0%

commit v1 on v0

--- a/solution.py
+++ b/solution.py
@@ -104,22 +104,28 @@
     home_of = jnp.sum(
         jnp.where(wanted[:, None] == slot_ids[None, :], adapter_home_row[None, :], 0), axis=1
     )
-    pieces = (
-        lax.all_gather(query_down_factor, ("req", "exp"), axis=0, tiled=True),
-        lax.all_gather(query_up_factor, ("req", "exp"), axis=0, tiled=True),
-        lax.all_gather(value_down_factor, ("req", "exp"), axis=0, tiled=True),
-        lax.all_gather(value_up_factor, ("req", "exp"), axis=0, tiled=True),
-    )
-    adapter_bank_rows = jnp.arange(pieces[0].shape[0], dtype=jnp.int32)
-    selector = (home_of[:, None] == adapter_bank_rows[None, :]).astype(jnp.bfloat16)
-    picked_now = tuple(
-        (
-            jnp.einsum("jn,nab->jab", selector, piece_in, preferred_element_type=jnp.float32)
-            for piece_in in pieces
-        )
-    )
-    chosen = tuple((fresh for fresh in picked_now))
-    qa_sel, qb_sel, va_sel, vb_sel = [member_in.astype(jnp.bfloat16) for member_in in chosen]
+    query_cols = q_local * HEAD_WIDTH
+    kv_cols = kv_local * HEAD_WIDTH
+    bank_local = query_down_factor.shape[0]
+    up_q = lax.dynamic_slice_in_dim(query_up_factor, hid_index * query_cols, query_cols, 2)
+    up_v = lax.dynamic_slice_in_dim(value_up_factor, hid_index * kv_cols, kv_cols, 2)
+    parts_in = (query_down_factor, up_q, value_down_factor, up_v)
+    part_shapes = [p.shape[1:] for p in parts_in]
+    part_sizes = [p.shape[1] * p.shape[2] for p in parts_in]
+    bank = jnp.concatenate([p.reshape(bank_local, -1) for p in parts_in], axis=1)
+    along_req = lax.all_gather(bank, "req", axis=0, tiled=True)
+    home_dev = home_of // bank_local
+    home_pick = (home_dev // exp_count) * bank_local + home_of % bank_local
+    mine = (home_dev % exp_count) == exp_index
+    rows_pick = jnp.take(along_req, home_pick, axis=0)
+    rows_pick = jnp.where(mine[:, None], rows_pick, jnp.zeros_like(rows_pick))
+    rows_pick = lax.psum(rows_pick, "exp")
+    chosen = []
+    start = 0
+    for shape_in, size_in in zip(part_shapes, part_sizes):
+        chosen.append(rows_pick[:, start:start + size_in].reshape((requests,) + shape_in))
+        start += size_in
+    qa_sel, qb_sel, va_sel, vb_sel = chosen
     normed_rows = rms_norm(layer_input_rows, attention_norm_gain)
 
     def low_rank_term(a_sel, b_sel, width_cols, offset):
@@ -131,13 +137,9 @@
             .reshape(query_rows, requests * adapter_rank_size)
             .astype(jnp.bfloat16)
         )
-        right_factor = lax.dynamic_slice_in_dim(b_sel, offset, width_cols, 2).reshape(
-            requests * adapter_rank_size, width_cols
-        )
+        right_factor = b_sel.reshape(requests * adapter_rank_size, width_cols)
         return jnp.dot(inner_terms, right_factor, preferred_element_type=jnp.float32)
 
-    query_cols = q_local * HEAD_WIDTH
-    kv_cols = kv_local * HEAD_WIDTH
     query_matrix = jnp.dot(
         normed_rows, query_weight, preferred_element_type=jnp.float32
     ) + low_rank_term(qa_sel, qb_sel, query_cols, hid_index * query_cols)

time: 739 us -> 537 us (0.73); the launches traced: 725 us -> 533 us
  waiting for transfers between devices: 445 us -> 220 us
  blocking collectives: 127 us -> 162 us
  matrix products: 57.6 us -> 42.8 us
  local copies, waits for them, and re-layouts: 43.5 us -> 57.7 us
    all_gather x4 -> x0, waiting for transfers between devices: 266 us -> none  [the longest x1 76.1 us: per_device(): lax.all_gather(query_down_factor, ('req', 'exp'), axis=0, tiled=True)]
    psum x0 -> x1, waiting for transfers between devices: none -> 41.2 us  [per_device(): rows_pick = lax.psum(rows_pick, 'exp')]
    all_gather x0 -> x1, blocking collectives: none -> 28.5 us  [per_device(): along_req = lax.all_gather(bank, 'req', axis=0, tiled=True)]
    dot_general x4 -> x0, matrix products: 18.9 us -> none  [per_device(): jnp.einsum('jn,nab->jab', selector, piece_in, preferred_element_type=jnp....]
  transfers between devices with their start and end apart: 6 -> 3, of which waited for: 6 -> 3; matrix products, arithmetic and copies ran while one was open for 5% -> 2% of each run, Pallas kernels for 0% -> 0%
where the time goes in v1:
time: 537 us; the launch traced here: 533 us
  waiting for transfers between devices  220 us (41%)
  blocking collectives  162 us (30%)
  local copies, waits for them, and re-layouts  57.7 us (11%)
  matrix products  42.8 us (8%)
  other arithmetic  28.6 us (5%)
  between operations  14.6 us (3%)
  starting transfers between devices  6.38 us (1%)
    all_to_all x1, waiting for transfers between devices, per_device(): lax.all_to_all(partials, ('exp', 'hid'), split_axis=0, concat_axis=1, til...  161 us
    all_to_all x1, blocking collectives, per_device(): lax.all_to_all(copies, ('exp', 'hid'), split_axis=1, concat_axis=0, tiled...  98.7 us
    psum x1, waiting for transfers between devices, per_device(): rows_pick = lax.psum(rows_pick, 'exp')  41.2 us
    all_gather x1, blocking collectives, per_device(): along_req = lax.all_gather(bank, 'req', axis=0, tiled=True)  28.5 us
    all_gather x1, blocking collectives, per_device(): key_piece = lax.all_gather(keys_own, 'exp', axis=0, tiled=True)  19.2 us
    reduce_scatter x1, waiting for transfers between devices, per_device(): lax.psum_scatter(jnp.dot(attended, attention_output_weight, preferred_ele...  18.2 us
    all_gather x1, blocking collectives, per_device(): value_piece = lax.all_gather(values_own, 'exp', axis=0, tiled=True)  15.9 us
    dot_general x1, matrix products, expert_rows(): jnp.einsum('ref,efd->red', hidden, expert_down_weight, preferred_element_...  12.2 us
  transfers between devices with their start and end apart: 3, of which 3 were waited for; matrix products, arithmetic and copies ran while one was open for 2% of the time, Pallas kernels for 0%

profile of v1, /device:TPU:3, one launch (start us, length us, event | category | flops | bytes accessed | tf_op | source)
XLA Modules:
  0.0 532.5 jit_solution(14082683978876960325)
XLA Ops:
  7.2 0.8 dynamic-slice_bitcast_fusion
  8.1 0.7 dynamic-slice_bitcast_fusion.1
  8.8 1.0 copy.99
  9.8 0.3 reshape.377
  10.1 1.0 copy.100
  11.1 0.3 reshape.379
  11.4 0.2 maximum_bitcast_fusion
  11.7 28.5 %all-gather = bf16[8,1,57344]{2,1,0:T(2,128)(2,1)S(1)} all-gather(bf16[1,1,57344]{2,1,0:T(2,128)(2,1)S(1)} %maximum_bitcast_fusion), channel_id=1, replica_groups=mesh['req'=8,'exp'=8,'hid'=4] {'req'}, dimensions={0}, use_global_device_ids=true | all-gather | bytes 1032192 | tf_op jit(solution)/shard_map/all_gather | solution.py:116
  40.2 1.0 copy.131
  41.2 0.2 dynamic-slice_reduce_fusion
  41.4 0.2 select_reduce_fusion.1
  41.7 1.0 gather_fusion
  42.7 1.1 select_select_fusion
  43.9 1.4 fusion.7
  45.3 0.2 reduce-window.10
  45.8 2.6 fusion.56
  48.5 0.5 fusion.58
  48.9 1.2 fusion.6
  50.2 0.2 multiply_cosine_fusion
  50.4 0.6 copy-done.8
  51.0 19.2 %all_gather.9 = bf16[2048,128]{0,1:T(8,128)(2,1)} all-gather(bf16[256,128]{0,1:T(8,128)(2,1)S(1)} %bitcast.160), channel_id=1, replica_groups=mesh['req'=8,'exp'=8,'hid'=4] {'exp'}, dimensions={0}, use_global_device_ids=true | all-gather | bytes 589824 | tf_op jit(solution)/shard_map/all_gather | solution.py:161
  70.2 41.2 %all-reduce.2.cloned.1.call-done = bf16[4,57344]{1,0:T(4,128)(2,1)} async-done(((bf16[4,57344]{1,0:T(4,128)(2,1)}), bf16[4,57344]{1,0:T(4,128)(2,1)}) %all-reduce.2.cloned.1.call-update) | async-done | bytes 458768 | tf_op jit(solution)/shard_map/psum | solution.py:122
  111.4 1.9 fusion.60
  113.3 2.1 reshape.381
  115.4 1.3 copy.101
  116.7 2.2 fusion.54
  118.9 2.1 reshape.383
  121.0 1.3 copy.103
  122.3 1.7 fusion.51
  124.0 0.8 slice.49
  124.8 0.9 select_convert_fusion.1
  125.7 0.2 convolution_add_fusion
  125.9 0.2 copy.102
  126.2 7.7 %fusion = (f32[2,3,256]{2,1,0:T(4,128)S(1)}, f32[2,2048,256,3]{2,1,3,0:T(8,128)}) fusion(pred[256,2048]{0,1:T(8,128)(4,1)S(1)} %copy-done.2, bf16[2048,2,64,1]{0,2,3,1:T(8,128)(2,1)} %bitcast.158, bf16[256,2,3,32]{0,3,2,1:T(8,128)(2,1)S(1)} %bitcast.169, bf16[256,2,3,32]{0,3,2,1:T(8,128)(2,1)S(1)} %bitcast.168), kind=kOutput, calls=%fused_computation.4 | convolution fusion | flops 412482048 | bytes 13834240 | tf_op jit(solution)/shard_map/qkgh,nkh->kgqn/dot_general | solution.py:170
  134.0 0.2 fusion.61
  134.2 1.4 fusion.21
  135.6 15.9 %all_gather.11 = bf16[2048,128]{1,0:T(8,128)(2,1)S(1)} all-gather(bf16[256,128]{1,0:T(8,128)(2,1)S(1)} %fusion.21), channel_id=1, replica_groups=mesh['req'=8,'exp'=8,'hid'=4] {'exp'}, dimensions={0}, use_global_device_ids=true | all-gather | bytes 589824 | tf_op jit(solution)/shard_map/all_gather | solution.py:162
  151.6 0.2 copy.104
  151.8 6.9 %fusion.1 = f32[2,3,256]{2,1,0:T(4,128)S(1)} fusion(f32[2,2048,256,3]{2,1,3,0:T(8,128)} %get-tuple-element.17, f32[2,3,256]{2,1,0:T(4,128)S(1)} %broadcast_maximum_fusion, pred[256,2048]{0,1:T(8,128)(4,1)S(1)} %copy-done.2), kind=kLoop, calls=%fused_computation.5 | loop fusion | flops 15727104 | bytes 13119488 | tf_op jit(solution)/shard_map/reduce_sum | solution.py:176
  158.6 1.4 copy-done.1
  160.0 3.6 fusion.25
  163.7 1.5 convolution_convert_fusion.1
  165.4 1.2 reduce-window.11
  166.6 0.2 slice_reduce_fusion
  167.3 0.5 fusion.17
  167.7 18.2 %reduce-scatter.2.cloned.1.call-done = bf16[64,1536]{1,0:T(8,128)(2,1)} async-done(((bf16[256,1536]{1,0:T(8,128)(2,1)}), bf16[64,1536]{1,0:T(8,128)(2,1)}) %reduce-scatter.2.cloned.1.call-update) | async-done | bytes 196624 | tf_op jit(solution)/shard_map/reduce_scatter | solution.py:187
  186.0 1.1 multiply_reduce_fusion.1
  187.1 3.0 convolution_convert_fusion
  190.1 4.3 broadcast_in_dim.153
  194.3 3.2 copy.113
  197.5 1.0 broadcast_in_dim.154
  198.5 98.7 %all_to_all.33 = bf16[16,160,1536]{2,0,1:T(8,128)(2,1)S(1)} all-to-all(bf16[16,160,1536]{2,0,1:T(8,128)(2,1)S(1)} %bitcast.152), channel_id=1, replica_groups=mesh['req'=8,'exp'=8,'hid'=4] {'exp','hid'}, dimensions={1} | all-to-all | bytes 15728640 | tf_op jit(solution)/shard_map/all_to_all | solution.py:220
  297.2 3.9 copy.114
  301.1 6.0 %convolution_bitcast_fusion.1 = f32[512,5,128]{2,0,1:T(8,128)S(1)} fusion(bf16[512,5,1536]{2,0,1:T(8,128)(2,1)} %bitcast.155, bf16[5,1536,128]{2,1,0:T(8,128)(2,1)} %param.35), kind=kOutput, calls=%fused_computation.23 | convolution fusion | flops 1006632960 | bytes 11141120 | tf_op jit(solution)/shard_map/red,edf->ref/dot_general | solution.py:54
  307.0 12.2 %convert_bitcast_fusion = bf16[512,5,1536]{2,0,1:T(8,128)(2,1)} fusion(bf16[5,128,1536]{2,1,0:T(8,128)(2,1)S(1)} %copy-done, bf16[512,5,1536]{2,0,1:T(8,128)(2,1)} %bitcast.156, bf16[5,1536,128]{2,1,0:T(8,128)(2,1)} %param.36, f32[512,5,128]{2,0,1:T(8,128)S(1)} %convolution_bitcast_fusion.1), kind=kOutput, calls=%fused_computation.7 | convolution fusion | flops 2019164160 | bytes 20971520 | tf_op jit(solution)/shard_map/ref,efd->red/dot_general | solution.py:61
  319.2 12.0 %copy.115 = bf16[512,5,1536]{2,1,0:T(8,128)(2,1)} copy(bf16[512,5,1536]{2,0,1:T(8,128)(2,1)} %convert_bitcast_fusion) | data formatting | bytes 15728640 | tf_op jit(solution)/shard_map/convert_element_type | solution.py:223
  331.2 6.3 %all-to-all-start.1 = ((bf16[512,5,1536]{2,1,0:T(8,128)(2,1)}), bf16[512,5,1536]{2,1,0:T(8,128)(2,1)}, u32[]{:S(2)}, u32[]{:S(2)}) async-start(bf16[512,5,1536]{2,1,0:T(8,128)(2,1)} %copy.115), calls=%async_computation.2 | async-start | bytes 25165824 | tf_op jit(solution)/shard_map/all_to_all | solution.py:224
  337.7 0.7 copy.106
  338.4 160.7 %all-to-all-done.1 = bf16[512,5,1536]{2,1,0:T(8,128)(2,1)} async-done(((bf16[512,5,1536]{2,1,0:T(8,128)(2,1)}), bf16[512,5,1536]{2,1,0:T(8,128)(2,1)}, u32[]{:S(2)}, u32[]{:S(2)}) %all-to-all-start.1) | async-done | bytes 7864352 | tf_op jit(solution)/shard_map/all_to_all | solution.py:224
  499.1 10.2 %reduce.1 = bf16[16,8,5,1536]{3,2,0,1:T(8,128)(2,1)} reduce(bf16[16,8,4,5,1536]{4,3,0,2,1:T(8,128)(2,1)} %bitcast.41, bf16[]{:T(256)} %constant.141.clone.1), dimensions={2}, to_apply=%region_15.16 | reduce | flops 2949120 | bytes 9830402 | tf_op jit(solution)/shard_map/reduce_sum | solution.py:226
  509.3 3.9 copy.117
  513.2 4.3 reshape.389
  517.5 5.4 %gather_fusion.1 = bf16[512,1536]{1,0:T(8,128)(2,1)S(1)} fusion(bf16[640,1536]{1,0:T(8,128)(2,1)} %reshape.389, s32[1024]{0:T(1024)S(1)} %pad_clamp_fusion), kind=kCustom, calls=%fused_computation.1 | custom fusion | bytes 3147776 | tf_op jit(solution)/shard_map/jit(_take)/gather | solution.py:228
  522.9 2.8 multiply_reduce_fusion
  (83 shorter events, 1.6 us)
Async XLA Ops:
  7.2 299.9 %copy-start = (bf16[5,128,1536]{2,1,0:T(8,128)(2,1)S(1)}, bf16[5,128,1536]{2,1,0:T(8,128)(2,1)}, u32[]{:S(2)}) copy-start(bf16[5,128,1536]{2,1,0:T(8,128)(2,1)} %param.37) | copy-start | bytes 5898244
  7.2 104.2 %all-reduce.2.cloned.1.call-start = ((), (), s32[]{:S(2)}) async-start(), calls=%async_computation.3 | async-start | bytes 917504 | tf_op jit(solution)/shard_map/psum | solution.py:122
  11.7 29.6 %copy-start.15 = (s32[8,4]{0,1:T(4,128)S(1)}, s32[8,4]{0,1:T(4,128)}, u32[]{:S(2)}) copy-start(s32[8,4]{0,1:T(4,128)} %param.30) | copy-start | bytes 388
  11.7 29.8 %copy-start.19 = (s32[64]{0:T(128)S(1)}, s32[64]{0:T(128)}, u32[]{:S(2)}) copy-start(s32[64]{0:T(128)} %param.31) | copy-start | bytes 772
  42.7 2.6 copy-start.20
  42.7 3.1 copy-start.3
  42.7 3.1 copy-start.17
  43.8 4.6 copy-start.16
  43.8 142.1 %reduce-scatter.2.cloned.1.call-start = ((), (), s32[]{:S(2)}) async-start(), calls=%async_computation.4 | async-start | bytes 983040 | tf_op jit(solution)/shard_map/reduce_scatter | solution.py:187
  50.4 0.6 copy-start.8
  50.4 0.6 copy-start.10
  122.3 3.4 copy-start.7
  122.3 3.9 copy-start.9
  122.3 3.9 copy-start.11
  122.3 3.9 copy-start.2
  126.2 7.8 %slice-start = ((bf16[4,57344]{1,0:T(4,128)(2,1)}), bf16[4,2048]{1,0:T(4,128)(2,1)S(1)}, s32[]{:S(2)}) async-start(bf16[4,57344]{1,0:T(4,128)(2,1)} %all-reduce.2.cloned.1.call-done), calls=%async_computation.5 | async-start | bytes 32768 | tf_op jit(solution)/shard_map/slice | solution.py:126
  126.2 8.0 %copy-start.4 = (bf16[256,1536]{1,0:T(8,128)(2,1)S(1)}, bf16[256,1536]{1,0:T(8,128)(2,1)}, u32[]{:S(2)}) copy-start(bf16[256,1536]{1,0:T(8,128)(2,1)} %param.19) | copy-start | bytes 2359300
  126.2 8.0 %copy-start.18 = (f32[1536]{0:T(1024)S(1)}, f32[1536]{0:T(1024)}, u32[]{:S(2)}) copy-start(f32[1536]{0:T(1024)} %param.20) | copy-start | bytes 18436
  151.8 8.2 %copy-start.1 = (f32[2,2048,256,3]{2,1,3,0:T(8,128)S(1)}, f32[2,2048,256,3]{2,1,3,0:T(8,128)}, u32[]{:S(2)}) copy-start(f32[2,2048,256,3]{2,1,3,0:T(8,128)} %get-tuple-element.17) | copy-start | bytes 37748740
  160.0 3.6 copy-start.6
  163.6 1.5 copy-start.12
  163.6 22.4 %copy-start.5 = (bf16[256,1536]{1,0:T(8,128)(2,1)S(1)}, bf16[256,1536]{1,0:T(8,128)(2,1)}, u32[]{:S(2)}) copy-start(bf16[256,1536]{1,0:T(8,128)(2,1)} %param.19) | copy-start | bytes 2359300
  163.6 23.5 %copy-start.13 = (f32[1536]{0:T(1024)S(1)}, f32[1536]{0:T(1024)}, u32[]{:S(2)}) copy-start(f32[1536]{0:T(1024)} %param.32) | copy-start | bytes 18436
  331.2 6.5 %copy-start.14 = (f32[64,8]{0,1:T(8,128)S(1)}, f32[64,8]{0,1:T(8,128)}, u32[]{:S(2)}) copy-start(f32[64,8]{0,1:T(8,128)} %param.34) | copy-start | bytes 6148
  331.2 167.9 %all-to-all-start.1 = ((bf16[512,5,1536]{2,1,0:T(8,128)(2,1)}), bf16[512,5,1536]{2,1,0:T(8,128)(2,1)}, u32[]{:S(2)}, u32[]{:S(2)}) async-start(bf16[512,5,1536]{2,1,0:T(8,128)(2,1)} %copy.115), calls=%async_computation.2 | async-start | bytes 25165824 | tf_op jit(solution)/shard_map/all_to_all | solution.py:224
Sparse Core Ops, SparseCore 0:
  43.9 67.4 all-reduce.1
  165.3 20.6 reduce-scatter.1

commit v2 on v1

--- a/solution.py
+++ b/solution.py
@@ -221,7 +221,11 @@
     partials = expert_rows(
         arrived, expert_gate_weight, expert_up_weight, expert_down_weight
     ).astype(jnp.bfloat16)
-    returned = lax.all_to_all(partials, ("exp", "hid"), split_axis=0, concat_axis=1, tiled=True)
+    partners = exp_count * hid_count
+    partials = jnp.transpose(
+        partials.reshape(partners, capacity, local_exp, width), (1, 0, 2, 3)
+    ).reshape(capacity, partners * local_exp, width)
+    returned = lax.all_to_all(partials, ("exp", "hid"), split_axis=1, concat_axis=1, tiled=True)
     returned = returned.reshape(capacity, exp_count, hid_count, local_exp, width)
     results = jnp.sum(returned.astype(jnp.float32), axis=2).astype(jnp.bfloat16)
     results = results.reshape(capacity * expert_count, width)

time: 537 us -> 459 us (0.85)
  waiting for transfers between devices: 220 us -> 150 us
    all_to_all x1, waiting for transfers between devices: 161 us -> 90.9 us  [per_device(): lax.all_to_all(partials, ('exp', 'hid'), split_axis=1, concat_axis=1, til...]
    convert_element_type x1 -> x0, local copies, waits for them, and re-layouts: 12 us -> none  [per_device(): partials = expert_rows(arrived, expert_gate_weight, expert_up_weight, exp...]
    reshape x0 -> x1, local copies, waits for them, and re-layouts: none -> 7.05 us  [per_device(): partials.reshape(partners, capacity, local_exp, width)]
where the time goes in v2:
time: 459 us; the launch traced here: 455 us
  blocking collectives  162 us (35%)
  waiting for transfers between devices  150 us (33%)
  local copies, waits for them, and re-layouts  53.2 us (12%)
  matrix products  42.8 us (9%)
  other arithmetic  25.1 us (5%)
  between operations  14.6 us (3%)
  starting transfers between devices  6.26 us (1%)
    all_to_all x1, blocking collectives, per_device(): lax.all_to_all(copies, ('exp', 'hid'), split_axis=1, concat_axis=0, tiled...  98.7 us
    all_to_all x1, waiting for transfers between devices, per_device(): lax.all_to_all(partials, ('exp', 'hid'), split_axis=1, concat_axis=1, til...  90.9 us
    psum x1, waiting for transfers between devices, per_device(): rows_pick = lax.psum(rows_pick, 'exp')  41.2 us
    all_gather x1, blocking collectives, per_device(): along_req = lax.all_gather(bank, 'req', axis=0, tiled=True)  28.5 us
    all_gather x1, blocking collectives, per_device(): key_piece = lax.all_gather(keys_own, 'exp', axis=0, tiled=True)  19.2 us
    reduce_scatter x1, waiting for transfers between devices, per_device(): lax.psum_scatter(jnp.dot(attended, attention_output_weight, preferred_ele...  18.2 us
    all_gather x1, blocking collectives, per_device(): value_piece = lax.all_gather(values_own, 'exp', axis=0, tiled=True)  15.9 us
    dot_general x1, matrix products, expert_rows(): jnp.einsum('ref,efd->red', hidden, expert_down_weight, preferred_element_...  12.2 us
  transfers between devices with their start and end apart: 3, of which 3 were waited for; matrix products, arithmetic and copies ran while one was open for 2% of the time, Pallas kernels for 0%

profile of v2, /device:TPU:3, one launch (start us, length us, event | category | flops | bytes accessed | tf_op | source)
XLA Modules:
  0.0 454.6 jit_solution(5914724247694926918)
XLA Ops:
  7.2 0.8 dynamic-slice_bitcast_fusion
  8.1 0.7 dynamic-slice_bitcast_fusion.1
  8.8 1.0 copy.97
  9.8 0.3 reshape.382
  10.1 1.0 copy.98
  11.1 0.3 reshape.384
  11.4 0.2 maximum_bitcast_fusion
  11.7 28.5 %all-gather = bf16[8,1,57344]{2,1,0:T(2,128)(2,1)S(1)} all-gather(bf16[1,1,57344]{2,1,0:T(2,128)(2,1)S(1)} %maximum_bitcast_fusion), channel_id=1, replica_groups=mesh['req'=8,'exp'=8,'hid'=4] {'req'}, dimensions={0}, use_global_device_ids=true | all-gather | bytes 1032192 | tf_op jit(solution)/shard_map/all_gather | solution.py:116
  40.2 1.0 copy.126
  41.2 0.2 dynamic-slice_reduce_fusion
  41.4 0.2 select_reduce_fusion.1
  41.7 1.0 gather_fusion
  42.7 1.1 select_select_fusion
  43.9 1.4 fusion.7
  45.3 0.2 reduce-window.10
  45.8 2.6 fusion.56
  48.5 0.5 fusion.58
  48.9 1.2 fusion.6
  50.2 0.2 multiply_cosine_fusion
  50.4 0.6 copy-done.8
  51.0 19.2 %all_gather.9 = bf16[2048,128]{0,1:T(8,128)(2,1)} all-gather(bf16[256,128]{0,1:T(8,128)(2,1)S(1)} %bitcast.159), channel_id=1, replica_groups=mesh['req'=8,'exp'=8,'hid'=4] {'exp'}, dimensions={0}, use_global_device_ids=true | all-gather | bytes 589824 | tf_op jit(solution)/shard_map/all_gather | solution.py:161
  70.2 41.2 %all-reduce.2.cloned.1.call-done = bf16[4,57344]{1,0:T(4,128)(2,1)} async-done(((bf16[4,57344]{1,0:T(4,128)(2,1)}), bf16[4,57344]{1,0:T(4,128)(2,1)}) %all-reduce.2.cloned.1.call-update) | async-done | bytes 458768 | tf_op jit(solution)/shard_map/psum | solution.py:122
  111.4 1.9 fusion.60
  113.3 2.1 reshape.386
  115.4 1.3 copy.99
  116.7 2.2 fusion.54
  118.9 2.1 reshape.388
  121.0 1.3 copy.101
  122.3 1.7 fusion.51
  124.0 0.8 slice.49
  124.8 0.9 select_convert_fusion.1
  125.7 0.2 convolution_add_fusion
  125.9 0.2 copy.100
  126.2 7.7 %fusion = (f32[2,3,256]{2,1,0:T(4,128)S(1)}, f32[2,2048,256,3]{2,1,3,0:T(8,128)}) fusion(pred[256,2048]{0,1:T(8,128)(4,1)S(1)} %copy-done.2, bf16[2048,2,64,1]{0,2,3,1:T(8,128)(2,1)} %bitcast.157, bf16[256,2,3,32]{0,3,2,1:T(8,128)(2,1)S(1)} %bitcast.168, bf16[256,2,3,32]{0,3,2,1:T(8,128)(2,1)S(1)} %bitcast.167), kind=kOutput, calls=%fused_computation.4 | convolution fusion | flops 412482048 | bytes 13834240 | tf_op jit(solution)/shard_map/qkgh,nkh->kgqn/dot_general | solution.py:170
  134.0 0.2 fusion.61
  134.2 1.4 fusion.21
  135.6 15.9 %all_gather.11 = bf16[2048,128]{1,0:T(8,128)(2,1)S(1)} all-gather(bf16[256,128]{1,0:T(8,128)(2,1)S(1)} %fusion.21), channel_id=1, replica_groups=mesh['req'=8,'exp'=8,'hid'=4] {'exp'}, dimensions={0}, use_global_device_ids=true | all-gather | bytes 589824 | tf_op jit(solution)/shard_map/all_gather | solution.py:162
  151.6 0.2 copy.102
  151.8 6.9 %fusion.1 = f32[2,3,256]{2,1,0:T(4,128)S(1)} fusion(f32[2,2048,256,3]{2,1,3,0:T(8,128)} %get-tuple-element.17, f32[2,3,256]{2,1,0:T(4,128)S(1)} %broadcast_maximum_fusion, pred[256,2048]{0,1:T(8,128)(4,1)S(1)} %copy-done.2), kind=kLoop, calls=%fused_computation.5 | loop fusion | flops 15727104 | bytes 13119488 | tf_op jit(solution)/shard_map/reduce_sum | solution.py:176
  158.6 1.4 copy-done.1
  160.0 3.6 fusion.25
  163.7 1.5 convolution_convert_fusion.2
  165.4 1.2 reduce-window.11
  166.6 0.2 slice_reduce_fusion
  167.3 0.5 fusion.17
  167.7 18.2 %reduce-scatter.2.cloned.1.call-done = bf16[64,1536]{1,0:T(8,128)(2,1)} async-done(((bf16[256,1536]{1,0:T(8,128)(2,1)}), bf16[64,1536]{1,0:T(8,128)(2,1)}) %reduce-scatter.2.cloned.1.call-update) | async-done | bytes 196624 | tf_op jit(solution)/shard_map/reduce_scatter | solution.py:187
  186.0 1.1 multiply_reduce_fusion.1
  187.1 3.0 convolution_convert_fusion.1
  190.1 4.3 broadcast_in_dim.153
  194.3 3.2 copy.111
  197.5 1.0 broadcast_in_dim.154
  198.5 98.7 %all_to_all.23 = bf16[16,160,1536]{2,0,1:T(8,128)(2,1)S(1)} all-to-all(bf16[16,160,1536]{2,0,1:T(8,128)(2,1)S(1)} %bitcast.150), channel_id=1, replica_groups=mesh['req'=8,'exp'=8,'hid'=4] {'exp','hid'}, dimensions={1} | all-to-all | bytes 15728640 | tf_op jit(solution)/shard_map/all_to_all | solution.py:220
  297.2 3.9 copy.112
  301.1 6.0 %convolution_bitcast_fusion.1 = f32[512,5,128]{2,0,1:T(8,128)S(1)} fusion(bf16[512,5,1536]{2,0,1:T(8,128)(2,1)} %bitcast.153, bf16[5,1536,128]{2,1,0:T(8,128)(2,1)} %param.35), kind=kOutput, calls=%fused_computation.23 | convolution fusion | flops 1006632960 | bytes 11141120 | tf_op jit(solution)/shard_map/red,edf->ref/dot_general | solution.py:54
  307.0 12.2 %convolution_convert_fusion = bf16[5,512,1536]{2,1,0:T(8,128)(2,1)} fusion(bf16[5,128,1536]{2,1,0:T(8,128)(2,1)S(1)} %copy-done, bf16[512,5,1536]{2,0,1:T(8,128)(2,1)} %bitcast.154, bf16[5,1536,128]{2,1,0:T(8,128)(2,1)} %param.36, f32[512,5,128]{2,0,1:T(8,128)S(1)} %convolution_bitcast_fusion.1), kind=kOutput, calls=%fused_computation.9 | convolution fusion | flops 2019164160 | bytes 20971520 | tf_op jit(solution)/shard_map/ref,efd->red/dot_general | solution.py:61
  319.2 7.0 %copy.113 = bf16[32,16,5,1536]{3,1,2,0:T(8,128)(2,1)} copy(bf16[32,16,5,1536]{3,1,0,2:T(8,128)(2,1)} %bitcast.155) | data formatting | bytes 15728640 | tf_op jit(solution)/shard_map/reshape | solution.py:226
  326.3 6.2 %all-to-all-start.1 = ((bf16[16,160,1536]{2,0,1:T(8,128)(2,1)}), bf16[16,160,1536]{2,0,1:T(8,128)(2,1)}, u32[]{:S(2)}, u32[]{:S(2)}) async-start(bf16[16,160,1536]{2,0,1:T(8,128)(2,1)} %bitcast.149), calls=%async_computation.2 | async-start | bytes 15728640 | tf_op jit(solution)/shard_map/all_to_all | solution.py:228
  332.7 0.7 copy.104
  333.4 90.9 %all-to-all-done.1 = bf16[16,160,1536]{2,0,1:T(8,128)(2,1)} async-done(((bf16[16,160,1536]{2,0,1:T(8,128)(2,1)}), bf16[16,160,1536]{2,0,1:T(8,128)(2,1)}, u32[]{:S(2)}, u32[]{:S(2)}) %all-to-all-start.1) | async-done | bytes 7864352 | tf_op jit(solution)/shard_map/all_to_all | solution.py:228
  424.3 6.7 %reduce_sum.104 = bf16[16,8,5,1536]{3,0,2,1:T(8,128)(2,1)} reduce(bf16[16,8,4,5,1536]{4,0,3,2,1:T(8,128)(2,1)} %bitcast.41, bf16[]{:T(256)} %constant.141.clone.1), dimensions={2}, to_apply=%region_15.16 | reduce | flops 2949120 | bytes 9830402 | tf_op jit(solution)/shard_map/reduce_sum | solution.py:230
  431.0 4.3 copy.114
  435.3 4.3 reshape.396
  439.6 5.4 %gather_fusion.1 = bf16[512,1536]{1,0:T(8,128)(2,1)S(1)} fusion(bf16[640,1536]{1,0:T(8,128)(2,1)} %reshape.396, s32[1024]{0:T(1024)S(1)} %pad_clamp_fusion), kind=kCustom, calls=%fused_computation.1 | custom fusion | bytes 3147776 | tf_op jit(solution)/shard_map/jit(_take)/gather | solution.py:232
  445.0 2.8 multiply_reduce_fusion
  (83 shorter events, 1.6 us)
Async XLA Ops:
  7.2 299.9 %copy-start = (bf16[5,128,1536]{2,1,0:T(8,128)(2,1)S(1)}, bf16[5,128,1536]{2,1,0:T(8,128)(2,1)}, u32[]{:S(2)}) copy-start(bf16[5,128,1536]{2,1,0:T(8,128)(2,1)} %param.37) | copy-start | bytes 5898244
  7.2 104.2 %all-reduce.2.cloned.1.call-start = ((), (), s32[]{:S(2)}) async-start(), calls=%async_computation.3 | async-start | bytes 917504 | tf_op jit(solution)/shard_map/psum | solution.py:122
  11.7 29.6 %copy-start.15 = (s32[8,4]{0,1:T(4,128)S(1)}, s32[8,4]{0,1:T(4,128)}, u32[]{:S(2)}) copy-start(s32[8,4]{0,1:T(4,128)} %param.30) | copy-start | bytes 388
  11.7 29.8 %copy-start.19 = (s32[64]{0:T(128)S(1)}, s32[64]{0:T(128)}, u32[]{:S(2)}) copy-start(s32[64]{0:T(128)} %param.31) | copy-start | bytes 772
  42.7 2.6 copy-start.20
  42.7 3.1 copy-start.3
  42.7 3.1 copy-start.17
  43.8 4.6 %copy-start.16 = (bf16[1536,128]{1,0:T(8,128)(2,1)S(1)}, bf16[1536,128]{1,0:T(8,128)(2,1)}, u32[]{:S(2)}) copy-start(bf16[1536,128]{1,0:T(8,128)(2,1)} %param.22) | copy-start | bytes 1179652
  43.8 142.1 %reduce-scatter.2.cloned.1.call-start = ((), (), s32[]{:S(2)}) async-start(), calls=%async_computation.4 | async-start | bytes 983040 | tf_op jit(solution)/shard_map/reduce_scatter | solution.py:187
  50.4 0.6 copy-start.8
  50.4 0.6 copy-start.10
  122.3 3.4 copy-start.7
  122.3 3.9 copy-start.9
  122.3 3.9 copy-start.11
  122.3 3.9 copy-start.2
  126.2 7.8 %slice-start = ((bf16[4,57344]{1,0:T(4,128)(2,1)}), bf16[4,2048]{1,0:T(4,128)(2,1)S(1)}, s32[]{:S(2)}) async-start(bf16[4,57344]{1,0:T(4,128)(2,1)} %all-reduce.2.cloned.1.call-done), calls=%async_computation.5 | async-start | bytes 32768 | tf_op jit(solution)/shard_map/slice | solution.py:126
  126.2 8.0 %copy-start.4 = (bf16[256,1536]{1,0:T(8,128)(2,1)S(1)}, bf16[256,1536]{1,0:T(8,128)(2,1)}, u32[]{:S(2)}) copy-start(bf16[256,1536]{1,0:T(8,128)(2,1)} %param.19) | copy-start | bytes 2359300
  126.2 8.0 %copy-start.18 = (f32[1536]{0:T(1024)S(1)}, f32[1536]{0:T(1024)}, u32[]{:S(2)}) copy-start(f32[1536]{0:T(1024)} %param.20) | copy-start | bytes 18436
  151.8 8.2 %copy-start.1 = (f32[2,2048,256,3]{2,1,3,0:T(8,128)S(1)}, f32[2,2048,256,3]{2,1,3,0:T(8,128)}, u32[]{:S(2)}) copy-start(f32[2,2048,256,3]{2,1,3,0:T(8,128)} %get-tuple-element.17) | copy-start | bytes 37748740
  160.0 3.6 copy-start.6
  163.6 1.5 copy-start.12
  163.6 22.4 %copy-start.5 = (bf16[256,1536]{1,0:T(8,128)(2,1)S(1)}, bf16[256,1536]{1,0:T(8,128)(2,1)}, u32[]{:S(2)}) copy-start(bf16[256,1536]{1,0:T(8,128)(2,1)} %param.19) | copy-start | bytes 2359300
  163.6 23.5 %copy-start.13 = (f32[1536]{0:T(1024)S(1)}, f32[1536]{0:T(1024)}, u32[]{:S(2)}) copy-start(f32[1536]{0:T(1024)} %param.32) | copy-start | bytes 18436
  326.3 6.4 %copy-start.14 = (f32[64,8]{0,1:T(8,128)S(1)}, f32[64,8]{0,1:T(8,128)}, u32[]{:S(2)}) copy-start(f32[64,8]{0,1:T(8,128)} %param.34) | copy-start | bytes 6148
  326.3 98.0 %all-to-all-start.1 = ((bf16[16,160,1536]{2,0,1:T(8,128)(2,1)}), bf16[16,160,1536]{2,0,1:T(8,128)(2,1)}, u32[]{:S(2)}, u32[]{:S(2)}) async-start(bf16[16,160,1536]{2,0,1:T(8,128)(2,1)} %bitcast.149), calls=%async_computation.2 | async-start | bytes 15728640 | tf_op jit(solution)/shard_map/all_to_all | solution.py:228
Sparse Core Ops, SparseCore 0:
  43.9 67.4 all-reduce.1
  165.3 20.6 reduce-scatter.1

commit v3 on v2

--- a/solution.py
+++ b/solution.py
@@ -109,7 +109,10 @@
     bank_local = query_down_factor.shape[0]
     up_q = lax.dynamic_slice_in_dim(query_up_factor, hid_index * query_cols, query_cols, 2)
     up_v = lax.dynamic_slice_in_dim(value_up_factor, hid_index * kv_cols, kv_cols, 2)
-    parts_in = (query_down_factor, up_q, value_down_factor, up_v)
+    down_rows = width // hid_count
+    down_q = lax.dynamic_slice_in_dim(query_down_factor, hid_index * down_rows, down_rows, 1)
+    down_v = lax.dynamic_slice_in_dim(value_down_factor, hid_index * down_rows, down_rows, 1)
+    parts_in = (down_q, up_q, down_v, up_v)
     part_shapes = [p.shape[1:] for p in parts_in]
     part_sizes = [p.shape[1] * p.shape[2] for p in parts_in]
     bank = jnp.concatenate([p.reshape(bank_local, -1) for p in parts_in], axis=1)
@@ -128,21 +131,27 @@
     qa_sel, qb_sel, va_sel, vb_sel = chosen
     normed_rows = rms_norm(layer_input_rows, attention_norm_gain)
 
-    def low_rank_term(a_sel, b_sel, width_cols, offset):
+    normed_slice = lax.dynamic_slice_in_dim(normed_rows, hid_index * down_rows, down_rows, 1)
+
+    def inner_part(a_sel):
         inner_terms = jnp.einsum(
-            "td,jdr->tjr", normed_rows, a_sel, preferred_element_type=jnp.float32
+            "td,jdr->tjr", normed_slice, a_sel, preferred_element_type=jnp.float32
         )
-        inner_terms = (
-            jnp.where(member[:, :, None], inner_terms, 0.0)
-            .reshape(query_rows, requests * adapter_rank_size)
-            .astype(jnp.bfloat16)
-        )
+        return jnp.sum(jnp.where(member[:, :, None], inner_terms, 0.0), axis=1)
+
+    inner_both = lax.psum(
+        jnp.concatenate([inner_part(qa_sel), inner_part(va_sel)], axis=1), "hid"
+    ).astype(jnp.bfloat16)
+
+    def low_rank_term(inner_own, b_sel, width_cols):
+        inner_terms = jnp.where(member[:, :, None], inner_own[:, None, :], jnp.zeros_like(inner_own[:, None, :]))
+        inner_terms = inner_terms.reshape(query_rows, requests * adapter_rank_size)
         right_factor = b_sel.reshape(requests * adapter_rank_size, width_cols)
         return jnp.dot(inner_terms, right_factor, preferred_element_type=jnp.float32)
 
     query_matrix = jnp.dot(
         normed_rows, query_weight, preferred_element_type=jnp.float32
-    ) + low_rank_term(qa_sel, qb_sel, query_cols, hid_index * query_cols)
+    ) + low_rank_term(inner_both[:, :adapter_rank_size], qb_sel, query_cols)
     query_matrix = rotary(query_matrix.reshape(query_rows, q_local, HEAD_WIDTH), position).astype(
         jnp.bfloat16
     )
@@ -155,7 +164,7 @@
     )
     values_own = jnp.dot(
         normed_rows, value_weight, preferred_element_type=jnp.float32
-    ) + low_rank_term(va_sel, vb_sel, kv_cols, hid_index * kv_cols)
+    ) + low_rank_term(inner_both[:, adapter_rank_size:], vb_sel, kv_cols)
     values_own = values_own.astype(jnp.bfloat16)
     running_max = jnp.full((kv_local, group_share, query_rows), neg_large, jnp.float32)
     key_piece = lax.all_gather(keys_own, "exp", axis=0, tiled=True)

time: 459 us -> 477 us (1.039)
  blocking collectives: 162 us -> 173 us
    psum x0 -> x1, blocking collectives: none -> 11.2 us  [per_device(): lax.psum(jnp.concatenate([inner_part(qa_sel), inner_part(va_sel)], axis=1...]
    all_gather x1, blocking collectives: 28.5 us -> 23.2 us  [per_device(): along_req = lax.all_gather(bank, 'req', axis=0, tiled=True)]
where the time goes in v3:
time: 477 us; the launch traced here: 473 us
  blocking collectives  173 us (36%)
  waiting for transfers between devices  150 us (31%)
  local copies, waits for them, and re-layouts  55.4 us (12%)
  matrix products  46.1 us (10%)
  other arithmetic  28.4 us (6%)
  between operations  14.5 us (3%)
  starting transfers between devices  6.26 us (1%)
    all_to_all x1, blocking collectives, per_device(): lax.all_to_all(copies, ('exp', 'hid'), split_axis=1, concat_axis=0, tiled...  98.7 us
    all_to_all x1, waiting for transfers between devices, per_device(): lax.all_to_all(partials, ('exp', 'hid'), split_axis=1, concat_axis=1, til...  90.9 us
    psum x1, waiting for transfers between devices, per_device(): rows_pick = lax.psum(rows_pick, 'exp')  39.7 us
    all_gather x1, blocking collectives, per_device(): along_req = lax.all_gather(bank, 'req', axis=0, tiled=True)  23.2 us
    all_gather x1, blocking collectives, per_device(): key_piece = lax.all_gather(keys_own, 'exp', axis=0, tiled=True)  21.4 us
    reduce_scatter x1, waiting for transfers between devices, per_device(): lax.psum_scatter(jnp.dot(attended, attention_output_weight, preferred_ele...  19.2 us
    all_gather x1, blocking collectives, per_device(): value_piece = lax.all_gather(values_own, 'exp', axis=0, tiled=True)  17.9 us
    dot_general x1, matrix products, expert_rows(): jnp.einsum('ref,efd->red', hidden, expert_down_weight, preferred_element_...  12.2 us
  transfers between devices with their start and end apart: 3, of which 3 were waited for; matrix products, arithmetic and copies ran while one was open for 2% of the time, Pallas kernels for 0%

profile of v3, /device:TPU:3, one launch (start us, length us, event | category | flops | bytes accessed | tf_op | source)
XLA Modules:
  0.0 473.0 jit_solution(13980971819895035935)
XLA Ops:
  7.3 0.9 constant_dynamic-slice_fusion
  8.7 0.7 dynamic-slice_bitcast_fusion
  9.4 0.7 dynamic-slice_bitcast_fusion.1
  10.2 23.2 %all-gather = bf16[8,1,20480]{2,1,0:T(2,128)(2,1)S(1)} all-gather(bf16[1,1,20480]{2,1,0:T(2,128)(2,1)S(1)} %maximum_bitcast_fusion), channel_id=1, replica_groups=mesh['req'=8,'exp'=8,'hid'=4] {'req'}, dimensions={0}, use_global_device_ids=true | all-gather | bytes 368640 | tf_op jit(solution)/shard_map/all_gather | solution.py:119
  33.4 0.4 copy.126
  34.3 0.7 gather_fusion
  35.0 0.8 select_select_fusion
  35.9 0.5 multiply_power_fusion
  37.1 0.2 fusion.9
  37.4 2.6 fusion.60
  40.0 1.4 fusion.59
  41.6 0.6 copy-done.7
  42.2 21.4 %all_gather.9 = bf16[2048,128]{0,1:T(8,128)(2,1)} all-gather(bf16[256,128]{0,1:T(8,128)(2,1)S(1)} %bitcast.165), channel_id=1, replica_groups=mesh['req'=8,'exp'=8,'hid'=4] {'exp'}, dimensions={0}, use_global_device_ids=true | all-gather | bytes 589824 | tf_op jit(solution)/shard_map/all_gather | solution.py:170
  63.6 1.2 fusion.6
  64.9 39.7 %all-reduce.2.cloned.1.call-done = bf16[4,20480]{1,0:T(4,128)(2,1)} async-done(((bf16[4,20480]{1,0:T(4,128)(2,1)}), bf16[4,20480]{1,0:T(4,128)(2,1)}) %all-reduce.2.cloned.1.call-update) | async-done | bytes 163856 | tf_op jit(solution)/shard_map/psum | solution.py:125
  104.6 1.5 fusion.57
  106.1 1.9 reshape.413
  108.0 1.8 copy.100
  109.7 1.6 fusion.37
  111.3 1.9 reshape.412
  113.2 1.8 copy.99
  114.9 1.0 fusion.39
  115.9 0.9 select_reduce_fusion.1
  116.8 0.6 pad_maximum_fusion.1
  117.4 11.2 %psum.15 = bf16[256,32]{0,1:T(8,128)(2,1)S(1)} all-reduce(f32[256,32]{0,1:T(8,128)} %pad_maximum_fusion.1), channel_id=1, replica_groups=mesh['req'=8,'exp'=8,'hid'=4] {'hid'}, use_global_device_ids=true, to_apply=%region_9.10 | all-reduce | flops 8192 | bytes 49152 | tf_op jit(solution)/shard_map/psum | solution.py:142
  128.7 0.6 fusion.58
  129.3 1.5 reshape_reshape.7
  130.7 1.3 broadcast_select_fusion.1
  132.1 2.0 convolution_add_fusion
  134.1 1.9 copy.101
  136.0 1.1 subtract_convert_fusion
  137.1 7.8 %fusion = (f32[2,3,256]{2,1,0:T(4,128)S(1)}, f32[2,2048,256,3]{2,1,3,0:T(8,128)}) fusion(pred[256,2048]{0,1:T(8,128)(4,1)} %fusion.6, bf16[2048,2,64,1]{0,2,3,1:T(8,128)(2,1)} %bitcast.161, bf16[256,2,3,32]{0,3,2,1:T(8,128)(2,1)S(1)} %bitcast.172, bf16[256,2,3,32]{0,3,2,1:T(8,128)(2,1)S(1)} %bitcast.171), kind=kOutput, calls=%fused_computation.4 | convolution fusion | flops 412482048 | bytes 13834240 | tf_op jit(solution)/shard_map/qkgh,nkh->kgqn/dot_general | solution.py:179
  144.9 0.6 broadcast_maximum_fusion
  145.5 0.6 reshape_reshape.8
  146.1 1.0 fusion.61
  147.1 1.4 fusion.21
  148.4 17.9 %all_gather.11 = bf16[2048,128]{1,0:T(8,128)(2,1)S(1)} all-gather(bf16[256,128]{1,0:T(8,128)(2,1)S(1)} %fusion.21), channel_id=1, replica_groups=mesh['req'=8,'exp'=8,'hid'=4] {'exp'}, dimensions={0}, use_global_device_ids=true | all-gather | bytes 589824 | tf_op jit(solution)/shard_map/all_gather | solution.py:171
  166.3 1.1 copy.102
  167.4 7.5 %fusion.1 = f32[2,3,256]{2,1,0:T(4,128)S(1)} fusion(f32[2,2048,256,3]{2,1,3,0:T(8,128)} %get-tuple-element.22, f32[2,3,256]{2,1,0:T(4,128)S(1)} %copy-done.9, pred[256,2048]{0,1:T(8,128)(4,1)} %fusion.6), kind=kLoop, calls=%fused_computation.5 | loop fusion | flops 15727104 | bytes 13119488 | tf_op jit(solution)/shard_map/reduce_sum | solution.py:185
  174.9 0.9 copy-done.1
  175.8 4.7 fusion.25
  180.6 1.5 convolution_convert_fusion.2
  182.4 0.4 copy-done.5
  182.8 1.2 reduce-window.11
  184.6 0.5 fusion.17
  185.1 19.2 %reduce-scatter.2.cloned.1.call-done = bf16[64,1536]{1,0:T(8,128)(2,1)} async-done(((bf16[256,1536]{1,0:T(8,128)(2,1)}), bf16[64,1536]{1,0:T(8,128)(2,1)}) %reduce-scatter.2.cloned.1.call-update) | async-done | bytes 196624 | tf_op jit(solution)/shard_map/reduce_scatter | solution.py:196
  204.3 1.1 multiply_reduce_fusion.1
  205.4 3.0 convolution_convert_fusion.1
  208.4 4.3 broadcast_in_dim.193
  212.7 3.2 copy.111
  215.8 1.0 broadcast_in_dim.194
  216.8 98.7 %all_to_all.23 = bf16[16,160,1536]{2,0,1:T(8,128)(2,1)S(1)} all-to-all(bf16[16,160,1536]{2,0,1:T(8,128)(2,1)S(1)} %bitcast.153), channel_id=1, replica_groups=mesh['req'=8,'exp'=8,'hid'=4] {'exp','hid'}, dimensions={1} | all-to-all | bytes 15728640 | tf_op jit(solution)/shard_map/all_to_all | solution.py:229
  315.6 3.9 copy.112
  319.4 6.0 %convolution_bitcast_fusion.1 = f32[512,5,128]{2,0,1:T(8,128)S(1)} fusion(bf16[512,5,1536]{2,0,1:T(8,128)(2,1)} %bitcast.156, bf16[5,1536,128]{2,1,0:T(8,128)(2,1)} %param.35), kind=kOutput, calls=%fused_computation.23 | convolution fusion | flops 1006632960 | bytes 11141120 | tf_op jit(solution)/shard_map/red,edf->ref/dot_general | solution.py:54
  325.4 12.2 %convolution_convert_fusion = bf16[5,512,1536]{2,1,0:T(8,128)(2,1)} fusion(bf16[5,128,1536]{2,1,0:T(8,128)(2,1)S(1)} %copy-done, bf16[512,5,1536]{2,0,1:T(8,128)(2,1)} %bitcast.157, bf16[5,1536,128]{2,1,0:T(8,128)(2,1)} %param.36, f32[512,5,128]{2,0,1:T(8,128)S(1)} %convolution_bitcast_fusion.1), kind=kOutput, calls=%fused_computation.9 | convolution fusion | flops 2019164160 | bytes 20971520 | tf_op jit(solution)/shard_map/ref,efd->red/dot_general | solution.py:61
  337.6 7.0 %copy.113 = bf16[32,16,5,1536]{3,1,2,0:T(8,128)(2,1)} copy(bf16[32,16,5,1536]{3,1,0,2:T(8,128)(2,1)} %bitcast.158) | data formatting | bytes 15728640 | tf_op jit(solution)/shard_map/reshape | solution.py:235
  344.7 6.2 %all-to-all-start.1 = ((bf16[16,160,1536]{2,0,1:T(8,128)(2,1)}), bf16[16,160,1536]{2,0,1:T(8,128)(2,1)}, u32[]{:S(2)}, u32[]{:S(2)}) async-start(bf16[16,160,1536]{2,0,1:T(8,128)(2,1)} %bitcast.152), calls=%async_computation.2 | async-start | bytes 15728640 | tf_op jit(solution)/shard_map/all_to_all | solution.py:237
  351.1 0.7 copy.104
  351.8 90.9 %all-to-all-done.1 = bf16[16,160,1536]{2,0,1:T(8,128)(2,1)} async-done(((bf16[16,160,1536]{2,0,1:T(8,128)(2,1)}), bf16[16,160,1536]{2,0,1:T(8,128)(2,1)}, u32[]{:S(2)}, u32[]{:S(2)}) %all-to-all-start.1) | async-done | bytes 7864352 | tf_op jit(solution)/shard_map/all_to_all | solution.py:237
  442.7 6.7 %reduce_sum.124 = bf16[16,8,5,1536]{3,0,2,1:T(8,128)(2,1)} reduce(bf16[16,8,4,5,1536]{4,0,3,2,1:T(8,128)(2,1)} %bitcast.41, bf16[]{:T(256)} %constant.142.clone.1), dimensions={2}, to_apply=%region_18.19 | reduce | flops 2949120 | bytes 9830402 | tf_op jit(solution)/shard_map/reduce_sum | solution.py:239
  449.4 4.3 copy.114
  453.7 4.3 reshape.422
  458.0 5.4 %gather_fusion.1 = bf16[512,1536]{1,0:T(8,128)(2,1)S(1)} fusion(bf16[640,1536]{1,0:T(8,128)(2,1)} %reshape.422, s32[1024]{0:T(1024)S(1)} %pad_clamp_fusion), kind=kCustom, calls=%fused_computation.1 | custom fusion | bytes 3147776 | tf_op jit(solution)/shard_map/jit(_take)/gather | solution.py:241
  463.4 2.8 multiply_reduce_fusion
  (84 shorter events, 3.3 us)
Async XLA Ops:
  7.2 318.2 %copy-start = (bf16[5,128,1536]{2,1,0:T(8,128)(2,1)S(1)}, bf16[5,128,1536]{2,1,0:T(8,128)(2,1)}, u32[]{:S(2)}) copy-start(bf16[5,128,1536]{2,1,0:T(8,128)(2,1)} %param.37) | copy-start | bytes 5898244
  7.2 26.6 %copy-start.15 = (s32[8,4]{0,1:T(4,128)S(1)}, s32[8,4]{0,1:T(4,128)}, u32[]{:S(2)}) copy-start(s32[8,4]{0,1:T(4,128)} %param.30) | copy-start | bytes 388
  7.2 26.8 %copy-start.17 = (s32[64]{0:T(128)S(1)}, s32[64]{0:T(128)}, u32[]{:S(2)}) copy-start(s32[64]{0:T(128)} %param.31) | copy-start | bytes 772
  7.2 97.4 %all-reduce.2.cloned.1.call-start = ((), (), s32[]{:S(2)}) async-start(), calls=%async_computation.3 | async-start | bytes 327680 | tf_op jit(solution)/shard_map/psum | solution.py:125
  8.4 28.0 %copy-start.2 = (bf16[256,1536]{1,0:T(8,128)(2,1)S(1)}, bf16[256,1536]{1,0:T(8,128)(2,1)}, u32[]{:S(2)}) copy-start(bf16[256,1536]{1,0:T(8,128)(2,1)} %param.19) | copy-start | bytes 2359300
  10.2 26.4 %copy-start.18 = (s32[1,4]{1,0:T(1,128)S(1)}, s32[1,4]{1,0:T(1,128)}, u32[]{:S(2)}) copy-start(s32[1,4]{1,0:T(1,128)} %param.29) | copy-start | bytes 52
  10.2 26.9 %copy-start.12 = (f32[1536]{0:T(1024)S(1)}, f32[1536]{0:T(1024)}, u32[]{:S(2)}) copy-start(f32[1536]{0:T(1024)} %param.20) | copy-start | bytes 18436
  35.8 168.5 %reduce-scatter.2.cloned.1.call-start = ((), (), s32[]{:S(2)}) async-start(), calls=%async_computation.4 | async-start | bytes 983040 | tf_op jit(solution)/shard_map/reduce_scatter | solution.py:196
  37.4 4.0 copy-start.16
  41.6 0.6 copy-start.7
  41.6 0.6 copy-start.8
  64.9 51.9 %copy-start.11 = (pred[256,4]{0,1:T(4,128)(4,1)}, pred[256,4]{0,1:T(4,128)(4,1)S(1)}, u32[]{:S(2)}) copy-start(pred[256,4]{0,1:T(4,128)(4,1)S(1)} %iota_compare_fusion.5) | copy-start | bytes 3076
  137.1 8.4 %slice-start = ((bf16[4,20480]{1,0:T(4,128)(2,1)}), bf16[4,2048]{1,0:T(4,128)(2,1)S(1)}, s32[]{:S(2)}) async-start(bf16[4,20480]{1,0:T(4,128)(2,1)} %all-reduce.2.cloned.1.call-done), calls=%async_computation.5 | async-start | bytes 32768 | tf_op jit(solution)/shard_map/slice | solution.py:129
  146.1 21.3 %copy-start.9 = (f32[2,3,256]{2,1,0:T(4,128)S(1)}, f32[2,3,256]{2,1,0:T(4,128)}, u32[]{:S(2)}) copy-start(f32[2,3,256]{2,1,0:T(4,128)} %broadcast_maximum_fusion) | copy-start | bytes 18436
  167.4 8.4 %copy-start.1 = (f32[2,2048,256,3]{2,1,3,0:T(8,128)S(1)}, f32[2,2048,256,3]{2,1,3,0:T(8,128)}, u32[]{:S(2)}) copy-start(f32[2,2048,256,3]{2,1,3,0:T(8,128)} %get-tuple-element.22) | copy-start | bytes 37748740
  167.4 8.4 %copy-start.3 = (pred[256,2048]{0,1:T(8,128)(4,1)S(1)}, pred[256,2048]{0,1:T(8,128)(4,1)}, u32[]{:S(2)}) copy-start(pred[256,2048]{0,1:T(8,128)(4,1)} %fusion.6) | copy-start | bytes 1572868
  175.8 4.8 %copy-start.4 = (bf16[384,1536]{1,0:T(8,128)(2,1)S(1)}, bf16[384,1536]{1,0:T(8,128)(2,1)}, u32[]{:S(2)}) copy-start(bf16[384,1536]{1,0:T(8,128)(2,1)} %param.24) | copy-start | bytes 3538948
  180.6 1.5 copy-start.10
  180.6 24.9 %copy-start.13 = (f32[1536]{0:T(1024)S(1)}, f32[1536]{0:T(1024)}, u32[]{:S(2)}) copy-start(f32[1536]{0:T(1024)} %param.32) | copy-start | bytes 18436
  182.2 0.6 copy-start.5
  344.7 6.2 %copy-start.6 = (s32[64,8]{1,0:T(8,128)S(1)}, s32[64,8]{1,0:T(8,128)}, u32[]{:S(2)}) copy-start(s32[64,8]{1,0:T(8,128)} %copy-done.5) | copy-start | bytes 6148
  344.7 6.4 %copy-start.14 = (f32[64,8]{0,1:T(8,128)S(1)}, f32[64,8]{0,1:T(8,128)}, u32[]{:S(2)}) copy-start(f32[64,8]{0,1:T(8,128)} %param.34) | copy-start | bytes 6148
  344.7 98.0 %all-to-all-start.1 = ((bf16[16,160,1536]{2,0,1:T(8,128)(2,1)}), bf16[16,160,1536]{2,0,1:T(8,128)(2,1)}, u32[]{:S(2)}, u32[]{:S(2)}) async-start(bf16[16,160,1536]{2,0,1:T(8,128)(2,1)} %bitcast.152), calls=%async_computation.2 | async-start | bytes 15728640 | tf_op jit(solution)/shard_map/all_to_all | solution.py:237
Sparse Core Ops, SparseCore 0:
  35.9 68.5 all-reduce.1
  182.2 22.0 reduce-scatter.1

commit v4 on v2

--- a/solution.py
+++ b/solution.py
@@ -119,7 +119,16 @@
     mine = (home_dev % exp_count) == exp_index
     rows_pick = jnp.take(along_req, home_pick, axis=0)
     rows_pick = jnp.where(mine[:, None], rows_pick, jnp.zeros_like(rows_pick))
-    rows_pick = lax.psum(rows_pick, "exp")
+    rows_pick = jnp.sum(
+        lax.all_to_all(
+            jnp.broadcast_to(rows_pick[None], (exp_count,) + rows_pick.shape),
+            "exp",
+            split_axis=0,
+            concat_axis=0,
+            tiled=True,
+        ).astype(jnp.float32),
+        axis=0,
+    ).astype(jnp.bfloat16)
     chosen = []
     start = 0
     for shape_in, size_in in zip(part_shapes, part_sizes):
@@ -184,14 +193,10 @@
     attended = (running_out / running_sum[..., None]).astype(jnp.bfloat16)
     attended = jnp.transpose(attended, (2, 0, 1, 3)).reshape(query_rows, query_cols)
     tok_rows = query_rows // hid_count
-    attn_out = lax.psum_scatter(
-        jnp.dot(attended, attention_output_weight, preferred_element_type=jnp.float32).astype(
-            jnp.bfloat16
-        ),
-        "hid",
-        scatter_dimension=0,
-        tiled=True,
-    )
+    head_sums = jnp.dot(attended, attention_output_weight, preferred_element_type=jnp.float32)
+    head_sums = head_sums.astype(jnp.bfloat16).reshape(hid_count, tok_rows, width)
+    head_sums = lax.all_to_all(head_sums, "hid", split_axis=0, concat_axis=0, tiled=True)
+    attn_out = jnp.sum(head_sums.astype(jnp.float32), axis=0).astype(jnp.bfloat16)
     own_rows = lax.dynamic_slice_in_dim(layer_input_rows, hid_index * tok_rows, tok_rows, 0)
     mixed_rows = own_rows.astype(jnp.float32) + residual_mult * attn_out.astype(jnp.float32)
     normed_moe = rms_norm(mixed_rows, expert_norm_gain)

time: 459 us -> 435 us (0.948)
  waiting for transfers between devices: 150 us -> 101 us
  blocking collectives: 162 us -> 185 us
  between operations: 14.6 us -> 1.23 us
  starting transfers between devices: 6.26 us -> 19.6 us
    psum x1 -> x0, waiting for transfers between devices: 41.2 us -> none  [per_device(): rows_pick = lax.psum(rows_pick, 'exp')]
    all_gather x1, blocking collectives: 19.2 us -> 48.8 us  [per_device(): key_piece = lax.all_gather(keys_own, 'exp', axis=0, tiled=True)]
    reduce_scatter x1 -> x0, waiting for transfers between devices: 18.2 us -> none  [per_device(): lax.psum_scatter(jnp.dot(attended, attention_output_weight, preferred_ele...]
    all_to_all x0 -> x2, starting transfers between devices: none -> 13.4 us  [the longest x1 9.02 us: per_device(): lax.all_to_all(jnp.broadcast_to(rows_pick[None], (exp_count,) + rows_pick...]
    all_to_all x0 -> x2, waiting for transfers between devices: none -> 9.91 us  [the longest x1 9.91 us: per_device(): lax.all_to_all(head_sums, 'hid', split_axis=0, concat_axis=0, tiled=True)]
  transfers between devices with their start and end apart: 3 -> 3, of which waited for: 3 -> 2; matrix products, arithmetic and copies ran while one was open for 2% -> 2% of each run, Pallas kernels for 0% -> 0%
where the time goes in v4:
time: 435 us; the launch traced here: 431 us
  blocking collectives  185 us (43%)
  waiting for transfers between devices  101 us (23%)
  local copies, waits for them, and re-layouts  55.6 us (13%)
  matrix products  41.6 us (10%)
  other arithmetic  27.1 us (6%)
  starting transfers between devices  19.6 us (5%)
    all_to_all x1, blocking collectives, per_device(): lax.all_to_all(copies, ('exp', 'hid'), split_axis=1, concat_axis=0, tiled...  94.7 us
    all_to_all x1, waiting for transfers between devices, per_device(): lax.all_to_all(partials, ('exp', 'hid'), split_axis=1, concat_axis=1, til...  90.9 us
    all_gather x1, blocking collectives, per_device(): key_piece = lax.all_gather(keys_own, 'exp', axis=0, tiled=True)  48.8 us
    all_gather x1, blocking collectives, per_device(): along_req = lax.all_gather(bank, 'req', axis=0, tiled=True)  28.5 us
    all_gather x1, blocking collectives, per_device(): value_piece = lax.all_gather(values_own, 'exp', axis=0, tiled=True)  13.3 us
    dot_general x1, matrix products, expert_rows(): jnp.einsum('ref,efd->red', hidden, expert_down_weight, preferred_element_...  12.2 us
    all_to_all x1, waiting for transfers between devices, per_device(): lax.all_to_all(head_sums, 'hid', split_axis=0, concat_axis=0, tiled=True)  9.91 us
    all_to_all x1, starting transfers between devices, per_device(): lax.all_to_all(jnp.broadcast_to(rows_pick[None], (exp_count,) + rows_pick...  9.02 us
  transfers between devices with their start and end apart: 3, of which 2 were waited for; matrix products, arithmetic and copies ran while one was open for 2% of the time, Pallas kernels for 0%

profile of v4, /device:TPU:3, one launch (start us, length us, event | category | flops | bytes accessed | tf_op | source)
XLA Modules:
  0.0 431.3 jit_solution(5187815631940104938)
XLA Ops:
  0.7 0.9 dynamic-slice_bitcast_fusion
  1.5 0.7 dynamic-slice_bitcast_fusion.1
  2.2 1.0 copy.115
  3.3 0.3 reshape.410
  3.5 1.0 copy.116
  4.6 0.3 reshape.412
  4.8 0.2 maximum_bitcast_fusion
  5.1 28.5 %all-gather = bf16[8,1,57344]{2,1,0:T(2,128)(2,1)S(1)} all-gather(bf16[1,1,57344]{2,1,0:T(2,128)(2,1)S(1)} %maximum_bitcast_fusion), channel_id=1, replica_groups=mesh['req'=8,'exp'=8,'hid'=4] {'req'}, dimensions={0}, use_global_device_ids=true | all-gather | bytes 1032192 | tf_op jit(solution)/shard_map/all_gather | solution.py:116
  33.6 1.0 copy.150
  34.7 0.2 dynamic-slice_reduce_fusion
  35.1 1.0 gather_fusion
  36.1 0.3 select_select_fusion
  36.4 2.8 broadcast_in_dim.154
  39.2 9.0 %all-to-all-start = ((bf16[8,4,57344]{2,1,0:T(4,128)(2,1)}), bf16[8,4,57344]{2,1,0:T(4,128)(2,1)}, u32[]{:S(2)}, u32[]{:S(2)}) async-start(bf16[8,4,57344]{2,1,0:T(4,128)(2,1)} %broadcast_in_dim.154), calls=%async_computation | async-start | bytes 7340032 | tf_op jit(solution)/shard_map/all_to_all | solution.py:123
  48.4 1.2 reduce-window.11
  49.6 0.2 slice_reduce_fusion
  49.9 0.7 eq.112
  51.0 0.2 fusion.7
  51.3 0.2 multiply_cosine_fusion
  51.5 0.5 fusion.58
  52.1 48.8 %all_gather.9 = bf16[2048,128]{0,1:T(8,128)(2,1)} all-gather(bf16[256,128]{0,1:T(8,128)(2,1)S(1)} %bitcast.160), channel_id=1, replica_groups=mesh['req'=8,'exp'=8,'hid'=4] {'exp'}, dimensions={0}, use_global_device_ids=true | all-gather | bytes 589824 | tf_op jit(solution)/shard_map/all_gather | solution.py:170
  100.9 1.4 fusion.56
  102.3 1.2 fusion.6
  103.5 3.8 reduce_sum.125
  107.4 0.9 fusion.60
  108.3 0.6 slice.49
  108.9 2.1 reshape.414
  111.0 1.3 copy.118
  112.3 2.2 fusion.54
  114.5 2.1 reshape.416
  116.6 1.3 copy.120
  117.9 1.7 fusion.51
  119.6 0.8 reshape_reshape.7
  120.4 0.9 select_convert_fusion.1
  121.3 0.2 convolution_add_fusion
  121.8 7.7 %fusion = (f32[2,3,256]{2,1,0:T(4,128)S(1)}, f32[2,2048,256,3]{2,1,3,0:T(8,128)}) fusion(pred[256,2048]{0,1:T(8,128)(4,1)S(1)} %copy-done.2, bf16[2048,2,64,1]{0,2,3,1:T(8,128)(2,1)} %bitcast.158, bf16[256,2,3,32]{0,3,2,1:T(8,128)(2,1)S(1)} %bitcast.169, bf16[256,2,3,32]{0,3,2,1:T(8,128)(2,1)S(1)} %bitcast.168), kind=kOutput, calls=%fused_computation.4 | convolution fusion | flops 412482048 | bytes 13834240 | tf_op jit(solution)/shard_map/qkgh,nkh->kgqn/dot_general | solution.py:179
  129.8 1.4 fusion.21
  131.2 13.3 %all_gather.11 = bf16[2048,128]{1,0:T(8,128)(2,1)S(1)} all-gather(bf16[256,128]{1,0:T(8,128)(2,1)S(1)} %fusion.21), channel_id=1, replica_groups=mesh['req'=8,'exp'=8,'hid'=4] {'exp'}, dimensions={0}, use_global_device_ids=true | all-gather | bytes 589824 | tf_op jit(solution)/shard_map/all_gather | solution.py:171
  144.6 0.2 copy.121
  144.8 6.9 %fusion.1 = f32[2,3,256]{2,1,0:T(4,128)S(1)} fusion(f32[2,2048,256,3]{2,1,3,0:T(8,128)} %get-tuple-element.17, f32[2,3,256]{2,1,0:T(4,128)S(1)} %broadcast_maximum_fusion, pred[256,2048]{0,1:T(8,128)(4,1)S(1)} %copy-done.2), kind=kLoop, calls=%fused_computation.5 | loop fusion | flops 15727104 | bytes 13119488 | tf_op jit(solution)/shard_map/reduce_sum | solution.py:185
  151.7 1.4 copy-done.1
  153.0 3.6 fusion.25
  156.7 1.5 convolution_convert_fusion.2
  158.1 4.4 %all-to-all-start.1 = ((bf16[4,64,1536]{2,1,0:T(8,128)(2,1)}), bf16[4,64,1536]{2,1,0:T(8,128)(2,1)S(1)}, u32[]{:S(2)}, u32[]{:S(2)}) async-start(bf16[4,64,1536]{2,1,0:T(8,128)(2,1)} %bitcast.30), calls=%async_computation.1 | async-start | bytes 1572864 | tf_op jit(solution)/shard_map/all_to_all | solution.py:198
  162.9 0.5 fusion.17
  163.4 9.9 %all-to-all-done.1 = bf16[4,64,1536]{2,1,0:T(8,128)(2,1)S(1)} async-done(((bf16[4,64,1536]{2,1,0:T(8,128)(2,1)}), bf16[4,64,1536]{2,1,0:T(8,128)(2,1)S(1)}, u32[]{:S(2)}, u32[]{:S(2)}) %all-to-all-start.1) | async-done | bytes 786464 | tf_op jit(solution)/shard_map/all_to_all | solution.py:198
  173.5 1.2 multiply_reduce_fusion.1
  174.7 3.0 convolution_convert_fusion.1
  177.6 4.3 broadcast_in_dim.160
  181.9 3.2 copy.130
  185.1 1.0 broadcast_in_dim.161
  186.1 94.7 %all_to_all.33 = bf16[16,160,1536]{2,0,1:T(8,128)(2,1)S(1)} all-to-all(bf16[16,160,1536]{2,0,1:T(8,128)(2,1)S(1)} %bitcast.151), channel_id=1, replica_groups=mesh['req'=8,'exp'=8,'hid'=4] {'exp','hid'}, dimensions={1} | all-to-all | bytes 15728640 | tf_op jit(solution)/shard_map/all_to_all | solution.py:225
  280.7 3.9 copy.131
  284.6 6.0 %convolution_bitcast_fusion.1 = f32[512,5,128]{2,0,1:T(8,128)S(1)} fusion(bf16[512,5,1536]{2,0,1:T(8,128)(2,1)} %bitcast.154, bf16[5,1536,128]{2,1,0:T(8,128)(2,1)} %param.35), kind=kOutput, calls=%fused_computation.23 | convolution fusion | flops 1006632960 | bytes 11141120 | tf_op jit(solution)/shard_map/red,edf->ref/dot_general | solution.py:54
  290.6 12.2 %convolution_convert_fusion = bf16[5,512,1536]{2,1,0:T(8,128)(2,1)} fusion(bf16[5,128,1536]{2,1,0:T(8,128)(2,1)S(1)} %copy-done, bf16[512,5,1536]{2,0,1:T(8,128)(2,1)} %bitcast.155, bf16[5,1536,128]{2,1,0:T(8,128)(2,1)} %param.36, f32[512,5,128]{2,0,1:T(8,128)S(1)} %convolution_bitcast_fusion.1), kind=kOutput, calls=%fused_computation.9 | convolution fusion | flops 2019164160 | bytes 20971520 | tf_op jit(solution)/shard_map/ref,efd->red/dot_general | solution.py:61
  302.8 7.0 %copy.132 = bf16[32,16,5,1536]{3,1,2,0:T(8,128)(2,1)} copy(bf16[32,16,5,1536]{3,1,0,2:T(8,128)(2,1)} %bitcast.156) | data formatting | bytes 15728640 | tf_op jit(solution)/shard_map/reshape | solution.py:231
  309.8 6.2 %all-to-all-start.3 = ((bf16[16,160,1536]{2,0,1:T(8,128)(2,1)}), bf16[16,160,1536]{2,0,1:T(8,128)(2,1)}, u32[]{:S(2)}, u32[]{:S(2)}) async-start(bf16[16,160,1536]{2,0,1:T(8,128)(2,1)} %bitcast.150), calls=%async_computation.3 | async-start | bytes 15728640 | tf_op jit(solution)/shard_map/all_to_all | solution.py:233
  316.2 0.7 copy.123
  316.9 90.9 %all-to-all-done.3 = bf16[16,160,1536]{2,0,1:T(8,128)(2,1)} async-done(((bf16[16,160,1536]{2,0,1:T(8,128)(2,1)}), bf16[16,160,1536]{2,0,1:T(8,128)(2,1)}, u32[]{:S(2)}, u32[]{:S(2)}) %all-to-all-start.3) | async-done | bytes 7864352 | tf_op jit(solution)/shard_map/all_to_all | solution.py:233
  407.8 6.7 %reduce_sum.130 = bf16[16,8,5,1536]{3,0,2,1:T(8,128)(2,1)} reduce(bf16[16,8,4,5,1536]{4,0,3,2,1:T(8,128)(2,1)} %bitcast.42, bf16[]{:T(256)} %constant.143.clone.1), dimensions={2}, to_apply=%region_15.16 | reduce | flops 2949120 | bytes 9830402 | tf_op jit(solution)/shard_map/reduce_sum | solution.py:235
  414.5 4.3 %copy.133 = bf16[16,8,5,1536]{3,2,1,0:T(8,128)(2,1)} copy(bf16[16,8,5,1536]{3,0,2,1:T(8,128)(2,1)} %reduce_sum.130) | data formatting | bytes 3932160 | tf_op jit(solution)/shard_map/reduce_sum | solution.py:235
  418.9 4.3 reshape.425
  423.2 5.4 %gather_fusion.1 = bf16[512,1536]{1,0:T(8,128)(2,1)S(1)} fusion(bf16[640,1536]{1,0:T(8,128)(2,1)} %reshape.425, s32[1024]{0:T(1024)S(1)} %pad_clamp_fusion), kind=kCustom, calls=%fused_computation.1 | custom fusion | bytes 3147776 | tf_op jit(solution)/shard_map/jit(_take)/gather | solution.py:237
  428.6 2.8 multiply_reduce_fusion
  (105 shorter events, 2.2 us)
Async XLA Ops:
  0.6 289.9 %copy-start = (bf16[5,128,1536]{2,1,0:T(8,128)(2,1)S(1)}, bf16[5,128,1536]{2,1,0:T(8,128)(2,1)}, u32[]{:S(2)}) copy-start(bf16[5,128,1536]{2,1,0:T(8,128)(2,1)} %param.37) | copy-start | bytes 5898244
  5.1 29.6 %copy-start.22 = (s32[8,4]{0,1:T(4,128)S(1)}, s32[8,4]{0,1:T(4,128)}, u32[]{:S(2)}) copy-start(s32[8,4]{0,1:T(4,128)} %param.30) | copy-start | bytes 388
  5.1 29.8 %copy-start.29 = (s32[64]{0:T(128)S(1)}, s32[64]{0:T(128)}, u32[]{:S(2)}) copy-start(s32[64]{0:T(128)} %param.31) | copy-start | bytes 772
  39.2 9.0 %copy-start.17 = (s32[64,8]{0,1:T(8,128)S(1)}, s32[64,8]{0,1:T(8,128)}, u32[]{:S(2)}) copy-start(s32[64,8]{0,1:T(8,128)} %param.33) | copy-start | bytes 6148
  39.2 11.3 %copy-start.30 = (s32[1,4]{1,0:T(1,128)S(1)}, s32[1,4]{1,0:T(1,128)}, u32[]{:S(2)}) copy-start(s32[1,4]{1,0:T(1,128)} %param.29) | copy-start | bytes 52
  39.2 11.8 %copy-start.5 = (bf16[256,1536]{1,0:T(8,128)(2,1)S(1)}, bf16[256,1536]{1,0:T(8,128)(2,1)}, u32[]{:S(2)}) copy-start(bf16[256,1536]{1,0:T(8,128)(2,1)} %param.19) | copy-start | bytes 2359300
  39.2 12.3 %copy-start.26 = (bf16[1536,128]{1,0:T(8,128)(2,1)S(1)}, bf16[1536,128]{1,0:T(8,128)(2,1)}, u32[]{:S(2)}) copy-start(bf16[1536,128]{1,0:T(8,128)(2,1)} %param.22) | copy-start | bytes 1179652
  39.2 12.3 %copy-start.27 = (f32[1536]{0:T(1024)S(1)}, f32[1536]{0:T(1024)}, u32[]{:S(2)}) copy-start(f32[1536]{0:T(1024)} %param.20) | copy-start | bytes 18436
  39.2 64.3 %all-to-all-start = ((bf16[8,4,57344]{2,1,0:T(4,128)(2,1)}), bf16[8,4,57344]{2,1,0:T(4,128)(2,1)}, u32[]{:S(2)}, u32[]{:S(2)}) async-start(bf16[8,4,57344]{2,1,0:T(4,128)(2,1)} %broadcast_in_dim.154), calls=%async_computation | async-start | bytes 7340032 | tf_op jit(solution)/shard_map/all_to_all | solution.py:123
  48.3 52.6 %copy-start.10 = (s32[64,8]{1,0:T(8,128)}, s32[64,8]{1,0:T(8,128)S(1)}, u32[]{:S(2)}) copy-start(s32[64,8]{1,0:T(8,128)S(1)} %copy.124) | copy-start | bytes 6148
  49.6 52.7 %copy-start.8 = (s32[40,4,128]{2,0,1:T(8,128)}, s32[40,4,128]{2,0,1:T(8,128)S(1)}, u32[]{:S(2)}) copy-start(s32[40,4,128]{2,0,1:T(8,128)S(1)} %reduce-window.11) | copy-start | bytes 245764
  50.7 51.6 %copy-start.18 = (s32[40,5]{0,1:T(8,128)}, s32[40,5]{0,1:T(8,128)S(1)}, u32[]{:S(2)}) copy-start(s32[40,5]{0,1:T(8,128)S(1)} %reduce-window.14) | copy-start | bytes 2404
  50.7 50.2 %copy-start.25 = (bf16[1536,384]{1,0:T(8,128)(2,1)S(1)}, bf16[1536,384]{1,0:T(8,128)(2,1)}, u32[]{:S(2)}) copy-start(bf16[1536,384]{1,0:T(8,128)(2,1)} %param.21) | copy-start | bytes 3538948
  51.3 66.6 %copy-start.23 = (f32[256]{0:T(256)}, f32[256]{0:T(256)S(1)}, u32[]{:S(2)}) copy-start(f32[256]{0:T(256)S(1)} %add_rsqrt_fusion) | copy-start | bytes 3076
  51.5 50.8 %copy-start.13 = (f32[256,32]{0,1:T(8,128)}, f32[256,32]{0,1:T(8,128)S(1)}, u32[]{:S(2)}) copy-start(f32[256,32]{0,1:T(8,128)S(1)} %get-tuple-element.10) | copy-start | bytes 98308
  51.5 50.8 %copy-start.15 = (f32[256,32]{0,1:T(8,128)}, f32[256,32]{0,1:T(8,128)S(1)}, u32[]{:S(2)}) copy-start(f32[256,32]{0,1:T(8,128)S(1)} %get-tuple-element.11) | copy-start | bytes 98308
  107.4 1.5 copy-start.3
  117.9 3.4 copy-start.12
  117.9 3.8 copy-start.14
  117.9 3.8 copy-start.16
  117.9 3.9 copy-start.2
  121.8 7.8 %slice-start = ((bf16[4,57344]{1,0:T(4,128)(2,1)}), bf16[4,2048]{1,0:T(4,128)(2,1)S(1)}, s32[]{:S(2)}) async-start(bf16[4,57344]{1,0:T(4,128)(2,1)} %copy-done.3), calls=%async_computation.4 | async-start | bytes 32768 | tf_op jit(solution)/shard_map/slice | solution.py:135
  121.8 8.0 %copy-start.6 = (bf16[256,1536]{1,0:T(8,128)(2,1)S(1)}, bf16[256,1536]{1,0:T(8,128)(2,1)}, u32[]{:S(2)}) copy-start(bf16[256,1536]{1,0:T(8,128)(2,1)} %param.19) | copy-start | bytes 2359300
  121.8 8.0 %copy-start.24 = (f32[256]{0:T(256)S(1)}, f32[256]{0:T(256)}, u32[]{:S(2)}) copy-start(f32[256]{0:T(256)} %copy-done.23) | copy-start | bytes 3076
  121.8 8.0 %copy-start.28 = (f32[1536]{0:T(1024)S(1)}, f32[1536]{0:T(1024)}, u32[]{:S(2)}) copy-start(f32[1536]{0:T(1024)} %param.20) | copy-start | bytes 18436
  144.8 8.2 %copy-start.1 = (f32[2,2048,256,3]{2,1,3,0:T(8,128)S(1)}, f32[2,2048,256,3]{2,1,3,0:T(8,128)}, u32[]{:S(2)}) copy-start(f32[2,2048,256,3]{2,1,3,0:T(8,128)} %get-tuple-element.17) | copy-start | bytes 37748740
  153.0 3.6 copy-start.7
  156.6 5.9 %copy-start.9 = (s32[40,4,128]{2,0,1:T(8,128)S(1)}, s32[40,4,128]{2,0,1:T(8,128)}, u32[]{:S(2)}) copy-start(s32[40,4,128]{2,0,1:T(8,128)} %copy-done.8) | copy-start | bytes 245764
  156.6 5.9 %slice-start.1 = ((s32[40,5]{0,1:T(8,128)}), s32[40,4]{0,1:T(4,128)S(1)}, s32[]{:S(2)}) async-start(s32[40,5]{0,1:T(8,128)} %copy-done.18), calls=%async_computation.5 | async-start | bytes 4096 | tf_op jit(solution)/shard_map/slice.1
  156.7 5.9 %copy-start.20 = (s32[512]{0:T(512)S(1)}, s32[512]{0:T(512)}, u32[]{:S(2)}) copy-start(s32[512]{0:T(512)} %eq.112) | copy-start | bytes 6148
  158.1 16.5 %copy-start.19 = (f32[1536]{0:T(1024)S(1)}, f32[1536]{0:T(1024)}, u32[]{:S(2)}) copy-start(f32[1536]{0:T(1024)} %param.32) | copy-start | bytes 18436
  158.1 15.2 %all-to-all-start.1 = ((bf16[4,64,1536]{2,1,0:T(8,128)(2,1)}), bf16[4,64,1536]{2,1,0:T(8,128)(2,1)S(1)}, u32[]{:S(2)}, u32[]{:S(2)}) async-start(bf16[4,64,1536]{2,1,0:T(8,128)(2,1)} %bitcast.30), calls=%async_computation.1 | async-start | bytes 1572864 | tf_op jit(solution)/shard_map/all_to_all | solution.py:198
  173.4 8.5 %copy-start.4 = (bf16[64,1536]{1,0:T(8,128)(2,1)}, bf16[64,1536]{1,0:T(8,128)(2,1)S(1)}, u32[]{:S(2)}) copy-start(bf16[64,1536]{1,0:T(8,128)(2,1)S(1)} %reduce_sum.127) | copy-start | bytes 589828
  309.8 6.2 %copy-start.11 = (s32[64,8]{1,0:T(8,128)S(1)}, s32[64,8]{1,0:T(8,128)}, u32[]{:S(2)}) copy-start(s32[64,8]{1,0:T(8,128)} %copy-done.10) | copy-start | bytes 6148
  309.8 6.4 %copy-start.21 = (f32[64,8]{0,1:T(8,128)S(1)}, f32[64,8]{0,1:T(8,128)}, u32[]{:S(2)}) copy-start(f32[64,8]{0,1:T(8,128)} %param.34) | copy-start | bytes 6148
  309.8 98.0 %all-to-all-start.3 = ((bf16[16,160,1536]{2,0,1:T(8,128)(2,1)}), bf16[16,160,1536]{2,0,1:T(8,128)(2,1)}, u32[]{:S(2)}, u32[]{:S(2)}) async-start(bf16[16,160,1536]{2,0,1:T(8,128)(2,1)} %bitcast.150), calls=%async_computation.3 | async-start | bytes 15728640 | tf_op jit(solution)/shard_map/all_to_all | solution.py:233

commit v5 on v4

--- a/solution.py
+++ b/solution.py
@@ -119,16 +119,14 @@
     mine = (home_dev % exp_count) == exp_index
     rows_pick = jnp.take(along_req, home_pick, axis=0)
     rows_pick = jnp.where(mine[:, None], rows_pick, jnp.zeros_like(rows_pick))
-    rows_pick = jnp.sum(
-        lax.all_to_all(
-            jnp.broadcast_to(rows_pick[None], (exp_count,) + rows_pick.shape),
-            "exp",
-            split_axis=0,
-            concat_axis=0,
-            tiled=True,
-        ).astype(jnp.float32),
-        axis=0,
-    ).astype(jnp.bfloat16)
+    rows_all = lax.all_to_all(
+        jnp.broadcast_to(rows_pick[None], (exp_count,) + rows_pick.shape),
+        "exp",
+        split_axis=0,
+        concat_axis=0,
+        tiled=True,
+    )
+    rows_pick = rows_all[home_dev % exp_count, jnp.arange(requests, dtype=jnp.int32)]
     chosen = []
     start = 0
     for shape_in, size_in in zip(part_shapes, part_sizes):
@@ -234,9 +232,15 @@
     returned = returned.reshape(capacity, exp_count, hid_count, local_exp, width)
     results = jnp.sum(returned.astype(jnp.float32), axis=2).astype(jnp.bfloat16)
     results = results.reshape(capacity * expert_count, width)
-    picked = jnp.take(results, slots, axis=0).reshape(tok_rows, top_count, width)
-    expert_out = jnp.sum(
-        router_expert_weight[:, :, None] * picked.astype(jnp.float32), axis=1
+    slot_hit = slots.reshape(tok_rows, top_count)[:, :, None] == slot_table[None, None, :]
+    combine = jnp.sum(
+        jnp.where(slot_hit, router_expert_weight[:, :, None], 0.0), axis=1
+    )
+    expert_out = jnp.dot(
+        combine,
+        results.astype(jnp.float32),
+        precision=lax.Precision.HIGHEST,
+        preferred_element_type=jnp.float32,
     ).astype(jnp.bfloat16)
     return (attn_out, expert_out)
 

time: 435 us -> 429 us (0.986)
  other arithmetic: 27.1 us -> 21 us
    reduce_sum x2 -> x1, other arithmetic: 6.6 us -> 0.47 us  [per_device(): jnp.sum(jnp.where(slot_hit, router_expert_weight[:, :, None], 0.0), axis=1)]
where the time goes in v5:
time: 429 us; the launch traced here: 426 us
  blocking collectives  188 us (44%)
  waiting for transfers between devices  99.8 us (23%)
  local copies, waits for them, and re-layouts  51.6 us (12%)
  matrix products  44.9 us (10%)
  other arithmetic  21 us (5%)
  starting transfers between devices  19.6 us (5%)
    all_to_all x1, blocking collectives, per_device(): lax.all_to_all(copies, ('exp', 'hid'), split_axis=1, concat_axis=0, tiled...  94.7 us
    all_to_all x1, waiting for transfers between devices, per_device(): lax.all_to_all(partials, ('exp', 'hid'), split_axis=1, concat_axis=1, til...  91.3 us
    all_gather x1, blocking collectives, per_device(): key_piece = lax.all_gather(keys_own, 'exp', axis=0, tiled=True)  51 us
    all_gather x1, blocking collectives, per_device(): along_req = lax.all_gather(bank, 'req', axis=0, tiled=True)  28.5 us
    all_gather x1, blocking collectives, per_device(): value_piece = lax.all_gather(values_own, 'exp', axis=0, tiled=True)  13.3 us
    dot_general x1, matrix products, expert_rows(): jnp.einsum('ref,efd->red', hidden, expert_down_weight, preferred_element_...  12.2 us
    all_to_all x1, starting transfers between devices, per_device(): lax.all_to_all(jnp.broadcast_to(rows_pick[None], (exp_count,) + rows_pick...  9.02 us
  transfers between devices with their start and end apart: 3, of which 2 were waited for; matrix products, arithmetic and copies ran while one was open for 2% of the time, Pallas kernels for 0%

profile of v5, /device:TPU:3, one launch (start us, length us, event | category | flops | bytes accessed | tf_op | source)
XLA Modules:
  0.0 425.5 jit_solution(4130110662894356563)
XLA Ops:
  0.7 0.9 dynamic-slice_bitcast_fusion
  1.5 0.7 dynamic-slice_bitcast_fusion.1
  2.2 1.0 copy.77
  3.3 0.3 reshape.393
  3.5 1.0 copy.78
  4.6 0.3 reshape.395
  4.8 0.2 maximum_bitcast_fusion
  5.1 28.5 %all-gather = bf16[8,1,57344]{2,1,0:T(2,128)(2,1)S(1)} all-gather(bf16[1,1,57344]{2,1,0:T(2,128)(2,1)S(1)} %maximum_bitcast_fusion), channel_id=1, replica_groups=mesh['req'=8,'exp'=8,'hid'=4] {'req'}, dimensions={0}, use_global_device_ids=true | all-gather | bytes 1032192 | tf_op jit(solution)/shard_map/all_gather | solution.py:116
  33.6 1.0 copy.103
  34.7 0.2 dynamic-slice_reduce_fusion
  34.9 0.2 select_reduce_fusion.2
  35.1 1.0 gather_fusion
  36.1 0.3 select_select_fusion
  36.4 2.8 broadcast_in_dim.159
  39.2 9.0 %all-to-all-start = ((bf16[8,4,57344]{2,1,0:T(4,128)(2,1)}), bf16[8,4,57344]{2,1,0:T(4,128)(2,1)}, u32[]{:S(2)}, u32[]{:S(2)}) async-start(bf16[8,4,57344]{2,1,0:T(4,128)(2,1)} %broadcast_in_dim.159), calls=%async_computation | async-start | bytes 7340032 | tf_op jit(solution)/shard_map/all_to_all | solution.py:122
  48.9 0.2 fusion.7
  49.2 0.2 multiply_cosine_fusion
  49.4 0.5 fusion.62
  49.9 51.0 %all_gather.9 = bf16[2048,128]{0,1:T(8,128)(2,1)} all-gather(bf16[256,128]{0,1:T(8,128)(2,1)S(1)} %bitcast.165), channel_id=1, replica_groups=mesh['req'=8,'exp'=8,'hid'=4] {'exp'}, dimensions={0}, use_global_device_ids=true | all-gather | bytes 589824 | tf_op jit(solution)/shard_map/all_gather | solution.py:168
  100.9 1.4 fusion.60
  102.3 1.2 fusion.6
  103.5 2.9 gather_fusion.1
  106.5 0.9 fusion.64
  107.4 0.6 slice.49
  108.0 2.1 reshape.397
  110.1 1.3 copy.79
  111.4 2.2 fusion.58
  113.6 2.1 reshape.399
  115.7 1.3 copy.81
  117.0 1.7 fusion.55
  118.6 0.8 reshape_reshape.7
  119.5 0.9 select_convert_fusion.1
  120.4 0.2 convolution_add_fusion
  120.9 7.7 %fusion = (f32[2,3,256]{2,1,0:T(4,128)S(1)}, f32[2,2048,256,3]{2,1,3,0:T(8,128)}) fusion(pred[256,2048]{0,1:T(8,128)(4,1)S(1)} %copy-done.2, bf16[2048,2,64,1]{0,2,3,1:T(8,128)(2,1)} %bitcast.163, bf16[256,2,3,32]{0,3,2,1:T(8,128)(2,1)S(1)} %bitcast.174, bf16[256,2,3,32]{0,3,2,1:T(8,128)(2,1)S(1)} %bitcast.173), kind=kOutput, calls=%fused_computation.4 | convolution fusion | flops 412482048 | bytes 13834240 | tf_op jit(solution)/shard_map/qkgh,nkh->kgqn/dot_general | solution.py:177
  128.7 0.2 fusion.65
  128.9 1.4 fusion.21
  130.3 13.3 %all_gather.11 = bf16[2048,128]{1,0:T(8,128)(2,1)S(1)} all-gather(bf16[256,128]{1,0:T(8,128)(2,1)S(1)} %fusion.21), channel_id=1, replica_groups=mesh['req'=8,'exp'=8,'hid'=4] {'exp'}, dimensions={0}, use_global_device_ids=true | all-gather | bytes 589824 | tf_op jit(solution)/shard_map/all_gather | solution.py:169
  143.6 0.2 copy.82
  143.9 6.9 %fusion.1 = f32[2,3,256]{2,1,0:T(4,128)S(1)} fusion(f32[2,2048,256,3]{2,1,3,0:T(8,128)} %get-tuple-element.17, f32[2,3,256]{2,1,0:T(4,128)S(1)} %broadcast_maximum_fusion, pred[256,2048]{0,1:T(8,128)(4,1)S(1)} %copy-done.2), kind=kLoop, calls=%fused_computation.5 | loop fusion | flops 15727104 | bytes 13119488 | tf_op jit(solution)/shard_map/reduce_sum | solution.py:183
  150.7 1.4 copy-done.1
  152.1 3.6 fusion.25
  155.7 1.5 convolution_convert_fusion.2
  157.2 4.4 %all-to-all-start.1 = ((bf16[4,64,1536]{2,1,0:T(8,128)(2,1)}), bf16[4,64,1536]{2,1,0:T(8,128)(2,1)S(1)}, u32[]{:S(2)}, u32[]{:S(2)}) async-start(bf16[4,64,1536]{2,1,0:T(8,128)(2,1)} %bitcast.31), calls=%async_computation.1 | async-start | bytes 1572864 | tf_op jit(solution)/shard_map/all_to_all | solution.py:196
  161.7 1.2 reduce-window.11
  162.9 0.2 slice_reduce_fusion
  163.4 0.5 fusion.17
  163.8 8.5 %all-to-all-done.1 = bf16[4,64,1536]{2,1,0:T(8,128)(2,1)S(1)} async-done(((bf16[4,64,1536]{2,1,0:T(8,128)(2,1)}), bf16[4,64,1536]{2,1,0:T(8,128)(2,1)S(1)}, u32[]{:S(2)}, u32[]{:S(2)}) %all-to-all-start.1) | async-done | bytes 786464 | tf_op jit(solution)/shard_map/all_to_all | solution.py:196
  172.5 1.2 multiply_reduce_fusion
  173.7 3.0 convolution_convert_fusion.1
  176.6 4.3 broadcast_in_dim.166
  180.9 3.2 copy.89
  184.1 1.0 broadcast_in_dim.167
  185.1 94.7 %all_to_all.33 = bf16[16,160,1536]{2,0,1:T(8,128)(2,1)S(1)} all-to-all(bf16[16,160,1536]{2,0,1:T(8,128)(2,1)S(1)} %bitcast.156), channel_id=1, replica_groups=mesh['req'=8,'exp'=8,'hid'=4] {'exp','hid'}, dimensions={1} | all-to-all | bytes 15728640 | tf_op jit(solution)/shard_map/all_to_all | solution.py:223
  279.8 3.9 copy.90
  283.6 6.0 %convolution_bitcast_fusion.1 = f32[512,5,128]{2,0,1:T(8,128)S(1)} fusion(bf16[512,5,1536]{2,0,1:T(8,128)(2,1)} %bitcast.159, bf16[5,1536,128]{2,1,0:T(8,128)(2,1)} %param.35), kind=kOutput, calls=%fused_computation.22 | convolution fusion | flops 1006632960 | bytes 11141120 | tf_op jit(solution)/shard_map/red,edf->ref/dot_general | solution.py:54
  289.6 12.2 %convolution_convert_fusion = bf16[5,512,1536]{2,1,0:T(8,128)(2,1)} fusion(bf16[5,128,1536]{2,1,0:T(8,128)(2,1)S(1)} %copy-done, bf16[512,5,1536]{2,0,1:T(8,128)(2,1)} %bitcast.160, bf16[5,1536,128]{2,1,0:T(8,128)(2,1)} %param.36, f32[512,5,128]{2,0,1:T(8,128)S(1)} %convolution_bitcast_fusion.1), kind=kOutput, calls=%fused_computation.9 | convolution fusion | flops 2019164160 | bytes 20971520 | tf_op jit(solution)/shard_map/ref,efd->red/dot_general | solution.py:61
  301.8 7.0 %copy.91 = bf16[32,16,5,1536]{3,1,2,0:T(8,128)(2,1)} copy(bf16[32,16,5,1536]{3,1,0,2:T(8,128)(2,1)} %bitcast.161) | data formatting | bytes 15728640 | tf_op jit(solution)/shard_map/reshape | solution.py:229
  308.8 6.2 %all-to-all-start.3 = ((bf16[16,160,1536]{2,0,1:T(8,128)(2,1)}), bf16[16,160,1536]{2,0,1:T(8,128)(2,1)}, u32[]{:S(2)}, u32[]{:S(2)}) async-start(bf16[16,160,1536]{2,0,1:T(8,128)(2,1)} %bitcast.155), calls=%async_computation.3 | async-start | bytes 15728640 | tf_op jit(solution)/shard_map/all_to_all | solution.py:231
  315.1 0.5 select_reduce_fusion
  315.6 91.3 %all-to-all-done.3 = bf16[16,160,1536]{2,0,1:T(8,128)(2,1)} async-done(((bf16[16,160,1536]{2,0,1:T(8,128)(2,1)}), bf16[16,160,1536]{2,0,1:T(8,128)(2,1)}, u32[]{:S(2)}, u32[]{:S(2)}) %all-to-all-start.3) | async-done | bytes 7864352 | tf_op jit(solution)/shard_map/all_to_all | solution.py:231
  406.9 6.7 %reduce_sum.118 = bf16[16,8,5,1536]{3,0,2,1:T(8,128)(2,1)} reduce(bf16[16,8,4,5,1536]{4,0,3,2,1:T(8,128)(2,1)} %bitcast.43, bf16[]{:T(256)} %constant.138.clone.1), dimensions={2}, to_apply=%region_15.16 | reduce | flops 2949120 | bytes 9830402 | tf_op jit(solution)/shard_map/reduce_sum | solution.py:233
  413.5 4.3 %copy.92 = bf16[16,8,5,1536]{3,2,1,0:T(8,128)(2,1)} copy(bf16[16,8,5,1536]{3,0,2,1:T(8,128)(2,1)} %reduce_sum.118) | data formatting | bytes 3932160 | tf_op jit(solution)/shard_map/reduce_sum | solution.py:233
  417.9 4.3 %reshape.408 = bf16[640,1536]{1,0:T(8,128)(2,1)} reshape(bf16[16,8,5,1536]{3,2,1,0:T(8,128)(2,1)} %copy.92) | data formatting | bytes 3932160 | tf_op jit(solution)/shard_map/reshape | solution.py:234
  422.2 3.3 convolution_convert_fusion.3
  (86 shorter events, 1.7 us)
Async XLA Ops:
  0.6 289.0 %copy-start = (bf16[5,128,1536]{2,1,0:T(8,128)(2,1)S(1)}, bf16[5,128,1536]{2,1,0:T(8,128)(2,1)}, u32[]{:S(2)}) copy-start(bf16[5,128,1536]{2,1,0:T(8,128)(2,1)} %param.37) | copy-start | bytes 5898244
  5.1 29.6 %copy-start.18 = (s32[8,4]{0,1:T(4,128)S(1)}, s32[8,4]{0,1:T(4,128)}, u32[]{:S(2)}) copy-start(s32[8,4]{0,1:T(4,128)} %param.30) | copy-start | bytes 388
  5.1 29.8 %copy-start.23 = (s32[64]{0:T(128)S(1)}, s32[64]{0:T(128)}, u32[]{:S(2)}) copy-start(s32[64]{0:T(128)} %param.31) | copy-start | bytes 772
  39.2 9.1 %copy-start.24 = (s32[1,4]{1,0:T(1,128)S(1)}, s32[1,4]{1,0:T(1,128)}, u32[]{:S(2)}) copy-start(s32[1,4]{1,0:T(1,128)} %param.29) | copy-start | bytes 52
  39.2 9.2 %copy-start.16 = (s32[64,8]{0,1:T(8,128)S(1)}, s32[64,8]{0,1:T(8,128)}, u32[]{:S(2)}) copy-start(s32[64,8]{0,1:T(8,128)} %param.33) | copy-start | bytes 6148
  39.2 9.7 %copy-start.5 = (bf16[256,1536]{1,0:T(8,128)(2,1)S(1)}, bf16[256,1536]{1,0:T(8,128)(2,1)}, u32[]{:S(2)}) copy-start(bf16[256,1536]{1,0:T(8,128)(2,1)} %param.19) | copy-start | bytes 2359300
  39.2 10.2 %copy-start.20 = (bf16[1536,128]{1,0:T(8,128)(2,1)S(1)}, bf16[1536,128]{1,0:T(8,128)(2,1)}, u32[]{:S(2)}) copy-start(bf16[1536,128]{1,0:T(8,128)(2,1)} %param.22) | copy-start | bytes 1179652
  39.2 10.2 %copy-start.21 = (f32[1536]{0:T(1024)S(1)}, f32[1536]{0:T(1024)}, u32[]{:S(2)}) copy-start(f32[1536]{0:T(1024)} %param.20) | copy-start | bytes 18436
  39.2 64.3 %all-to-all-start = ((bf16[8,4,57344]{2,1,0:T(4,128)(2,1)}), bf16[8,4,57344]{2,1,0:T(4,128)(2,1)}, u32[]{:S(2)}, u32[]{:S(2)}) async-start(bf16[8,4,57344]{2,1,0:T(4,128)(2,1)} %broadcast_in_dim.159), calls=%async_computation | async-start | bytes 7340032 | tf_op jit(solution)/shard_map/all_to_all | solution.py:122
  48.5 53.8 %copy-start.8 = (s32[64,8]{1,0:T(8,128)}, s32[64,8]{1,0:T(8,128)S(1)}, u32[]{:S(2)}) copy-start(s32[64,8]{1,0:T(8,128)S(1)} %copy.84) | copy-start | bytes 6148
  48.6 52.3 %copy-start.19 = (bf16[1536,384]{1,0:T(8,128)(2,1)S(1)}, bf16[1536,384]{1,0:T(8,128)(2,1)}, u32[]{:S(2)}) copy-start(bf16[1536,384]{1,0:T(8,128)(2,1)} %param.21) | copy-start | bytes 3538948
  49.4 52.9 %copy-start.11 = (f32[256,32]{0,1:T(8,128)}, f32[256,32]{0,1:T(8,128)S(1)}, u32[]{:S(2)}) copy-start(f32[256,32]{0,1:T(8,128)S(1)} %get-tuple-element.8) | copy-start | bytes 98308
  49.4 52.9 %copy-start.13 = (f32[256,32]{0,1:T(8,128)}, f32[256,32]{0,1:T(8,128)S(1)}, u32[]{:S(2)}) copy-start(f32[256,32]{0,1:T(8,128)S(1)} %get-tuple-element.9) | copy-start | bytes 98308
  106.5 1.5 copy-start.3
  116.9 3.4 copy-start.10
  116.9 3.8 copy-start.12
  116.9 3.8 copy-start.14
  117.0 3.9 copy-start.2
  120.9 7.8 %slice-start = ((bf16[4,57344]{1,0:T(4,128)(2,1)}), bf16[4,2048]{1,0:T(4,128)(2,1)S(1)}, s32[]{:S(2)}) async-start(bf16[4,57344]{1,0:T(4,128)(2,1)} %copy-done.3), calls=%async_computation.4 | async-start | bytes 32768 | tf_op jit(solution)/shard_map/slice | solution.py:133
  120.9 8.0 %copy-start.6 = (bf16[256,1536]{1,0:T(8,128)(2,1)S(1)}, bf16[256,1536]{1,0:T(8,128)(2,1)}, u32[]{:S(2)}) copy-start(bf16[256,1536]{1,0:T(8,128)(2,1)} %param.19) | copy-start | bytes 2359300
  120.9 8.0 %copy-start.22 = (f32[1536]{0:T(1024)S(1)}, f32[1536]{0:T(1024)}, u32[]{:S(2)}) copy-start(f32[1536]{0:T(1024)} %param.20) | copy-start | bytes 18436
  143.8 8.2 %copy-start.1 = (f32[2,2048,256,3]{2,1,3,0:T(8,128)S(1)}, f32[2,2048,256,3]{2,1,3,0:T(8,128)}, u32[]{:S(2)}) copy-start(f32[2,2048,256,3]{2,1,3,0:T(8,128)} %get-tuple-element.17) | copy-start | bytes 37748740
  152.1 3.6 copy-start.7
  155.7 5.9 %copy-start.9 = (s32[64,8]{1,0:T(8,128)S(1)}, s32[64,8]{1,0:T(8,128)}, u32[]{:S(2)}) copy-start(s32[64,8]{1,0:T(8,128)} %copy-done.8) | copy-start | bytes 6148
  157.2 16.5 %copy-start.15 = (f32[1536]{0:T(1024)S(1)}, f32[1536]{0:T(1024)}, u32[]{:S(2)}) copy-start(f32[1536]{0:T(1024)} %param.32) | copy-start | bytes 18436
  157.2 15.2 %all-to-all-start.1 = ((bf16[4,64,1536]{2,1,0:T(8,128)(2,1)}), bf16[4,64,1536]{2,1,0:T(8,128)(2,1)S(1)}, u32[]{:S(2)}, u32[]{:S(2)}) async-start(bf16[4,64,1536]{2,1,0:T(8,128)(2,1)} %bitcast.31), calls=%async_computation.1 | async-start | bytes 1572864 | tf_op jit(solution)/shard_map/all_to_all | solution.py:196
  172.4 8.4 %copy-start.4 = (bf16[64,1536]{1,0:T(8,128)(2,1)}, bf16[64,1536]{1,0:T(8,128)(2,1)S(1)}, u32[]{:S(2)}) copy-start(bf16[64,1536]{1,0:T(8,128)(2,1)S(1)} %reduce_sum.114) | copy-start | bytes 589828
  308.8 6.2 %copy-start.17 = (f32[64,8]{0,1:T(8,128)S(1)}, f32[64,8]{0,1:T(8,128)}, u32[]{:S(2)}) copy-start(f32[64,8]{0,1:T(8,128)} %param.34) | copy-start | bytes 6148
  308.8 98.0 %all-to-all-start.3 = ((bf16[16,160,1536]{2,0,1:T(8,128)(2,1)}), bf16[16,160,1536]{2,0,1:T(8,128)(2,1)}, u32[]{:S(2)}, u32[]{:S(2)}) async-start(bf16[16,160,1536]{2,0,1:T(8,128)(2,1)} %bitcast.155), calls=%async_computation.3 | async-start | bytes 15728640 | tf_op jit(solution)/shard_map/all_to_all | solution.py:231

commit v6 on v5

--- a/solution.py
+++ b/solution.py
@@ -215,33 +215,38 @@
     ).astype(jnp.bfloat16)
     outgoing = jnp.dot(placed, normed_moe, preferred_element_type=jnp.float32).astype(jnp.bfloat16)
     outgoing = outgoing.reshape(capacity, expert_count, width)
-    copies = jnp.broadcast_to(
-        outgoing.reshape(capacity, exp_count, 1, local_exp, width),
-        (capacity, exp_count, hid_count, local_exp, width),
-    )
-    copies = copies.reshape(capacity, exp_count * hid_count * local_exp, width)
-    arrived = lax.all_to_all(copies, ("exp", "hid"), split_axis=1, concat_axis=0, tiled=True)
-    partials = expert_rows(
-        arrived, expert_gate_weight, expert_up_weight, expert_down_weight
-    ).astype(jnp.bfloat16)
     partners = exp_count * hid_count
-    partials = jnp.transpose(
-        partials.reshape(partners, capacity, local_exp, width), (1, 0, 2, 3)
-    ).reshape(capacity, partners * local_exp, width)
-    returned = lax.all_to_all(partials, ("exp", "hid"), split_axis=1, concat_axis=1, tiled=True)
-    returned = returned.reshape(capacity, exp_count, hid_count, local_exp, width)
-    results = jnp.sum(returned.astype(jnp.float32), axis=2).astype(jnp.bfloat16)
-    results = results.reshape(capacity * expert_count, width)
+    halves = 2 if capacity % 2 == 0 else 1
+    cap_part = capacity // halves
     slot_hit = slots.reshape(tok_rows, top_count)[:, :, None] == slot_table[None, None, :]
-    combine = jnp.sum(
-        jnp.where(slot_hit, router_expert_weight[:, :, None], 0.0), axis=1
-    )
-    expert_out = jnp.dot(
-        combine,
-        results.astype(jnp.float32),
-        precision=lax.Precision.HIGHEST,
-        preferred_element_type=jnp.float32,
-    ).astype(jnp.bfloat16)
+    combine = jnp.sum(jnp.where(slot_hit, router_expert_weight[:, :, None], 0.0), axis=1)
+    expert_acc = jnp.zeros((tok_rows, width), jnp.float32)
+    for half in range(halves):
+        part_out = outgoing[half * cap_part:(half + 1) * cap_part]
+        copies = jnp.broadcast_to(
+            part_out.reshape(cap_part, exp_count, 1, local_exp, width),
+            (cap_part, exp_count, hid_count, local_exp, width),
+        )
+        copies = copies.reshape(cap_part, partners * local_exp, width)
+        arrived = lax.all_to_all(copies, ("exp", "hid"), split_axis=1, concat_axis=0, tiled=True)
+        partials = expert_rows(
+            arrived, expert_gate_weight, expert_up_weight, expert_down_weight
+        ).astype(jnp.bfloat16)
+        partials = jnp.transpose(
+            partials.reshape(partners, cap_part, local_exp, width), (1, 0, 2, 3)
+        ).reshape(cap_part, partners * local_exp, width)
+        returned = lax.all_to_all(partials, ("exp", "hid"), split_axis=1, concat_axis=1, tiled=True)
+        returned = returned.reshape(cap_part, exp_count, hid_count, local_exp, width)
+        results = jnp.sum(returned.astype(jnp.float32), axis=2).astype(jnp.bfloat16)
+        results = results.reshape(cap_part * expert_count, width)
+        part_cols = combine[:, half * cap_part * expert_count:(half + 1) * cap_part * expert_count]
+        expert_acc = expert_acc + jnp.dot(
+            part_cols,
+            results.astype(jnp.float32),
+            precision=lax.Precision.HIGHEST,
+            preferred_element_type=jnp.float32,
+        )
+    expert_out = expert_acc.astype(jnp.bfloat16)
     return (attn_out, expert_out)
 
 

time: 429 us -> 416 us (0.970)
  blocking collectives: 188 us -> 92.8 us
  waiting for transfers between devices: 99.8 us -> 159 us
  starting transfers between devices: 19.6 us -> 36.4 us
    all_to_all x1 -> x0, blocking collectives: 94.7 us -> none  [per_device(): lax.all_to_all(copies, ('exp', 'hid'), split_axis=1, concat_axis=0, tiled...]
    all_to_all x0 -> x2, waiting for transfers between devices: none -> 77.6 us  [per_device(): lax.all_to_all(copies, ('exp', 'hid'), split_axis=1, concat_axis=0, tiled...]
    all_to_all x1 -> x2, waiting for transfers between devices: 91.3 us -> 72.6 us  [per_device(): lax.all_to_all(partials, ('exp', 'hid'), split_axis=1, concat_axis=1, til...]
    all_to_all x0 -> x2, starting transfers between devices: none -> 12.2 us  [per_device(): lax.all_to_all(copies, ('exp', 'hid'), split_axis=1, concat_axis=0, tiled...]
    all_to_all x1 -> x2, starting transfers between devices: 6.17 us -> 10.8 us  [per_device(): lax.all_to_all(partials, ('exp', 'hid'), split_axis=1, concat_axis=1, til...]
    broadcast_in_dim x3 -> x6, local copies, waits for them, and re-layouts: 8.41 us -> 10.9 us  [per_device(): jnp.broadcast_to(part_out.reshape(cap_part, exp_count, 1, local_exp, widt...]
    dot_general x1 -> x2, matrix products: 12.2 us -> 13.7 us  [expert_rows(): jnp.einsum('ref,efd->red', hidden, expert_down_weight, preferred_element_...]
    reshape x2 -> x4, local copies, waits for them, and re-layouts: 11.4 us -> 11.1 us  [the longest x2 8.61 us: per_device(): partials.reshape(partners, cap_part, local_exp, width)]
  transfers between devices with their start and end apart: 3 -> 6, of which waited for: 2 -> 5; matrix products, arithmetic and copies ran while one was open for 2% -> 12% of each run, Pallas kernels for 0% -> 0%
where the time goes in v6:
time: 416 us; the launch traced here: 411 us
  waiting for transfers between devices  159 us (38%)
  blocking collectives  92.8 us (22%)
  local copies, waits for them, and re-layouts  50.4 us (12%)
  matrix products  47.9 us (12%)
  starting transfers between devices  36.4 us (9%)
  other arithmetic  22.9 us (6%)
    all_to_all x2, waiting for transfers between devices, per_device(): lax.all_to_all(copies, ('exp', 'hid'), split_axis=1, concat_axis=0, tiled...  77.6 us
    all_to_all x2, waiting for transfers between devices, per_device(): lax.all_to_all(partials, ('exp', 'hid'), split_axis=1, concat_axis=1, til...  72.6 us
    all_gather x1, blocking collectives, per_device(): key_piece = lax.all_gather(keys_own, 'exp', axis=0, tiled=True)  51 us
    all_gather x1, blocking collectives, per_device(): along_req = lax.all_gather(bank, 'req', axis=0, tiled=True)  28.5 us
    dot_general x2, matrix products, expert_rows(): jnp.einsum('ref,efd->red', hidden, expert_down_weight, preferred_element_...  13.7 us
    all_gather x1, blocking collectives, per_device(): value_piece = lax.all_gather(values_own, 'exp', axis=0, tiled=True)  13.3 us
    all_to_all x2, starting transfers between devices, per_device(): lax.all_to_all(copies, ('exp', 'hid'), split_axis=1, concat_axis=0, tiled...  12.2 us
    broadcast_in_dim x6, local copies, waits for them, and re-layouts, per_device(): jnp.broadcast_to(part_out.reshape(cap_part, exp_count, 1, local_exp, widt...  10.9 us
  transfers between devices with their start and end apart: 6, of which 5 were waited for; matrix products, arithmetic and copies ran while one was open for 12% of the time, Pallas kernels for 0%

profile of v6, /device:TPU:3, one launch (start us, length us, event | category | flops | bytes accessed | tf_op | source)
XLA Modules:
  0.0 410.6 jit_solution(3254555754656600177)
XLA Ops:
  0.7 0.9 dynamic-slice_bitcast_fusion
  1.5 0.7 dynamic-slice_bitcast_fusion.1
  2.2 1.0 copy.88
  3.5 1.0 copy.89
  5.1 28.5 %all-gather = bf16[8,1,57344]{2,1,0:T(2,128)(2,1)S(1)} all-gather(bf16[1,1,57344]{2,1,0:T(2,128)(2,1)S(1)} %maximum_bitcast_fusion), channel_id=1, replica_groups=mesh['req'=8,'exp'=8,'hid'=4] {'req'}, dimensions={0}, use_global_device_ids=true | all-gather | bytes 1032192 | tf_op jit(solution)/shard_map/all_gather | solution.py:116
  33.6 1.0 copy.154
  35.1 1.0 gather_fusion
  36.4 2.8 broadcast_in_dim.166
  39.2 9.0 %all-to-all-start = ((bf16[8,4,57344]{2,1,0:T(4,128)(2,1)}), bf16[8,4,57344]{2,1,0:T(4,128)(2,1)}, u32[]{:S(2)}, u32[]{:S(2)}) async-start(bf16[8,4,57344]{2,1,0:T(4,128)(2,1)} %broadcast_in_dim.166), calls=%async_computation | async-start | bytes 7340032 | tf_op jit(solution)/shard_map/all_to_all | solution.py:122
  49.9 51.0 %all_gather.9 = bf16[2048,128]{0,1:T(8,128)(2,1)} all-gather(bf16[256,128]{0,1:T(8,128)(2,1)S(1)} %bitcast.216), channel_id=1, replica_groups=mesh['req'=8,'exp'=8,'hid'=4] {'exp'}, dimensions={0}, use_global_device_ids=true | all-gather | bytes 589824 | tf_op jit(solution)/shard_map/all_gather | solution.py:168
  100.9 1.4 fusion.111
  102.3 1.2 fusion.21
  103.5 2.9 gather_fusion.1
  106.5 0.9 fusion.116
  108.0 2.1 reshape.420
  110.1 1.3 copy.90
  111.4 2.2 fusion.109
  113.6 2.1 reshape.422
  115.7 1.3 copy.92
  117.0 1.7 fusion.106
  118.7 0.8 reshape_reshape.6
  119.5 0.9 select_convert_fusion.1
  120.9 7.7 %fusion = (f32[2,3,256]{2,1,0:T(4,128)S(1)}, f32[2,2048,256,3]{2,1,3,0:T(8,128)}) fusion(pred[256,2048]{0,1:T(8,128)(4,1)S(1)} %copy-done.3, bf16[2048,2,64,1]{0,2,3,1:T(8,128)(2,1)} %bitcast.214, bf16[256,2,3,32]{0,3,2,1:T(8,128)(2,1)S(1)} %bitcast.225, bf16[256,2,3,32]{0,3,2,1:T(8,128)(2,1)S(1)} %bitcast.224), kind=kOutput, calls=%fused_computation.4 | convolution fusion | flops 412482048 | bytes 13834240 | tf_op jit(solution)/shard_map/qkgh,nkh->kgqn/dot_general | solution.py:177
  128.9 1.4 fusion.53
  130.3 13.3 %all_gather.11 = bf16[2048,128]{1,0:T(8,128)(2,1)S(1)} all-gather(bf16[256,128]{1,0:T(8,128)(2,1)S(1)} %fusion.53), channel_id=1, replica_groups=mesh['req'=8,'exp'=8,'hid'=4] {'exp'}, dimensions={0}, use_global_device_ids=true | all-gather | bytes 589824 | tf_op jit(solution)/shard_map/all_gather | solution.py:169
  143.8 6.9 %fusion.1 = f32[2,3,256]{2,1,0:T(4,128)S(1)} fusion(f32[2,2048,256,3]{2,1,3,0:T(8,128)} %get-tuple-element.19, f32[2,3,256]{2,1,0:T(4,128)S(1)} %broadcast_maximum_fusion, pred[256,2048]{0,1:T(8,128)(4,1)S(1)} %copy-done.3), kind=kLoop, calls=%fused_computation.5 | loop fusion | flops 15727104 | bytes 13119488 | tf_op jit(solution)/shard_map/reduce_sum | solution.py:183
  150.7 1.4 copy-done.1
  152.1 3.6 fusion.57
  155.7 1.5 convolution_convert_fusion.3
  157.2 4.4 %all-to-all-start.1 = ((bf16[4,64,1536]{2,1,0:T(8,128)(2,1)}), bf16[4,64,1536]{2,1,0:T(8,128)(2,1)S(1)}, u32[]{:S(2)}, u32[]{:S(2)}) async-start(bf16[4,64,1536]{2,1,0:T(8,128)(2,1)} %bitcast.31), calls=%async_computation.1 | async-start | bytes 1572864 | tf_op jit(solution)/shard_map/all_to_all | solution.py:196
  161.7 1.2 reduce-window.11
  163.9 8.4 %all-to-all-done.1 = bf16[4,64,1536]{2,1,0:T(8,128)(2,1)S(1)} async-done(((bf16[4,64,1536]{2,1,0:T(8,128)(2,1)}), bf16[4,64,1536]{2,1,0:T(8,128)(2,1)S(1)}, u32[]{:S(2)}, u32[]{:S(2)}) %all-to-all-start.1) | async-done | bytes 786464 | tf_op jit(solution)/shard_map/all_to_all | solution.py:196
  172.4 1.2 multiply_reduce_fusion
  173.6 1.7 convolution_convert_fusion.2
  175.3 1.5 fusion.115
  176.8 1.4 broadcast_in_dim.175
  178.3 0.6 copy.104
  178.9 2.2 broadcast_in_dim.176
  181.1 6.8 %all-to-all-start.4 = ((bf16[8,160,1536]{2,0,1:T(8,128)(2,1)}), bf16[8,160,1536]{2,0,1:T(8,128)(2,1)}, u32[]{:S(2)}, u32[]{:S(2)}) async-start(bf16[8,160,1536]{2,0,1:T(8,128)(2,1)} %bitcast.212), calls=%async_computation.4 | async-start | bytes 7864320 | tf_op jit(solution)/shard_map/all_to_all | solution.py:231
  187.9 1.4 broadcast_in_dim.173
  189.4 1.7 copy.100
  191.1 44.9 %all-to-all-done.4 = bf16[8,160,1536]{2,0,1:T(8,128)(2,1)} async-done(((bf16[8,160,1536]{2,0,1:T(8,128)(2,1)}), bf16[8,160,1536]{2,0,1:T(8,128)(2,1)}, u32[]{:S(2)}, u32[]{:S(2)}) %all-to-all-start.4) | async-done | bytes 3932192 | tf_op jit(solution)/shard_map/all_to_all | solution.py:231
  236.0 3.5 broadcast_in_dim.174
  239.5 5.4 %all-to-all-start.2 = ((bf16[8,160,1536]{2,0,1:T(8,128)(2,1)}), bf16[8,160,1536]{2,0,1:T(8,128)(2,1)}, u32[]{:S(2)}, u32[]{:S(2)}) async-start(bf16[8,160,1536]{2,0,1:T(8,128)(2,1)} %bitcast.211), calls=%async_computation.2 | async-start | bytes 7864320 | tf_op jit(solution)/shard_map/all_to_all | solution.py:231
  244.9 3.9 fusion.32
  248.9 6.8 %fusion.15 = bf16[32,8,5,1536]{3,1,0,2:T(8,128)(2,1)} fusion(bf16[5,128,1536]{2,1,0:T(8,128)(2,1)S(1)} %copy-done, bf16[5,1536,128]{2,1,0:T(8,128)(2,1)} %param.36, bf16[32,8,5,1536]{3,1,2,0:T(8,128)(2,1)} %bitcast.46, f32[256,5,128]{2,0,1:T(8,128)S(1)} %fusion.32), kind=kOutput, calls=%fused_computation.20 | convolution fusion | flops 1009582080 | bytes 12451840 | tf_op jit(solution)/shard_map/ref,efd->red/dot_general | solution.py:61
  255.7 4.3 %copy.106 = bf16[32,8,5,1536]{3,1,2,0:T(8,128)(2,1)} copy(bf16[32,8,5,1536]{3,1,0,2:T(8,128)(2,1)} %fusion.15) | data formatting | bytes 7864320 | tf_op jit(solution)/shard_map/reshape | solution.py:236
  260.0 32.6 %all-to-all-done.2 = bf16[8,160,1536]{2,0,1:T(8,128)(2,1)} async-done(((bf16[8,160,1536]{2,0,1:T(8,128)(2,1)}), bf16[8,160,1536]{2,0,1:T(8,128)(2,1)}, u32[]{:S(2)}, u32[]{:S(2)}) %all-to-all-start.2) | async-done | bytes 3932192 | tf_op jit(solution)/shard_map/all_to_all | solution.py:231
  292.7 5.1 %all-to-all-start.5 = ((bf16[8,160,1536]{2,0,1:T(8,128)(2,1)}), bf16[8,160,1536]{2,0,1:T(8,128)(2,1)}, u32[]{:S(2)}, u32[]{:S(2)}) async-start(bf16[8,160,1536]{2,0,1:T(8,128)(2,1)} %bitcast.210), calls=%async_computation.5 | async-start | bytes 7864320 | tf_op jit(solution)/shard_map/all_to_all | solution.py:238
  297.8 3.9 fusion.26
  301.7 6.9 %fusion.14 = bf16[32,8,5,1536]{3,1,0,2:T(8,128)(2,1)} fusion(bf16[5,128,1536]{2,1,0:T(8,128)(2,1)S(1)} %copy-done, bf16[5,1536,128]{2,1,0:T(8,128)(2,1)} %param.36, bf16[32,8,5,1536]{3,1,2,0:T(8,128)(2,1)} %bitcast.35, f32[256,5,128]{2,0,1:T(8,128)S(1)} %fusion.26), kind=kOutput, calls=%fused_computation.19 | convolution fusion | flops 1009582080 | bytes 12451840 | tf_op jit(solution)/shard_map/ref,efd->red/dot_general | solution.py:61
  308.6 4.3 %copy.102 = bf16[32,8,5,1536]{3,1,2,0:T(8,128)(2,1)} copy(bf16[32,8,5,1536]{3,1,0,2:T(8,128)(2,1)} %fusion.14) | data formatting | bytes 7864320 | tf_op jit(solution)/shard_map/reshape | solution.py:236
  312.9 32.9 %all-to-all-done.5 = bf16[8,160,1536]{2,0,1:T(8,128)(2,1)} async-done(((bf16[8,160,1536]{2,0,1:T(8,128)(2,1)}), bf16[8,160,1536]{2,0,1:T(8,128)(2,1)}, u32[]{:S(2)}, u32[]{:S(2)}) %all-to-all-start.5) | async-done | bytes 3932192 | tf_op jit(solution)/shard_map/all_to_all | solution.py:238
  345.8 5.7 %all-to-all-start.3 = ((bf16[8,160,1536]{2,0,1:T(8,128)(2,1)}), bf16[8,160,1536]{2,0,1:T(8,128)(2,1)}, u32[]{:S(2)}, u32[]{:S(2)}) async-start(bf16[8,160,1536]{2,0,1:T(8,128)(2,1)} %bitcast.209), calls=%async_computation.3 | async-start | bytes 7864320 | tf_op jit(solution)/shard_map/all_to_all | solution.py:238
  351.5 1.1 select_reduce_fusion
  352.7 4.0 reduce_sum.131
  356.6 1.6 copy.107
  358.2 1.2 reshape.436
  359.4 39.7 %all-to-all-done.3 = bf16[8,160,1536]{2,0,1:T(8,128)(2,1)} async-done(((bf16[8,160,1536]{2,0,1:T(8,128)(2,1)}), bf16[8,160,1536]{2,0,1:T(8,128)(2,1)}, u32[]{:S(2)}, u32[]{:S(2)}) %all-to-all-start.3) | async-done | bytes 3932192 | tf_op jit(solution)/shard_map/all_to_all | solution.py:238
  399.2 4.0 reduce_sum.130
  403.2 1.6 copy.103
  404.7 1.2 reshape.431
  406.0 2.0 fusion.85
  408.0 2.3 fusion.20
  (107 shorter events, 6.1 us)
Async XLA Ops:
  0.6 248.2 %copy-start = (bf16[5,128,1536]{2,1,0:T(8,128)(2,1)S(1)}, bf16[5,128,1536]{2,1,0:T(8,128)(2,1)}, u32[]{:S(2)}) copy-start(bf16[5,128,1536]{2,1,0:T(8,128)(2,1)} %param.37) | copy-start | bytes 5898244
  5.1 29.6 %copy-start.21 = (s32[8,4]{0,1:T(4,128)S(1)}, s32[8,4]{0,1:T(4,128)}, u32[]{:S(2)}) copy-start(s32[8,4]{0,1:T(4,128)} %param.30) | copy-start | bytes 388
  5.1 29.8 %copy-start.26 = (s32[64]{0:T(128)S(1)}, s32[64]{0:T(128)}, u32[]{:S(2)}) copy-start(s32[64]{0:T(128)} %param.31) | copy-start | bytes 772
  39.2 9.1 %copy-start.27 = (s32[1,4]{1,0:T(1,128)S(1)}, s32[1,4]{1,0:T(1,128)}, u32[]{:S(2)}) copy-start(s32[1,4]{1,0:T(1,128)} %param.29) | copy-start | bytes 52
  39.2 9.2 %copy-start.19 = (s32[64,8]{0,1:T(8,128)S(1)}, s32[64,8]{0,1:T(8,128)}, u32[]{:S(2)}) copy-start(s32[64,8]{0,1:T(8,128)} %param.33) | copy-start | bytes 6148
  39.2 9.7 %copy-start.6 = (bf16[256,1536]{1,0:T(8,128)(2,1)S(1)}, bf16[256,1536]{1,0:T(8,128)(2,1)}, u32[]{:S(2)}) copy-start(bf16[256,1536]{1,0:T(8,128)(2,1)} %param.19) | copy-start | bytes 2359300
  39.2 10.2 %copy-start.23 = (bf16[1536,128]{1,0:T(8,128)(2,1)S(1)}, bf16[1536,128]{1,0:T(8,128)(2,1)}, u32[]{:S(2)}) copy-start(bf16[1536,128]{1,0:T(8,128)(2,1)} %param.22) | copy-start | bytes 1179652
  39.2 10.2 %copy-start.24 = (f32[1536]{0:T(1024)S(1)}, f32[1536]{0:T(1024)}, u32[]{:S(2)}) copy-start(f32[1536]{0:T(1024)} %param.20) | copy-start | bytes 18436
  39.2 64.3 %all-to-all-start = ((bf16[8,4,57344]{2,1,0:T(4,128)(2,1)}), bf16[8,4,57344]{2,1,0:T(4,128)(2,1)}, u32[]{:S(2)}, u32[]{:S(2)}) async-start(bf16[8,4,57344]{2,1,0:T(4,128)(2,1)} %broadcast_in_dim.166), calls=%async_computation | async-start | bytes 7340032 | tf_op jit(solution)/shard_map/all_to_all | solution.py:122
  48.5 53.8 %copy-start.9 = (s32[64,8]{1,0:T(8,128)}, s32[64,8]{1,0:T(8,128)S(1)}, u32[]{:S(2)}) copy-start(s32[64,8]{1,0:T(8,128)S(1)} %copy.95) | copy-start | bytes 6148
  48.6 52.3 %copy-start.22 = (bf16[1536,384]{1,0:T(8,128)(2,1)S(1)}, bf16[1536,384]{1,0:T(8,128)(2,1)}, u32[]{:S(2)}) copy-start(bf16[1536,384]{1,0:T(8,128)(2,1)} %param.21) | copy-start | bytes 3538948
  49.4 52.9 %copy-start.14 = (f32[256,32]{0,1:T(8,128)}, f32[256,32]{0,1:T(8,128)S(1)}, u32[]{:S(2)}) copy-start(f32[256,32]{0,1:T(8,128)S(1)} %get-tuple-element.10) | copy-start | bytes 98308
  49.4 52.9 %copy-start.16 = (f32[256,32]{0,1:T(8,128)}, f32[256,32]{0,1:T(8,128)S(1)}, u32[]{:S(2)}) copy-start(f32[256,32]{0,1:T(8,128)S(1)} %get-tuple-element.11) | copy-start | bytes 98308
  106.5 1.5 copy-start.4
  117.0 3.4 copy-start.11
  117.0 3.8 copy-start.15
  117.0 3.8 copy-start.17
  117.0 3.9 copy-start.3
  120.9 7.8 %slice-start = ((bf16[4,57344]{1,0:T(4,128)(2,1)}), bf16[4,2048]{1,0:T(4,128)(2,1)S(1)}, s32[]{:S(2)}) async-start(bf16[4,57344]{1,0:T(4,128)(2,1)} %copy-done.4), calls=%async_computation.6 | async-start | bytes 32768 | tf_op jit(solution)/shard_map/slice | solution.py:133
  120.9 8.0 %copy-start.7 = (bf16[256,1536]{1,0:T(8,128)(2,1)S(1)}, bf16[256,1536]{1,0:T(8,128)(2,1)}, u32[]{:S(2)}) copy-start(bf16[256,1536]{1,0:T(8,128)(2,1)} %param.19) | copy-start | bytes 2359300
  120.9 8.0 %copy-start.25 = (f32[1536]{0:T(1024)S(1)}, f32[1536]{0:T(1024)}, u32[]{:S(2)}) copy-start(f32[1536]{0:T(1024)} %param.20) | copy-start | bytes 18436
  143.8 8.2 %copy-start.1 = (f32[2,2048,256,3]{2,1,3,0:T(8,128)S(1)}, f32[2,2048,256,3]{2,1,3,0:T(8,128)}, u32[]{:S(2)}) copy-start(f32[2,2048,256,3]{2,1,3,0:T(8,128)} %get-tuple-element.19) | copy-start | bytes 37748740
  152.1 3.6 copy-start.8
  155.7 5.9 %copy-start.10 = (s32[64,8]{1,0:T(8,128)S(1)}, s32[64,8]{1,0:T(8,128)}, u32[]{:S(2)}) copy-start(s32[64,8]{1,0:T(8,128)} %copy-done.9) | copy-start | bytes 6148
  157.2 16.5 %copy-start.18 = (f32[1536]{0:T(1024)S(1)}, f32[1536]{0:T(1024)}, u32[]{:S(2)}) copy-start(f32[1536]{0:T(1024)} %param.32) | copy-start | bytes 18436
  157.2 15.1 %all-to-all-start.1 = ((bf16[4,64,1536]{2,1,0:T(8,128)(2,1)}), bf16[4,64,1536]{2,1,0:T(8,128)(2,1)S(1)}, u32[]{:S(2)}, u32[]{:S(2)}) async-start(bf16[4,64,1536]{2,1,0:T(8,128)(2,1)} %bitcast.31), calls=%async_computation.1 | async-start | bytes 1572864 | tf_op jit(solution)/shard_map/all_to_all | solution.py:196
  163.3 0.6 copy-start.12
  172.4 4.4 %copy-start.5 = (bf16[64,1536]{1,0:T(8,128)(2,1)}, bf16[64,1536]{1,0:T(8,128)(2,1)S(1)}, u32[]{:S(2)}) copy-start(bf16[64,1536]{1,0:T(8,128)(2,1)S(1)} %reduce_sum.126) | copy-start | bytes 589828
  181.1 54.9 %all-to-all-start.4 = ((bf16[8,160,1536]{2,0,1:T(8,128)(2,1)}), bf16[8,160,1536]{2,0,1:T(8,128)(2,1)}, u32[]{:S(2)}, u32[]{:S(2)}) async-start(bf16[8,160,1536]{2,0,1:T(8,128)(2,1)} %bitcast.212), calls=%async_computation.4 | async-start | bytes 7864320 | tf_op jit(solution)/shard_map/all_to_all | solution.py:231
  239.5 53.2 %all-to-all-start.2 = ((bf16[8,160,1536]{2,0,1:T(8,128)(2,1)}), bf16[8,160,1536]{2,0,1:T(8,128)(2,1)}, u32[]{:S(2)}, u32[]{:S(2)}) async-start(bf16[8,160,1536]{2,0,1:T(8,128)(2,1)} %bitcast.211), calls=%async_computation.2 | async-start | bytes 7864320 | tf_op jit(solution)/shard_map/all_to_all | solution.py:231
  292.7 53.1 %all-to-all-start.5 = ((bf16[8,160,1536]{2,0,1:T(8,128)(2,1)}), bf16[8,160,1536]{2,0,1:T(8,128)(2,1)}, u32[]{:S(2)}, u32[]{:S(2)}) async-start(bf16[8,160,1536]{2,0,1:T(8,128)(2,1)} %bitcast.210), calls=%async_computation.5 | async-start | bytes 7864320 | tf_op jit(solution)/shard_map/all_to_all | solution.py:238
  345.8 5.7 %copy-start.20 = (f32[64,8]{0,1:T(8,128)S(1)}, f32[64,8]{0,1:T(8,128)}, u32[]{:S(2)}) copy-start(f32[64,8]{0,1:T(8,128)} %param.34) | copy-start | bytes 6148
  345.8 5.8 %copy-start.13 = (s32[64,8]{1,0:T(8,128)S(1)}, s32[64,8]{1,0:T(8,128)}, u32[]{:S(2)}) copy-start(s32[64,8]{1,0:T(8,128)} %copy-done.12) | copy-start | bytes 6148
  345.8 53.4 %all-to-all-start.3 = ((bf16[8,160,1536]{2,0,1:T(8,128)(2,1)}), bf16[8,160,1536]{2,0,1:T(8,128)(2,1)}, u32[]{:S(2)}, u32[]{:S(2)}) async-start(bf16[8,160,1536]{2,0,1:T(8,128)(2,1)} %bitcast.209), calls=%async_computation.3 | async-start | bytes 7864320 | tf_op jit(solution)/shard_map/all_to_all | solution.py:238
  406.0 2.0 copy-start.2

commit v7 on v6

--- a/solution.py
+++ b/solution.py
@@ -165,8 +165,11 @@
     ) + low_rank_term(va_sel, vb_sel, kv_cols, hid_index * kv_cols)
     values_own = values_own.astype(jnp.bfloat16)
     running_max = jnp.full((kv_local, group_share, query_rows), neg_large, jnp.float32)
-    key_piece = lax.all_gather(keys_own, "exp", axis=0, tiled=True)
-    value_piece = lax.all_gather(values_own, "exp", axis=0, tiled=True)
+    kv_piece = lax.all_gather(
+        jnp.concatenate([keys_own, values_own], axis=1), "exp", axis=0, tiled=True
+    )
+    key_piece = kv_piece[:, :kv_cols]
+    value_piece = kv_piece[:, kv_cols:]
     piece_len = key_piece.shape[0]
     key_ids = jnp.arange(piece_len, dtype=jnp.int32)
     key_request = request_of(key_ids, group_len)

time: 416 us -> 412 us (level)
  blocking collectives: 92.8 us -> 28.5 us
  waiting for transfers between devices: 159 us -> 218 us
  between operations: 1.54 us -> 14.8 us
  matrix products: 47.9 us -> 43.7 us
    all_gather x2 -> x0, blocking collectives: 64.3 us -> none  [the longest x1 51 us: per_device(): key_piece = lax.all_gather(keys_own, 'exp', axis=0, tiled=True)]
    all_to_all x1, waiting for transfers between devices: 0.01 us -> 40.4 us  [per_device(): lax.all_to_all(jnp.broadcast_to(rows_pick[None], (exp_count,) + rows_pick...]
    all_gather x0 -> x1, waiting for transfers between devices: none -> 19 us  [per_device(): lax.all_gather(jnp.concatenate([keys_own, values_own], axis=1), 'exp', ax...]
    dot_general x1, matrix products: 7.73 us -> 2.07 us  [per_device(): jnp.einsum('qkgh,nkh->kgqn', query_matrix, key_heads, preferred_element_t...]
  transfers between devices with their start and end apart: 6 -> 7, of which waited for: 5 -> 7; matrix products, arithmetic and copies ran while one was open for 12% -> 12% of each run, Pallas kernels for 0% -> 0%
where the time goes in v7:
time: 412 us; the launch traced here: 411 us
  waiting for transfers between devices  218 us (53%)
  local copies, waits for them, and re-layouts  48.9 us (12%)
  matrix products  43.7 us (11%)
  starting transfers between devices  36.1 us (9%)
  blocking collectives  28.5 us (7%)
  other arithmetic  20.4 us (5%)
  between operations  14.8 us (4%)
    all_to_all x2, waiting for transfers between devices, per_device(): lax.all_to_all(copies, ('exp', 'hid'), split_axis=1, concat_axis=0, tiled...  77.7 us
    all_to_all x2, waiting for transfers between devices, per_device(): lax.all_to_all(partials, ('exp', 'hid'), split_axis=1, concat_axis=1, til...  72.8 us
    all_to_all x1, waiting for transfers between devices, per_device(): lax.all_to_all(jnp.broadcast_to(rows_pick[None], (exp_count,) + rows_pick...  40.4 us
    all_gather x1, blocking collectives, per_device(): along_req = lax.all_gather(bank, 'req', axis=0, tiled=True)  28.5 us
    all_gather x1, waiting for transfers between devices, per_device(): lax.all_gather(jnp.concatenate([keys_own, values_own], axis=1), 'exp', ax...  19 us
    dot_general x2, matrix products, expert_rows(): jnp.einsum('ref,efd->red', hidden, expert_down_weight, preferred_element_...  13.7 us
    all_to_all x2, starting transfers between devices, per_device(): lax.all_to_all(copies, ('exp', 'hid'), split_axis=1, concat_axis=0, tiled...  12.3 us
    broadcast_in_dim x6, local copies, waits for them, and re-layouts, per_device(): jnp.broadcast_to(part_out.reshape(cap_part, exp_count, 1, local_exp, widt...  10.9 us
  transfers between devices with their start and end apart: 7, of which 7 were waited for; matrix products, arithmetic and copies ran while one was open for 12% of the time, Pallas kernels for 0%

profile of v7, /device:TPU:3, one launch (start us, length us, event | category | flops | bytes accessed | tf_op | source)
XLA Modules:
  0.0 410.5 jit_solution(1728946172586464742)
XLA Ops:
  7.2 0.8 dynamic-slice_bitcast_fusion.1
  8.0 1.0 copy.85
  9.3 0.7 dynamic-slice_bitcast_fusion
  10.1 1.0 copy.84
  11.6 28.5 %all-gather = bf16[8,1,57344]{2,1,0:T(2,128)(2,1)S(1)} all-gather(bf16[1,1,57344]{2,1,0:T(2,128)(2,1)S(1)} %maximum_bitcast_fusion), channel_id=1, replica_groups=mesh['req'=8,'exp'=8,'hid'=4] {'req'}, dimensions={0}, use_global_device_ids=true | all-gather | bytes 1032192 | tf_op jit(solution)/shard_map/all_gather | solution.py:116
  40.2 1.0 copy.149
  41.6 1.0 gather_fusion
  42.9 2.8 broadcast_in_dim.166
  45.7 9.0 %all-to-all-start = ((bf16[8,4,57344]{2,1,0:T(4,128)(2,1)}), bf16[8,4,57344]{2,1,0:T(4,128)(2,1)}, u32[]{:S(2)}, u32[]{:S(2)}) async-start(bf16[8,4,57344]{2,1,0:T(4,128)(2,1)} %broadcast_in_dim.166), calls=%async_computation | async-start | bytes 7340032 | tf_op jit(solution)/shard_map/all_to_all | solution.py:122
  56.3 0.6 pad_maximum_fusion.1
  57.5 40.4 %all-to-all-done = bf16[8,4,57344]{2,1,0:T(4,128)(2,1)} async-done(((bf16[8,4,57344]{2,1,0:T(4,128)(2,1)}), bf16[8,4,57344]{2,1,0:T(4,128)(2,1)}, u32[]{:S(2)}, u32[]{:S(2)}) %all-to-all-start) | async-done | bytes 3670048 | tf_op jit(solution)/shard_map/all_to_all | solution.py:122
  97.9 2.9 gather_fusion.1
  100.9 0.9 fusion.117
  101.8 2.1 reshape.421
  103.9 1.4 copy.87
  105.3 2.2 fusion.106
  107.5 2.1 reshape.419
  109.7 1.3 copy.86
  111.0 1.7 fusion.110
  112.7 0.9 select_convert_fusion
  114.4 0.7 pad_maximum_fusion
  115.4 2.6 fusion.108
  118.6 1.2 convolution_add_fusion.1
  120.1 19.0 %all-gather.3.cloned.1.call-done = bf16[2048,256]{0,1:T(8,128)(2,1)} async-done(((bf16[256,256]{0,1:T(8,128)(2,1)}), bf16[2048,256]{0,1:T(8,128)(2,1)}) %all-gather.3.cloned.1.call-update) | async-done | bytes 1048592 | tf_op jit(solution)/shard_map/all_gather | solution.py:168
  139.1 1.3 fusion.116
  140.4 2.1 fusion
  142.5 3.2 fusion.1
  145.7 3.6 fusion.57
  149.3 1.5 convolution_convert_fusion.3
  150.8 4.4 %all-to-all-start.1 = ((bf16[4,64,1536]{2,1,0:T(8,128)(2,1)}), bf16[4,64,1536]{2,1,0:T(8,128)(2,1)S(1)}, u32[]{:S(2)}, u32[]{:S(2)}) async-start(bf16[4,64,1536]{2,1,0:T(8,128)(2,1)} %bitcast.31), calls=%async_computation.1 | async-start | bytes 1572864 | tf_op jit(solution)/shard_map/all_to_all | solution.py:199
  155.3 1.2 reduce-window.11
  157.6 8.2 %all-to-all-done.1 = bf16[4,64,1536]{2,1,0:T(8,128)(2,1)S(1)} async-done(((bf16[4,64,1536]{2,1,0:T(8,128)(2,1)}), bf16[4,64,1536]{2,1,0:T(8,128)(2,1)S(1)}, u32[]{:S(2)}, u32[]{:S(2)}) %all-to-all-start.1) | async-done | bytes 786464 | tf_op jit(solution)/shard_map/all_to_all | solution.py:199
  166.0 1.2 multiply_reduce_fusion
  167.2 1.7 convolution_convert_fusion.2
  168.8 1.5 fusion.115
  170.3 1.4 broadcast_in_dim.173
  171.7 0.6 copy.95
  172.4 2.2 broadcast_in_dim.174
  174.6 7.2 %all-to-all-start.2 = ((bf16[8,160,1536]{2,0,1:T(8,128)(2,1)}), bf16[8,160,1536]{2,0,1:T(8,128)(2,1)}, u32[]{:S(2)}, u32[]{:S(2)}) async-start(bf16[8,160,1536]{2,0,1:T(8,128)(2,1)} %bitcast.212), calls=%async_computation.2 | async-start | bytes 7864320 | tf_op jit(solution)/shard_map/all_to_all | solution.py:234
  181.8 1.4 broadcast_in_dim.175
  183.3 1.7 copy.99
  185.0 44.8 %all-to-all-done.2 = bf16[8,160,1536]{2,0,1:T(8,128)(2,1)} async-done(((bf16[8,160,1536]{2,0,1:T(8,128)(2,1)}), bf16[8,160,1536]{2,0,1:T(8,128)(2,1)}, u32[]{:S(2)}, u32[]{:S(2)}) %all-to-all-start.2) | async-done | bytes 3932192 | tf_op jit(solution)/shard_map/all_to_all | solution.py:234
  229.8 3.4 broadcast_in_dim.176
  233.2 5.1 %all-to-all-start.4 = ((bf16[8,160,1536]{2,0,1:T(8,128)(2,1)}), bf16[8,160,1536]{2,0,1:T(8,128)(2,1)}, u32[]{:S(2)}, u32[]{:S(2)}) async-start(bf16[8,160,1536]{2,0,1:T(8,128)(2,1)} %bitcast.211), calls=%async_computation.4 | async-start | bytes 7864320 | tf_op jit(solution)/shard_map/all_to_all | solution.py:234
  238.3 3.9 fusion.26
  242.3 6.8 %fusion.14 = bf16[32,8,5,1536]{3,1,0,2:T(8,128)(2,1)} fusion(bf16[5,128,1536]{2,1,0:T(8,128)(2,1)S(1)} %copy-done, bf16[5,1536,128]{2,1,0:T(8,128)(2,1)} %param.36, bf16[32,8,5,1536]{3,1,2,0:T(8,128)(2,1)} %bitcast.35, f32[256,5,128]{2,0,1:T(8,128)S(1)} %fusion.26), kind=kOutput, calls=%fused_computation.19 | convolution fusion | flops 1009582080 | bytes 12451840 | tf_op jit(solution)/shard_map/ref,efd->red/dot_general | solution.py:61
  249.1 4.3 %copy.97 = bf16[32,8,5,1536]{3,1,2,0:T(8,128)(2,1)} copy(bf16[32,8,5,1536]{3,1,0,2:T(8,128)(2,1)} %fusion.14) | data formatting | bytes 7864320 | tf_op jit(solution)/shard_map/reshape | solution.py:239
  253.4 32.9 %all-to-all-done.4 = bf16[8,160,1536]{2,0,1:T(8,128)(2,1)} async-done(((bf16[8,160,1536]{2,0,1:T(8,128)(2,1)}), bf16[8,160,1536]{2,0,1:T(8,128)(2,1)}, u32[]{:S(2)}, u32[]{:S(2)}) %all-to-all-start.4) | async-done | bytes 3932192 | tf_op jit(solution)/shard_map/all_to_all | solution.py:234
  286.3 5.1 %all-to-all-start.3 = ((bf16[8,160,1536]{2,0,1:T(8,128)(2,1)}), bf16[8,160,1536]{2,0,1:T(8,128)(2,1)}, u32[]{:S(2)}, u32[]{:S(2)}) async-start(bf16[8,160,1536]{2,0,1:T(8,128)(2,1)} %bitcast.210), calls=%async_computation.3 | async-start | bytes 7864320 | tf_op jit(solution)/shard_map/all_to_all | solution.py:241
  291.4 3.9 fusion.32
  295.3 6.9 %fusion.15 = bf16[32,8,5,1536]{3,1,0,2:T(8,128)(2,1)} fusion(bf16[5,128,1536]{2,1,0:T(8,128)(2,1)S(1)} %copy-done, bf16[5,1536,128]{2,1,0:T(8,128)(2,1)} %param.36, bf16[32,8,5,1536]{3,1,2,0:T(8,128)(2,1)} %bitcast.46, f32[256,5,128]{2,0,1:T(8,128)S(1)} %fusion.32), kind=kOutput, calls=%fused_computation.20 | convolution fusion | flops 1009582080 | bytes 12451840 | tf_op jit(solution)/shard_map/ref,efd->red/dot_general | solution.py:61
  302.2 4.3 %copy.101 = bf16[32,8,5,1536]{3,1,2,0:T(8,128)(2,1)} copy(bf16[32,8,5,1536]{3,1,0,2:T(8,128)(2,1)} %fusion.15) | data formatting | bytes 7864320 | tf_op jit(solution)/shard_map/reshape | solution.py:239
  306.5 32.9 %all-to-all-done.3 = bf16[8,160,1536]{2,0,1:T(8,128)(2,1)} async-done(((bf16[8,160,1536]{2,0,1:T(8,128)(2,1)}), bf16[8,160,1536]{2,0,1:T(8,128)(2,1)}, u32[]{:S(2)}, u32[]{:S(2)}) %all-to-all-start.3) | async-done | bytes 3932192 | tf_op jit(solution)/shard_map/all_to_all | solution.py:241
  339.4 5.2 %all-to-all-start.5 = ((bf16[8,160,1536]{2,0,1:T(8,128)(2,1)}), bf16[8,160,1536]{2,0,1:T(8,128)(2,1)}, u32[]{:S(2)}, u32[]{:S(2)}) async-start(bf16[8,160,1536]{2,0,1:T(8,128)(2,1)} %bitcast.209), calls=%async_computation.5 | async-start | bytes 7864320 | tf_op jit(solution)/shard_map/all_to_all | solution.py:241
  344.7 1.1 select_reduce_fusion
  345.8 4.0 reduce_sum.130
  349.8 1.6 copy.98
  351.4 1.2 reshape.431
  352.6 40.0 %all-to-all-done.5 = bf16[8,160,1536]{2,0,1:T(8,128)(2,1)} async-done(((bf16[8,160,1536]{2,0,1:T(8,128)(2,1)}), bf16[8,160,1536]{2,0,1:T(8,128)(2,1)}, u32[]{:S(2)}, u32[]{:S(2)}) %all-to-all-start.5) | async-done | bytes 3932192 | tf_op jit(solution)/shard_map/all_to_all | solution.py:241
  392.6 4.0 reduce_sum.131
  396.5 1.6 copy.102
  398.1 1.2 reshape.436
  399.3 2.0 fusion.85
  401.4 2.3 fusion.20
  (118 shorter events, 6.9 us)
Async XLA Ops:
  7.2 235.1 %copy-start = (bf16[5,128,1536]{2,1,0:T(8,128)(2,1)S(1)}, bf16[5,128,1536]{2,1,0:T(8,128)(2,1)}, u32[]{:S(2)}) copy-start(bf16[5,128,1536]{2,1,0:T(8,128)(2,1)} %param.37) | copy-start | bytes 5898244
  11.6 29.6 %copy-start.23 = (s32[8,4]{0,1:T(4,128)S(1)}, s32[8,4]{0,1:T(4,128)}, u32[]{:S(2)}) copy-start(s32[8,4]{0,1:T(4,128)} %param.30) | copy-start | bytes 388
  11.6 29.8 %copy-start.30 = (s32[64]{0:T(128)S(1)}, s32[64]{0:T(128)}, u32[]{:S(2)}) copy-start(s32[64]{0:T(128)} %param.31) | copy-start | bytes 772
  45.7 9.0 %copy-start.31 = (s32[1,4]{1,0:T(1,128)S(1)}, s32[1,4]{1,0:T(1,128)}, u32[]{:S(2)}) copy-start(s32[1,4]{1,0:T(1,128)} %param.29) | copy-start | bytes 52
  45.7 9.4 %copy-start.4 = (bf16[256,1536]{1,0:T(8,128)(2,1)S(1)}, bf16[256,1536]{1,0:T(8,128)(2,1)}, u32[]{:S(2)}) copy-start(bf16[256,1536]{1,0:T(8,128)(2,1)} %param.19) | copy-start | bytes 2359300
  45.7 9.9 %copy-start.26 = (bf16[1536,128]{1,0:T(8,128)(2,1)S(1)}, bf16[1536,128]{1,0:T(8,128)(2,1)}, u32[]{:S(2)}) copy-start(bf16[1536,128]{1,0:T(8,128)(2,1)} %param.22) | copy-start | bytes 1179652
  45.7 9.9 %copy-start.28 = (f32[1536]{0:T(1024)S(1)}, f32[1536]{0:T(1024)}, u32[]{:S(2)}) copy-start(f32[1536]{0:T(1024)} %param.20) | copy-start | bytes 18436
  45.7 52.2 %all-to-all-start = ((bf16[8,4,57344]{2,1,0:T(4,128)(2,1)}), bf16[8,4,57344]{2,1,0:T(4,128)(2,1)}, u32[]{:S(2)}, u32[]{:S(2)}) async-start(bf16[8,4,57344]{2,1,0:T(4,128)(2,1)} %broadcast_in_dim.166), calls=%async_computation | async-start | bytes 7340032 | tf_op jit(solution)/shard_map/all_to_all | solution.py:122
  54.8 84.3 %all-gather.3.cloned.1.call-start = ((), (), s32[]{:S(2)}) async-start(), calls=%async_computation.6 | async-start | bytes 1179648 | tf_op jit(solution)/shard_map/all_gather | solution.py:168
  55.0 45.9 %copy-start.21 = (s32[4,1]{0,1:T(1,128)}, s32[4,1]{0,1:T(1,128)S(1)}, u32[]{:S(2)}) copy-start(s32[4,1]{0,1:T(1,128)S(1)} %reduce-window.10) | copy-start | bytes 52
  55.0 45.9 %copy-start.17 = (s32[256]{0:T(256)}, s32[256]{0:T(256)S(1)}, u32[]{:S(2)}) copy-start(s32[256]{0:T(256)S(1)} %iota_add_fusion) | copy-start | bytes 3076
  55.1 1.9 copy-start.14
  55.4 49.9 %copy-start.24 = (f32[256]{0:T(256)}, f32[256]{0:T(256)S(1)}, u32[]{:S(2)}) copy-start(f32[256]{0:T(256)S(1)} %add_rsqrt_fusion) | copy-start | bytes 3076
  55.7 0.6 copy-start.9
  55.7 0.6 copy-start.11
  100.9 0.9 copy-start.2
  109.6 3.0 slice-start
  110.9 2.9 copy-start.5
  110.9 2.9 copy-start.25
  110.9 2.9 copy-start.27
  110.9 2.9 copy-start.29
  110.9 3.4 copy-start.13
  110.9 4.1 %copy-start.19 = (s32[64,8]{0,1:T(8,128)S(1)}, s32[64,8]{0,1:T(8,128)}, u32[]{:S(2)}) copy-start(s32[64,8]{0,1:T(8,128)} %param.33) | copy-start | bytes 6148
  111.0 4.3 %copy-start.22 = (s32[4,1]{0,1:T(1,128)S(1)}, s32[4,1]{0,1:T(1,128)}, u32[]{:S(2)}) copy-start(s32[4,1]{0,1:T(1,128)} %copy-done.21) | copy-start | bytes 52
  114.3 3.7 copy-start.15
  114.3 3.7 copy-start.18
  114.3 4.2 %slice-start.1 = ((bf16[4,57344]{1,0:T(4,128)(2,1)}), bf16[4,6144]{1,0:T(4,128)(2,1)S(1)}, s32[]{:S(2)}) async-start(bf16[4,57344]{1,0:T(4,128)(2,1)} %copy-done.2), calls=%async_computation.8 | async-start | bytes 98304 | tf_op jit(solution)/shard_map/slice | solution.py:133
  115.3 4.7 %copy-start.10 = (f32[256,32]{0,1:T(8,128)S(1)}, f32[256,32]{0,1:T(8,128)}, u32[]{:S(2)}) copy-start(f32[256,32]{0,1:T(8,128)} %copy-done.9) | copy-start | bytes 98308
  115.3 4.7 %copy-start.12 = (f32[256,32]{0,1:T(8,128)S(1)}, f32[256,32]{0,1:T(8,128)}, u32[]{:S(2)}) copy-start(f32[256,32]{0,1:T(8,128)} %copy-done.11) | copy-start | bytes 98308
  145.7 3.6 copy-start.6
  150.8 16.4 %copy-start.16 = (f32[1536]{0:T(1024)S(1)}, f32[1536]{0:T(1024)}, u32[]{:S(2)}) copy-start(f32[1536]{0:T(1024)} %param.32) | copy-start | bytes 18436
  150.8 15.0 %all-to-all-start.1 = ((bf16[4,64,1536]{2,1,0:T(8,128)(2,1)}), bf16[4,64,1536]{2,1,0:T(8,128)(2,1)S(1)}, u32[]{:S(2)}, u32[]{:S(2)}) async-start(bf16[4,64,1536]{2,1,0:T(8,128)(2,1)} %bitcast.31), calls=%async_computation.1 | async-start | bytes 1572864 | tf_op jit(solution)/shard_map/all_to_all | solution.py:199
  156.9 0.6 copy-start.7
  165.9 4.4 %copy-start.3 = (bf16[64,1536]{1,0:T(8,128)(2,1)}, bf16[64,1536]{1,0:T(8,128)(2,1)S(1)}, u32[]{:S(2)}) copy-start(bf16[64,1536]{1,0:T(8,128)(2,1)S(1)} %reduce_sum.126) | copy-start | bytes 589828
  174.6 55.2 %all-to-all-start.2 = ((bf16[8,160,1536]{2,0,1:T(8,128)(2,1)}), bf16[8,160,1536]{2,0,1:T(8,128)(2,1)}, u32[]{:S(2)}, u32[]{:S(2)}) async-start(bf16[8,160,1536]{2,0,1:T(8,128)(2,1)} %bitcast.212), calls=%async_computation.2 | async-start | bytes 7864320 | tf_op jit(solution)/shard_map/all_to_all | solution.py:234
  233.2 53.1 %all-to-all-start.4 = ((bf16[8,160,1536]{2,0,1:T(8,128)(2,1)}), bf16[8,160,1536]{2,0,1:T(8,128)(2,1)}, u32[]{:S(2)}, u32[]{:S(2)}) async-start(bf16[8,160,1536]{2,0,1:T(8,128)(2,1)} %bitcast.211), calls=%async_computation.4 | async-start | bytes 7864320 | tf_op jit(solution)/shard_map/all_to_all | solution.py:234
  286.3 53.1 %all-to-all-start.3 = ((bf16[8,160,1536]{2,0,1:T(8,128)(2,1)}), bf16[8,160,1536]{2,0,1:T(8,128)(2,1)}, u32[]{:S(2)}, u32[]{:S(2)}) async-start(bf16[8,160,1536]{2,0,1:T(8,128)(2,1)} %bitcast.210), calls=%async_computation.3 | async-start | bytes 7864320 | tf_op jit(solution)/shard_map/all_to_all | solution.py:241
  339.4 5.2 %copy-start.20 = (f32[64,8]{0,1:T(8,128)S(1)}, f32[64,8]{0,1:T(8,128)}, u32[]{:S(2)}) copy-start(f32[64,8]{0,1:T(8,128)} %param.34) | copy-start | bytes 6148
  339.4 5.3 %copy-start.8 = (s32[64,8]{1,0:T(8,128)S(1)}, s32[64,8]{1,0:T(8,128)}, u32[]{:S(2)}) copy-start(s32[64,8]{1,0:T(8,128)} %copy-done.7) | copy-start | bytes 6148
  339.4 53.2 %all-to-all-start.5 = ((bf16[8,160,1536]{2,0,1:T(8,128)(2,1)}), bf16[8,160,1536]{2,0,1:T(8,128)(2,1)}, u32[]{:S(2)}, u32[]{:S(2)}) async-start(bf16[8,160,1536]{2,0,1:T(8,128)(2,1)} %bitcast.209), calls=%async_computation.5 | async-start | bytes 7864320 | tf_op jit(solution)/shard_map/all_to_all | solution.py:241
  399.3 2.0 copy-start.1
Sparse Core Ops, SparseCore 0:
  115.2 23.9 all-gather.2

commit v8 on v7

--- a/solution.py
+++ b/solution.py
@@ -165,9 +165,14 @@
     ) + low_rank_term(va_sel, vb_sel, kv_cols, hid_index * kv_cols)
     values_own = values_own.astype(jnp.bfloat16)
     running_max = jnp.full((kv_local, group_share, query_rows), neg_large, jnp.float32)
-    kv_piece = lax.all_gather(
-        jnp.concatenate([keys_own, values_own], axis=1), "exp", axis=0, tiled=True
-    )
+    kv_own = jnp.concatenate([keys_own, values_own], axis=1)
+    kv_piece = lax.all_to_all(
+        jnp.broadcast_to(kv_own[None], (exp_count,) + kv_own.shape),
+        "exp",
+        split_axis=0,
+        concat_axis=0,
+        tiled=True,
+    ).reshape(exp_count * query_rows, 2 * kv_cols)
     key_piece = kv_piece[:, :kv_cols]
     value_piece = kv_piece[:, kv_cols:]
     piece_len = key_piece.shape[0]

time: 412 us -> 398 us (0.966)
  waiting for transfers between devices: 218 us -> 202 us
  between operations: 14.8 us -> 1.33 us
  local copies, waits for them, and re-layouts: 48.9 us -> 57.4 us
  starting transfers between devices: 36.1 us -> 40.9 us
    all_gather x1 -> x0, waiting for transfers between devices: 19 us -> none  [per_device(): lax.all_gather(jnp.concatenate([keys_own, values_own], axis=1), 'exp', ax...]
    all_to_all x0 -> x1, waiting for transfers between devices: none -> 5.86 us  [per_device(): lax.all_to_all(jnp.broadcast_to(kv_own[None], (exp_count,) + kv_own.shape...]
    all_to_all x0 -> x1, starting transfers between devices: none -> 4.44 us  [per_device(): lax.all_to_all(jnp.broadcast_to(kv_own[None], (exp_count,) + kv_own.shape...]
  transfers between devices with their start and end apart: 7 -> 7, of which waited for: 7 -> 7; matrix products, arithmetic and copies ran while one was open for 12% -> 15% of each run, Pallas kernels for 0% -> 0%
where the time goes in v8:
time: 398 us; the launch traced here: 396 us
  waiting for transfers between devices  202 us (51%)
  local copies, waits for them, and re-layouts  57.4 us (14%)
  matrix products  44.1 us (11%)
  starting transfers between devices  40.9 us (10%)
  blocking collectives  28.5 us (7%)
  other arithmetic  22.6 us (6%)
    all_to_all x2, waiting for transfers between devices, per_device(): lax.all_to_all(copies, ('exp', 'hid'), split_axis=1, concat_axis=0, tiled...  77.8 us
    all_to_all x2, waiting for transfers between devices, per_device(): lax.all_to_all(partials, ('exp', 'hid'), split_axis=1, concat_axis=1, til...  72.8 us
    all_to_all x1, waiting for transfers between devices, per_device(): lax.all_to_all(jnp.broadcast_to(rows_pick[None], (exp_count,) + rows_pick...  37.6 us
    all_gather x1, blocking collectives, per_device(): along_req = lax.all_gather(bank, 'req', axis=0, tiled=True)  28.5 us
    dot_general x2, matrix products, expert_rows(): jnp.einsum('ref,efd->red', hidden, expert_down_weight, preferred_element_...  13.7 us
    all_to_all x2, starting transfers between devices, per_device(): lax.all_to_all(copies, ('exp', 'hid'), split_axis=1, concat_axis=0, tiled...  12.7 us
    broadcast_in_dim x6, local copies, waits for them, and re-layouts, per_device(): jnp.broadcast_to(part_out.reshape(cap_part, exp_count, 1, local_exp, widt...  10.9 us
    all_to_all x2, starting transfers between devices, per_device(): lax.all_to_all(partials, ('exp', 'hid'), split_axis=1, concat_axis=1, til...  10.4 us
  transfers between devices with their start and end apart: 7, of which 7 were waited for; matrix products, arithmetic and copies ran while one was open for 15% of the time, Pallas kernels for 0%

profile of v8, /device:TPU:3, one launch (start us, length us, event | category | flops | bytes accessed | tf_op | source)
XLA Modules:
  0.0 396.5 jit_solution(12851483804816842418)
XLA Ops:
  1.5 1.0 copy.88
  3.5 1.0 copy.87
  5.1 28.5 %all-gather = bf16[8,1,57344]{2,1,0:T(2,128)(2,1)S(1)} all-gather(bf16[1,1,57344]{2,1,0:T(2,128)(2,1)S(1)} %maximum_bitcast_fusion), channel_id=1, replica_groups=mesh['req'=8,'exp'=8,'hid'=4] {'req'}, dimensions={0}, use_global_device_ids=true | all-gather | bytes 1032192 | tf_op jit(solution)/shard_map/all_gather | solution.py:116
  33.6 1.0 copy.155
  36.4 2.8 broadcast_in_dim.172
  39.2 9.0 %all-to-all-start = ((bf16[8,4,57344]{2,1,0:T(4,128)(2,1)}), bf16[8,4,57344]{2,1,0:T(4,128)(2,1)}, u32[]{:S(2)}, u32[]{:S(2)}) async-start(bf16[8,4,57344]{2,1,0:T(4,128)(2,1)} %broadcast_in_dim.172), calls=%async_computation | async-start | bytes 7340032 | tf_op jit(solution)/shard_map/all_to_all | solution.py:122
  52.4 1.4 fusion.108
  53.8 37.6 %all-to-all-done = bf16[8,4,57344]{2,1,0:T(4,128)(2,1)} async-done(((bf16[8,4,57344]{2,1,0:T(4,128)(2,1)}), bf16[8,4,57344]{2,1,0:T(4,128)(2,1)}, u32[]{:S(2)}, u32[]{:S(2)}) %all-to-all-start) | async-done | bytes 3670048 | tf_op jit(solution)/shard_map/all_to_all | solution.py:122
  91.4 2.9 gather_fusion.1
  95.2 2.1 reshape.426
  97.3 1.3 copy.92
  98.6 2.2 fusion.106
  100.8 2.1 reshape.423
  102.9 1.3 copy.89
  104.2 1.7 fusion.110
  105.9 1.5 select_convert_fusion
  108.2 1.0 broadcast_in_dim.174
  109.2 4.4 %all-to-all-start.1 = ((bf16[8,256,256]{1,2,0:T(8,128)(2,1)}), bf16[8,256,256]{1,2,0:T(8,128)(2,1)S(1)}, u32[]{:S(2)}, u32[]{:S(2)}) async-start(bf16[8,256,256]{1,2,0:T(8,128)(2,1)} %broadcast_in_dim.174), calls=%async_computation.1 | async-start | bytes 2097152 | tf_op jit(solution)/shard_map/all_to_all | solution.py:169
  114.2 1.4 slice.77
  115.7 1.5 reshape_reshape.7
  117.1 2.0 convolution_add_fusion.1
  119.1 1.9 copy.93
  121.1 1.7 subtract_convert_fusion
  122.8 5.9 %all-to-all-done.1 = bf16[8,256,256]{1,2,0:T(8,128)(2,1)S(1)} async-done(((bf16[8,256,256]{1,2,0:T(8,128)(2,1)}), bf16[8,256,256]{1,2,0:T(8,128)(2,1)S(1)}, u32[]{:S(2)}, u32[]{:S(2)}) %all-to-all-start.1) | async-done | bytes 1048608 | tf_op jit(solution)/shard_map/all_to_all | solution.py:169
  128.7 1.3 copy.90
  130.0 1.3 fusion.116
  132.4 3.0 fusion
  135.5 3.1 fusion.1
  138.7 3.6 fusion.57
  142.3 1.5 convolution_convert_fusion.3
  143.8 4.4 %all-to-all-start.2 = ((bf16[4,64,1536]{2,1,0:T(8,128)(2,1)}), bf16[4,64,1536]{2,1,0:T(8,128)(2,1)S(1)}, u32[]{:S(2)}, u32[]{:S(2)}) async-start(bf16[4,64,1536]{2,1,0:T(8,128)(2,1)} %bitcast.32), calls=%async_computation.2 | async-start | bytes 1572864 | tf_op jit(solution)/shard_map/all_to_all | solution.py:204
  148.3 1.2 reduce-window.11
  150.6 7.5 %all-to-all-done.2 = bf16[4,64,1536]{2,1,0:T(8,128)(2,1)S(1)} async-done(((bf16[4,64,1536]{2,1,0:T(8,128)(2,1)}), bf16[4,64,1536]{2,1,0:T(8,128)(2,1)S(1)}, u32[]{:S(2)}, u32[]{:S(2)}) %all-to-all-start.2) | async-done | bytes 786464 | tf_op jit(solution)/shard_map/all_to_all | solution.py:204
  158.3 1.2 multiply_reduce_fusion
  159.5 1.7 convolution_convert_fusion.2
  161.2 1.4 fusion.115
  162.6 1.4 broadcast_in_dim.180
  164.7 2.2 broadcast_in_dim.181
  166.9 7.6 %all-to-all-start.3 = ((bf16[8,160,1536]{2,0,1:T(8,128)(2,1)}), bf16[8,160,1536]{2,0,1:T(8,128)(2,1)}, u32[]{:S(2)}, u32[]{:S(2)}) async-start(bf16[8,160,1536]{2,0,1:T(8,128)(2,1)} %bitcast.213), calls=%async_computation.3 | async-start | bytes 7864320 | tf_op jit(solution)/shard_map/all_to_all | solution.py:239
  174.5 1.4 broadcast_in_dim.182
  176.0 1.7 copy.105
  177.7 44.9 %all-to-all-done.3 = bf16[8,160,1536]{2,0,1:T(8,128)(2,1)} async-done(((bf16[8,160,1536]{2,0,1:T(8,128)(2,1)}), bf16[8,160,1536]{2,0,1:T(8,128)(2,1)}, u32[]{:S(2)}, u32[]{:S(2)}) %all-to-all-start.3) | async-done | bytes 3932192 | tf_op jit(solution)/shard_map/all_to_all | solution.py:239
  222.6 3.5 broadcast_in_dim.183
  226.1 5.1 %all-to-all-start.5 = ((bf16[8,160,1536]{2,0,1:T(8,128)(2,1)}), bf16[8,160,1536]{2,0,1:T(8,128)(2,1)}, u32[]{:S(2)}, u32[]{:S(2)}) async-start(bf16[8,160,1536]{2,0,1:T(8,128)(2,1)} %bitcast.212), calls=%async_computation.5 | async-start | bytes 7864320 | tf_op jit(solution)/shard_map/all_to_all | solution.py:239
  231.2 3.9 fusion.26
  235.1 6.8 %fusion.14 = bf16[32,8,5,1536]{3,1,0,2:T(8,128)(2,1)} fusion(bf16[5,128,1536]{2,1,0:T(8,128)(2,1)S(1)} %copy-done, bf16[5,1536,128]{2,1,0:T(8,128)(2,1)} %param.36, bf16[32,8,5,1536]{3,1,2,0:T(8,128)(2,1)} %bitcast.36, f32[256,5,128]{2,0,1:T(8,128)S(1)} %fusion.26), kind=kOutput, calls=%fused_computation.19 | convolution fusion | flops 1009582080 | bytes 12451840 | tf_op jit(solution)/shard_map/ref,efd->red/dot_general | solution.py:61
  241.9 4.3 %copy.103 = bf16[32,8,5,1536]{3,1,2,0:T(8,128)(2,1)} copy(bf16[32,8,5,1536]{3,1,0,2:T(8,128)(2,1)} %fusion.14) | data formatting | bytes 7864320 | tf_op jit(solution)/shard_map/reshape | solution.py:244
  246.3 32.8 %all-to-all-done.5 = bf16[8,160,1536]{2,0,1:T(8,128)(2,1)} async-done(((bf16[8,160,1536]{2,0,1:T(8,128)(2,1)}), bf16[8,160,1536]{2,0,1:T(8,128)(2,1)}, u32[]{:S(2)}, u32[]{:S(2)}) %all-to-all-start.5) | async-done | bytes 3932192 | tf_op jit(solution)/shard_map/all_to_all | solution.py:239
  279.1 5.1 %all-to-all-start.4 = ((bf16[8,160,1536]{2,0,1:T(8,128)(2,1)}), bf16[8,160,1536]{2,0,1:T(8,128)(2,1)}, u32[]{:S(2)}, u32[]{:S(2)}) async-start(bf16[8,160,1536]{2,0,1:T(8,128)(2,1)} %bitcast.211), calls=%async_computation.4 | async-start | bytes 7864320 | tf_op jit(solution)/shard_map/all_to_all | solution.py:246
  284.2 3.9 fusion.32
  288.1 6.9 %fusion.15 = bf16[32,8,5,1536]{3,1,0,2:T(8,128)(2,1)} fusion(bf16[5,128,1536]{2,1,0:T(8,128)(2,1)S(1)} %copy-done, bf16[5,1536,128]{2,1,0:T(8,128)(2,1)} %param.36, bf16[32,8,5,1536]{3,1,2,0:T(8,128)(2,1)} %bitcast.47, f32[256,5,128]{2,0,1:T(8,128)S(1)} %fusion.32), kind=kOutput, calls=%fused_computation.20 | convolution fusion | flops 1009582080 | bytes 12451840 | tf_op jit(solution)/shard_map/ref,efd->red/dot_general | solution.py:61
  295.0 4.3 %copy.107 = bf16[32,8,5,1536]{3,1,2,0:T(8,128)(2,1)} copy(bf16[32,8,5,1536]{3,1,0,2:T(8,128)(2,1)} %fusion.15) | data formatting | bytes 7864320 | tf_op jit(solution)/shard_map/reshape | solution.py:244
  299.3 32.9 %all-to-all-done.4 = bf16[8,160,1536]{2,0,1:T(8,128)(2,1)} async-done(((bf16[8,160,1536]{2,0,1:T(8,128)(2,1)}), bf16[8,160,1536]{2,0,1:T(8,128)(2,1)}, u32[]{:S(2)}, u32[]{:S(2)}) %all-to-all-start.4) | async-done | bytes 3932192 | tf_op jit(solution)/shard_map/all_to_all | solution.py:246
  332.2 5.2 %all-to-all-start.6 = ((bf16[8,160,1536]{2,0,1:T(8,128)(2,1)}), bf16[8,160,1536]{2,0,1:T(8,128)(2,1)}, u32[]{:S(2)}, u32[]{:S(2)}) async-start(bf16[8,160,1536]{2,0,1:T(8,128)(2,1)} %bitcast.210), calls=%async_computation.6 | async-start | bytes 7864320 | tf_op jit(solution)/shard_map/all_to_all | solution.py:246
  337.5 1.1 select_reduce_fusion
  338.6 4.0 %reduce_sum.130 = bf16[8,8,5,1536]{3,0,2,1:T(8,128)(2,1)} reduce(bf16[8,8,4,5,1536]{4,0,3,2,1:T(8,128)(2,1)} %bitcast.44, bf16[]{:T(256)} %constant.140.clone.1), dimensions={2}, to_apply=%region_15.16 | reduce | flops 1474560 | bytes 4915202 | tf_op jit(solution)/shard_map/reduce_sum | solution.py:248
  342.6 1.6 copy.104
  344.2 1.2 reshape.436
  345.4 40.0 %all-to-all-done.6 = bf16[8,160,1536]{2,0,1:T(8,128)(2,1)} async-done(((bf16[8,160,1536]{2,0,1:T(8,128)(2,1)}), bf16[8,160,1536]{2,0,1:T(8,128)(2,1)}, u32[]{:S(2)}, u32[]{:S(2)}) %all-to-all-start.6) | async-done | bytes 3932192 | tf_op jit(solution)/shard_map/all_to_all | solution.py:246
  385.4 4.0 %reduce_sum.131 = bf16[8,8,5,1536]{3,0,2,1:T(8,128)(2,1)} reduce(bf16[8,8,4,5,1536]{4,0,3,2,1:T(8,128)(2,1)} %bitcast.55, bf16[]{:T(256)} %constant.140.clone.1), dimensions={2}, to_apply=%region_16.17 | reduce | flops 1474560 | bytes 4915202 | tf_op jit(solution)/shard_map/reduce_sum | solution.py:248
  389.4 1.6 copy.108
  390.9 1.2 reshape.441
  392.1 2.0 fusion.85
  394.2 2.3 fusion.20
  (124 shorter events, 13.7 us)
Async XLA Ops:
  0.6 234.4 %copy-start = (bf16[5,128,1536]{2,1,0:T(8,128)(2,1)S(1)}, bf16[5,128,1536]{2,1,0:T(8,128)(2,1)}, u32[]{:S(2)}) copy-start(bf16[5,128,1536]{2,1,0:T(8,128)(2,1)} %param.37) | copy-start | bytes 5898244
  5.1 29.6 %copy-start.24 = (s32[8,4]{0,1:T(4,128)S(1)}, s32[8,4]{0,1:T(4,128)}, u32[]{:S(2)}) copy-start(s32[8,4]{0,1:T(4,128)} %param.30) | copy-start | bytes 388
  5.1 29.8 %copy-start.32 = (s32[64]{0:T(128)S(1)}, s32[64]{0:T(128)}, u32[]{:S(2)}) copy-start(s32[64]{0:T(128)} %param.31) | copy-start | bytes 772
  39.2 9.0 %copy-start.33 = (s32[1,4]{1,0:T(1,128)S(1)}, s32[1,4]{1,0:T(1,128)}, u32[]{:S(2)}) copy-start(s32[1,4]{1,0:T(1,128)} %param.29) | copy-start | bytes 52
  39.2 9.2 %copy-start.22 = (s32[64,8]{0,1:T(8,128)S(1)}, s32[64,8]{0,1:T(8,128)}, u32[]{:S(2)}) copy-start(s32[64,8]{0,1:T(8,128)} %param.33) | copy-start | bytes 6148
  39.2 10.9 %copy-start.4 = (bf16[256,1536]{1,0:T(8,128)(2,1)S(1)}, bf16[256,1536]{1,0:T(8,128)(2,1)}, u32[]{:S(2)}) copy-start(bf16[256,1536]{1,0:T(8,128)(2,1)} %param.19) | copy-start | bytes 2359300
  39.2 11.4 %copy-start.28 = (bf16[1536,128]{1,0:T(8,128)(2,1)S(1)}, bf16[1536,128]{1,0:T(8,128)(2,1)}, u32[]{:S(2)}) copy-start(bf16[1536,128]{1,0:T(8,128)(2,1)} %param.22) | copy-start | bytes 1179652
  39.2 11.4 %copy-start.30 = (f32[1536]{0:T(1024)S(1)}, f32[1536]{0:T(1024)}, u32[]{:S(2)}) copy-start(f32[1536]{0:T(1024)} %param.20) | copy-start | bytes 18436
  39.2 52.2 %all-to-all-start = ((bf16[8,4,57344]{2,1,0:T(4,128)(2,1)}), bf16[8,4,57344]{2,1,0:T(4,128)(2,1)}, u32[]{:S(2)}, u32[]{:S(2)}) async-start(bf16[8,4,57344]{2,1,0:T(4,128)(2,1)} %broadcast_in_dim.172), calls=%async_computation | async-start | bytes 7340032 | tf_op jit(solution)/shard_map/all_to_all | solution.py:122
  48.5 5.3 %copy-start.7 = (s32[64,8]{1,0:T(8,128)}, s32[64,8]{1,0:T(8,128)S(1)}, u32[]{:S(2)}) copy-start(s32[64,8]{1,0:T(8,128)S(1)} %copy.96) | copy-start | bytes 6148
  49.2 3.2 copy-start.27
  49.2 4.6 %copy-start.20 = (s32[256]{0:T(256)}, s32[256]{0:T(256)S(1)}, u32[]{:S(2)}) copy-start(s32[256]{0:T(256)S(1)} %iota_add_fusion) | copy-start | bytes 3076
  50.0 1.8 copy-start.16
  50.3 48.2 %copy-start.25 = (f32[256]{0:T(256)}, f32[256]{0:T(256)S(1)}, u32[]{:S(2)}) copy-start(f32[256]{0:T(256)S(1)} %add_rsqrt_fusion) | copy-start | bytes 3076
  50.6 0.6 copy-start.12
  50.6 0.6 copy-start.13
  94.3 0.9 copy-start.2
  102.9 3.0 slice-start
  104.2 3.4 copy-start.5
  104.2 3.4 copy-start.26
  104.2 3.5 copy-start.29
  104.2 3.5 copy-start.31
  104.2 4.0 %copy-start.14 = (bf16[256,2,64]{0,2,1:T(8,128)(2,1)S(1)}, bf16[256,2,64]{0,2,1:T(8,128)(2,1)}, u32[]{:S(2)}) copy-start(bf16[256,2,64]{0,2,1:T(8,128)(2,1)} %pad_maximum_fusion.1) | copy-start | bytes 196612
  108.1 5.5 %copy-start.15 = (s32[2048]{0:T(1024)S(1)}, s32[2048]{0:T(1024)}, u32[]{:S(2)}) copy-start(s32[2048]{0:T(1024)} %convert_reduce_fusion) | copy-start | bytes 24580
  108.1 5.5 %copy-start.17 = (s32[256]{0:T(256)S(1)}, s32[256]{0:T(256)}, u32[]{:S(2)}) copy-start(s32[256]{0:T(256)} %copy-done.16) | copy-start | bytes 3076
  108.2 5.5 %copy-start.21 = (s32[256]{0:T(256)S(1)}, s32[256]{0:T(256)}, u32[]{:S(2)}) copy-start(s32[256]{0:T(256)} %copy-done.20) | copy-start | bytes 3076
  109.2 19.4 %all-to-all-start.1 = ((bf16[8,256,256]{1,2,0:T(8,128)(2,1)}), bf16[8,256,256]{1,2,0:T(8,128)(2,1)S(1)}, u32[]{:S(2)}, u32[]{:S(2)}) async-start(bf16[8,256,256]{1,2,0:T(8,128)(2,1)} %broadcast_in_dim.174), calls=%async_computation.1 | async-start | bytes 2097152 | tf_op jit(solution)/shard_map/all_to_all | solution.py:169
  135.5 3.2 copy-start.9
  138.6 3.7 copy-start.6
  142.3 5.9 %copy-start.19 = (s32[4,128]{1,0:T(4,128)S(1)}, s32[4,128]{1,0:T(4,128)}, u32[]{:S(2)}) copy-start(s32[4,128]{1,0:T(4,128)} %eq.130) | copy-start | bytes 6148
  142.3 5.9 %copy-start.8 = (s32[64,8]{1,0:T(8,128)S(1)}, s32[64,8]{1,0:T(8,128)}, u32[]{:S(2)}) copy-start(s32[64,8]{1,0:T(8,128)} %copy-done.7) | copy-start | bytes 6148
  143.8 15.7 %copy-start.18 = (f32[1536]{0:T(1024)S(1)}, f32[1536]{0:T(1024)}, u32[]{:S(2)}) copy-start(f32[1536]{0:T(1024)} %param.32) | copy-start | bytes 18436
  143.8 14.4 %all-to-all-start.2 = ((bf16[4,64,1536]{2,1,0:T(8,128)(2,1)}), bf16[4,64,1536]{2,1,0:T(8,128)(2,1)S(1)}, u32[]{:S(2)}, u32[]{:S(2)}) async-start(bf16[4,64,1536]{2,1,0:T(8,128)(2,1)} %bitcast.32), calls=%async_computation.2 | async-start | bytes 1572864 | tf_op jit(solution)/shard_map/all_to_all | solution.py:204
  150.0 0.6 copy-start.10
  158.3 4.3 %copy-start.3 = (bf16[64,1536]{1,0:T(8,128)(2,1)}, bf16[64,1536]{1,0:T(8,128)(2,1)S(1)}, u32[]{:S(2)}) copy-start(bf16[64,1536]{1,0:T(8,128)(2,1)S(1)} %reduce_sum.126) | copy-start | bytes 589828
  166.9 55.7 %all-to-all-start.3 = ((bf16[8,160,1536]{2,0,1:T(8,128)(2,1)}), bf16[8,160,1536]{2,0,1:T(8,128)(2,1)}, u32[]{:S(2)}, u32[]{:S(2)}) async-start(bf16[8,160,1536]{2,0,1:T(8,128)(2,1)} %bitcast.213), calls=%async_computation.3 | async-start | bytes 7864320 | tf_op jit(solution)/shard_map/all_to_all | solution.py:239
  226.1 53.0 %all-to-all-start.5 = ((bf16[8,160,1536]{2,0,1:T(8,128)(2,1)}), bf16[8,160,1536]{2,0,1:T(8,128)(2,1)}, u32[]{:S(2)}, u32[]{:S(2)}) async-start(bf16[8,160,1536]{2,0,1:T(8,128)(2,1)} %bitcast.212), calls=%async_computation.5 | async-start | bytes 7864320 | tf_op jit(solution)/shard_map/all_to_all | solution.py:239
  279.1 53.1 %all-to-all-start.4 = ((bf16[8,160,1536]{2,0,1:T(8,128)(2,1)}), bf16[8,160,1536]{2,0,1:T(8,128)(2,1)}, u32[]{:S(2)}, u32[]{:S(2)}) async-start(bf16[8,160,1536]{2,0,1:T(8,128)(2,1)} %bitcast.211), calls=%async_computation.4 | async-start | bytes 7864320 | tf_op jit(solution)/shard_map/all_to_all | solution.py:246
  332.2 5.3 %copy-start.23 = (f32[64,8]{0,1:T(8,128)S(1)}, f32[64,8]{0,1:T(8,128)}, u32[]{:S(2)}) copy-start(f32[64,8]{0,1:T(8,128)} %param.34) | copy-start | bytes 6148
  332.2 5.4 %copy-start.11 = (s32[64,8]{1,0:T(8,128)S(1)}, s32[64,8]{1,0:T(8,128)}, u32[]{:S(2)}) copy-start(s32[64,8]{1,0:T(8,128)} %copy-done.10) | copy-start | bytes 6148
  332.2 53.2 %all-to-all-start.6 = ((bf16[8,160,1536]{2,0,1:T(8,128)(2,1)}), bf16[8,160,1536]{2,0,1:T(8,128)(2,1)}, u32[]{:S(2)}, u32[]{:S(2)}) async-start(bf16[8,160,1536]{2,0,1:T(8,128)(2,1)} %bitcast.210), calls=%async_computation.6 | async-start | bytes 7864320 | tf_op jit(solution)/shard_map/all_to_all | solution.py:246
  392.1 2.0 copy-start.1

commit v9 on v8

--- a/solution.py
+++ b/solution.py
@@ -113,7 +113,14 @@
     part_shapes = [p.shape[1:] for p in parts_in]
     part_sizes = [p.shape[1] * p.shape[2] for p in parts_in]
     bank = jnp.concatenate([p.reshape(bank_local, -1) for p in parts_in], axis=1)
-    along_req = lax.all_gather(bank, "req", axis=0, tiled=True)
+    req_count = lax.axis_size("req")
+    along_req = lax.all_to_all(
+        jnp.broadcast_to(bank[None], (req_count,) + bank.shape),
+        "req",
+        split_axis=0,
+        concat_axis=0,
+        tiled=True,
+    ).reshape(req_count * bank_local, bank.shape[1])
     home_dev = home_of // bank_local
     home_pick = (home_dev // exp_count) * bank_local + home_of % bank_local
     mine = (home_dev % exp_count) == exp_index

time: 398 us -> 425 us (1.068); the launches traced: 396 us -> 417 us
  blocking collectives: 28.5 us -> 0 us
  waiting for transfers between devices: 202 us -> 227 us
  local copies, waits for them, and re-layouts: 57.4 us -> 66.6 us
  other arithmetic: 22.6 us -> 30.6 us
  starting transfers between devices: 40.9 us -> 46.4 us
    all_gather x1 -> x0, blocking collectives: 28.5 us -> none  [per_device(): along_req = lax.all_gather(bank, 'req', axis=0, tiled=True)]
    all_to_all x0 -> x1, waiting for transfers between devices: none -> 25.9 us  [per_device(): lax.all_to_all(jnp.broadcast_to(bank[None], (req_count,) + bank.shape), '...]
    all_to_all x0 -> x1, starting transfers between devices: none -> 8.38 us  [per_device(): lax.all_to_all(jnp.broadcast_to(bank[None], (req_count,) + bank.shape), '...]
    broadcast_in_dim x0 -> x1, other arithmetic: none -> 7.52 us  [per_device(): jnp.broadcast_to(bank[None], (req_count,) + bank.shape)]
    unnamed x77 -> x79, local copies, waits for them, and re-layouts: 5.17 us -> 11.6 us
  transfers between devices with their start and end apart: 7 -> 8, of which waited for: 7 -> 8; matrix products, arithmetic and copies ran while one was open for 15% -> 14% of each run, Pallas kernels for 0% -> 0%
where the time goes in v9:
time: 425 us; the launch traced here: 417 us
  waiting for transfers between devices  227 us (53%)
  local copies, waits for them, and re-layouts  66.6 us (16%)
  starting transfers between devices  46.4 us (11%)
  matrix products  44.1 us (10%)
  other arithmetic  30.6 us (7%)
    all_to_all x2, waiting for transfers between devices, per_device(): lax.all_to_all(copies, ('exp', 'hid'), split_axis=1, concat_axis=0, tiled...  77.6 us
    all_to_all x2, waiting for transfers between devices, per_device(): lax.all_to_all(partials, ('exp', 'hid'), split_axis=1, concat_axis=1, til...  72.6 us
    all_to_all x1, waiting for transfers between devices, per_device(): lax.all_to_all(jnp.broadcast_to(rows_pick[None], (exp_count,) + rows_pick...  37.6 us
    all_to_all x1, waiting for transfers between devices, per_device(): lax.all_to_all(jnp.broadcast_to(bank[None], (req_count,) + bank.shape), '...  25.9 us
    dot_general x2, matrix products, expert_rows(): jnp.einsum('ref,efd->red', hidden, expert_down_weight, preferred_element_...  13.7 us
    all_to_all x2, starting transfers between devices, per_device(): lax.all_to_all(copies, ('exp', 'hid'), split_axis=1, concat_axis=0, tiled...  13.1 us
    unnamed x79, local copies, waits for them, and re-layouts  11.6 us
    broadcast_in_dim x6, local copies, waits for them, and re-layouts, per_device(): jnp.broadcast_to(part_out.reshape(cap_part, exp_count, 1, local_exp, widt...  10.9 us
  transfers between devices with their start and end apart: 8, of which 8 were waited for; matrix products, arithmetic and copies ran while one was open for 14% of the time, Pallas kernels for 0%

profile of v9, /device:TPU:3, one launch (start us, length us, event | category | flops | bytes accessed | tf_op | source)
XLA Modules:
  0.0 416.7 jit_solution(8997145442299503796)
XLA Ops:
  5.5 2.2 broadcast_in_dim.179
  8.2 7.5 %reduce.9 = bf16[8,57344]{1,0:T(8,128)(2,1)S(1)} reduce(bf16[8,1,57344]{2,1,0:T(2,128)(2,1)} %broadcast_in_dim.179, bf16[]{:T(256)} %broadcast.482), dimensions={1}, to_apply=%broadcast_in_dim.179.reduce_sub_computation | reduce | bytes 1835010 | tf_op jit(solution)/shard_map/broadcast_in_dim | solution.py:118
  15.8 1.7 reshape.472
  17.5 8.4 %all-to-all-start = ((bf16[8,2,28672]{2,1,0:T(2,128)(2,1)}), bf16[8,2,28672]{2,1,0:T(2,128)(2,1)S(1)}, u32[]{:S(2)}, u32[]{:S(2)}) async-start(bf16[8,2,28672]{2,1,0:T(2,128)(2,1)} %reshape.472), calls=%async_computation | async-start | bytes 1835008 | tf_op jit(solution)/shard_map/all_to_all | solution.py:117
  26.3 25.9 %all-to-all-done = bf16[8,2,28672]{2,1,0:T(2,128)(2,1)S(1)} async-done(((bf16[8,2,28672]{2,1,0:T(2,128)(2,1)}), bf16[8,2,28672]{2,1,0:T(2,128)(2,1)S(1)}, u32[]{:S(2)}, u32[]{:S(2)}) %all-to-all-start) | async-done | bytes 917536 | tf_op jit(solution)/shard_map/all_to_all | solution.py:117
  52.2 3.3 reshape.473
  55.5 2.5 copy.155
  59.3 2.8 broadcast_in_dim.182
  62.1 5.1 %all-to-all-start.1 = ((bf16[8,4,57344]{2,1,0:T(4,128)(2,1)}), bf16[8,4,57344]{2,1,0:T(4,128)(2,1)}, u32[]{:S(2)}, u32[]{:S(2)}) async-start(bf16[8,4,57344]{2,1,0:T(4,128)(2,1)} %broadcast_in_dim.182), calls=%async_computation.1 | async-start | bytes 7340032 | tf_op jit(solution)/shard_map/all_to_all | solution.py:129
  71.4 1.4 fusion.108
  72.8 37.6 %all-to-all-done.1 = bf16[8,4,57344]{2,1,0:T(4,128)(2,1)} async-done(((bf16[8,4,57344]{2,1,0:T(4,128)(2,1)}), bf16[8,4,57344]{2,1,0:T(4,128)(2,1)}, u32[]{:S(2)}, u32[]{:S(2)}) %all-to-all-start.1) | async-done | bytes 3670048 | tf_op jit(solution)/shard_map/all_to_all | solution.py:129
  110.4 3.0 gather_fusion.1
  114.2 2.1 reshape.433
  116.3 1.3 copy.92
  117.6 2.2 fusion.106
  119.8 2.1 reshape.430
  121.9 1.3 copy.89
  123.2 1.7 fusion.110
  124.9 1.5 select_convert_fusion
  128.3 4.7 %all-to-all-start.2 = ((bf16[8,256,256]{1,2,0:T(8,128)(2,1)}), bf16[8,256,256]{1,2,0:T(8,128)(2,1)S(1)}, u32[]{:S(2)}, u32[]{:S(2)}) async-start(bf16[8,256,256]{1,2,0:T(8,128)(2,1)} %broadcast_in_dim.184), calls=%async_computation.2 | async-start | bytes 2097152 | tf_op jit(solution)/shard_map/all_to_all | solution.py:176
  133.5 1.4 slice.77
  134.9 1.5 reshape_reshape.7
  136.4 2.0 convolution_add_fusion.1
  138.4 1.9 copy.93
  140.3 1.7 subtract_convert_fusion
  142.1 5.8 %all-to-all-done.2 = bf16[8,256,256]{1,2,0:T(8,128)(2,1)S(1)} async-done(((bf16[8,256,256]{1,2,0:T(8,128)(2,1)}), bf16[8,256,256]{1,2,0:T(8,128)(2,1)S(1)}, u32[]{:S(2)}, u32[]{:S(2)}) %all-to-all-start.2) | async-done | bytes 1048608 | tf_op jit(solution)/shard_map/all_to_all | solution.py:176
  147.9 1.3 copy.90
  149.2 1.3 fusion.116
  151.7 3.0 fusion
  154.7 3.1 fusion.1
  157.9 3.6 fusion.57
  161.6 1.5 convolution_convert_fusion.3
  163.0 4.4 %all-to-all-start.3 = ((bf16[4,64,1536]{2,1,0:T(8,128)(2,1)}), bf16[4,64,1536]{2,1,0:T(8,128)(2,1)S(1)}, u32[]{:S(2)}, u32[]{:S(2)}) async-start(bf16[4,64,1536]{2,1,0:T(8,128)(2,1)} %bitcast.31), calls=%async_computation.3 | async-start | bytes 1572864 | tf_op jit(solution)/shard_map/all_to_all | solution.py:211
  169.8 7.5 %all-to-all-done.3 = bf16[4,64,1536]{2,1,0:T(8,128)(2,1)S(1)} async-done(((bf16[4,64,1536]{2,1,0:T(8,128)(2,1)}), bf16[4,64,1536]{2,1,0:T(8,128)(2,1)S(1)}, u32[]{:S(2)}, u32[]{:S(2)}) %all-to-all-start.3) | async-done | bytes 786464 | tf_op jit(solution)/shard_map/all_to_all | solution.py:211
  177.5 1.2 multiply_reduce_fusion
  178.7 1.7 convolution_convert_fusion.2
  180.4 1.4 fusion.115
  181.9 1.4 broadcast_in_dim.190
  184.0 2.2 broadcast_in_dim.191
  186.2 7.6 %all-to-all-start.4 = ((bf16[8,160,1536]{2,0,1:T(8,128)(2,1)}), bf16[8,160,1536]{2,0,1:T(8,128)(2,1)}, u32[]{:S(2)}, u32[]{:S(2)}) async-start(bf16[8,160,1536]{2,0,1:T(8,128)(2,1)} %bitcast.211), calls=%async_computation.4 | async-start | bytes 7864320 | tf_op jit(solution)/shard_map/all_to_all | solution.py:246
  193.8 1.4 broadcast_in_dim.192
  195.2 1.7 copy.105
  196.9 44.9 %all-to-all-done.4 = bf16[8,160,1536]{2,0,1:T(8,128)(2,1)} async-done(((bf16[8,160,1536]{2,0,1:T(8,128)(2,1)}), bf16[8,160,1536]{2,0,1:T(8,128)(2,1)}, u32[]{:S(2)}, u32[]{:S(2)}) %all-to-all-start.4) | async-done | bytes 3932192 | tf_op jit(solution)/shard_map/all_to_all | solution.py:246
  241.9 3.5 broadcast_in_dim.193
  245.3 5.5 %all-to-all-start.6 = ((bf16[8,160,1536]{2,0,1:T(8,128)(2,1)}), bf16[8,160,1536]{2,0,1:T(8,128)(2,1)}, u32[]{:S(2)}, u32[]{:S(2)}) async-start(bf16[8,160,1536]{2,0,1:T(8,128)(2,1)} %bitcast.210), calls=%async_computation.6 | async-start | bytes 7864320 | tf_op jit(solution)/shard_map/all_to_all | solution.py:246
  250.8 3.9 fusion.26
  254.7 6.8 %fusion.14 = bf16[32,8,5,1536]{3,1,0,2:T(8,128)(2,1)} fusion(bf16[5,128,1536]{2,1,0:T(8,128)(2,1)S(1)} %copy-done, bf16[5,1536,128]{2,1,0:T(8,128)(2,1)} %param.36, bf16[32,8,5,1536]{3,1,2,0:T(8,128)(2,1)} %bitcast.35, f32[256,5,128]{2,0,1:T(8,128)S(1)} %fusion.26), kind=kOutput, calls=%fused_computation.19 | convolution fusion | flops 1009582080 | bytes 12451840 | tf_op jit(solution)/shard_map/ref,efd->red/dot_general | solution.py:61
  261.6 4.3 %copy.103 = bf16[32,8,5,1536]{3,1,2,0:T(8,128)(2,1)} copy(bf16[32,8,5,1536]{3,1,0,2:T(8,128)(2,1)} %fusion.14) | data formatting | bytes 7864320 | tf_op jit(solution)/shard_map/reshape | solution.py:251
  265.9 32.6 %all-to-all-done.6 = bf16[8,160,1536]{2,0,1:T(8,128)(2,1)} async-done(((bf16[8,160,1536]{2,0,1:T(8,128)(2,1)}), bf16[8,160,1536]{2,0,1:T(8,128)(2,1)}, u32[]{:S(2)}, u32[]{:S(2)}) %all-to-all-start.6) | async-done | bytes 3932192 | tf_op jit(solution)/shard_map/all_to_all | solution.py:246
  298.6 5.1 %all-to-all-start.5 = ((bf16[8,160,1536]{2,0,1:T(8,128)(2,1)}), bf16[8,160,1536]{2,0,1:T(8,128)(2,1)}, u32[]{:S(2)}, u32[]{:S(2)}) async-start(bf16[8,160,1536]{2,0,1:T(8,128)(2,1)} %bitcast.209), calls=%async_computation.5 | async-start | bytes 7864320 | tf_op jit(solution)/shard_map/all_to_all | solution.py:253
  303.7 3.9 fusion.32
  307.6 6.9 %fusion.15 = bf16[32,8,5,1536]{3,1,0,2:T(8,128)(2,1)} fusion(bf16[5,128,1536]{2,1,0:T(8,128)(2,1)S(1)} %copy-done, bf16[5,1536,128]{2,1,0:T(8,128)(2,1)} %param.36, bf16[32,8,5,1536]{3,1,2,0:T(8,128)(2,1)} %bitcast.46, f32[256,5,128]{2,0,1:T(8,128)S(1)} %fusion.32), kind=kOutput, calls=%fused_computation.20 | convolution fusion | flops 1009582080 | bytes 12451840 | tf_op jit(solution)/shard_map/ref,efd->red/dot_general | solution.py:61
  314.5 4.3 %copy.107 = bf16[32,8,5,1536]{3,1,2,0:T(8,128)(2,1)} copy(bf16[32,8,5,1536]{3,1,0,2:T(8,128)(2,1)} %fusion.15) | data formatting | bytes 7864320 | tf_op jit(solution)/shard_map/reshape | solution.py:251
  318.8 32.9 %all-to-all-done.5 = bf16[8,160,1536]{2,0,1:T(8,128)(2,1)} async-done(((bf16[8,160,1536]{2,0,1:T(8,128)(2,1)}), bf16[8,160,1536]{2,0,1:T(8,128)(2,1)}, u32[]{:S(2)}, u32[]{:S(2)}) %all-to-all-start.5) | async-done | bytes 3932192 | tf_op jit(solution)/shard_map/all_to_all | solution.py:253
  351.6 5.7 %all-to-all-start.7 = ((bf16[8,160,1536]{2,0,1:T(8,128)(2,1)}), bf16[8,160,1536]{2,0,1:T(8,128)(2,1)}, u32[]{:S(2)}, u32[]{:S(2)}) async-start(bf16[8,160,1536]{2,0,1:T(8,128)(2,1)} %bitcast.208), calls=%async_computation.7 | async-start | bytes 7864320 | tf_op jit(solution)/shard_map/all_to_all | solution.py:253
  358.6 4.0 reduce_sum.130
  362.6 1.6 copy.104
  364.1 1.2 reshape.443
  365.3 39.7 %all-to-all-done.7 = bf16[8,160,1536]{2,0,1:T(8,128)(2,1)} async-done(((bf16[8,160,1536]{2,0,1:T(8,128)(2,1)}), bf16[8,160,1536]{2,0,1:T(8,128)(2,1)}, u32[]{:S(2)}, u32[]{:S(2)}) %all-to-all-start.7) | async-done | bytes 3932192 | tf_op jit(solution)/shard_map/all_to_all | solution.py:253
  405.1 4.0 reduce_sum.131
  409.1 1.6 copy.108
  410.6 1.2 reshape.448
  411.9 2.0 fusion.85
  413.9 2.3 fusion.20
  (130 shorter events, 20.1 us)
Async XLA Ops:
  0.6 254.1 %copy-start = (bf16[5,128,1536]{2,1,0:T(8,128)(2,1)S(1)}, bf16[5,128,1536]{2,1,0:T(8,128)(2,1)}, u32[]{:S(2)}) copy-start(bf16[5,128,1536]{2,1,0:T(8,128)(2,1)} %param.37) | copy-start | bytes 5898244
  15.8 10.1 %copy-start.24 = (s32[8,4]{0,1:T(4,128)S(1)}, s32[8,4]{0,1:T(4,128)}, u32[]{:S(2)}) copy-start(s32[8,4]{0,1:T(4,128)} %param.30) | copy-start | bytes 388
  15.8 10.3 %copy-start.32 = (s32[64]{0:T(128)S(1)}, s32[64]{0:T(128)}, u32[]{:S(2)}) copy-start(s32[64]{0:T(128)} %param.31) | copy-start | bytes 772
  17.5 34.7 %all-to-all-start = ((bf16[8,2,28672]{2,1,0:T(2,128)(2,1)}), bf16[8,2,28672]{2,1,0:T(2,128)(2,1)S(1)}, u32[]{:S(2)}, u32[]{:S(2)}) async-start(bf16[8,2,28672]{2,1,0:T(2,128)(2,1)} %reshape.472), calls=%async_computation | async-start | bytes 1835008 | tf_op jit(solution)/shard_map/all_to_all | solution.py:117
  62.1 5.1 %copy-start.33 = (s32[1,4]{1,0:T(1,128)S(1)}, s32[1,4]{1,0:T(1,128)}, u32[]{:S(2)}) copy-start(s32[1,4]{1,0:T(1,128)} %param.29) | copy-start | bytes 52
  62.1 5.3 %copy-start.22 = (s32[64,8]{0,1:T(8,128)S(1)}, s32[64,8]{0,1:T(8,128)}, u32[]{:S(2)}) copy-start(s32[64,8]{0,1:T(8,128)} %param.33) | copy-start | bytes 6148
  62.1 7.0 %copy-start.4 = (bf16[256,1536]{1,0:T(8,128)(2,1)S(1)}, bf16[256,1536]{1,0:T(8,128)(2,1)}, u32[]{:S(2)}) copy-start(bf16[256,1536]{1,0:T(8,128)(2,1)} %param.19) | copy-start | bytes 2359300
  62.1 7.4 %copy-start.28 = (bf16[1536,128]{1,0:T(8,128)(2,1)S(1)}, bf16[1536,128]{1,0:T(8,128)(2,1)}, u32[]{:S(2)}) copy-start(bf16[1536,128]{1,0:T(8,128)(2,1)} %param.22) | copy-start | bytes 1179652
  62.1 7.4 %copy-start.30 = (f32[1536]{0:T(1024)S(1)}, f32[1536]{0:T(1024)}, u32[]{:S(2)}) copy-start(f32[1536]{0:T(1024)} %param.20) | copy-start | bytes 18436
  62.1 48.3 %all-to-all-start.1 = ((bf16[8,4,57344]{2,1,0:T(4,128)(2,1)}), bf16[8,4,57344]{2,1,0:T(4,128)(2,1)}, u32[]{:S(2)}, u32[]{:S(2)}) async-start(bf16[8,4,57344]{2,1,0:T(4,128)(2,1)} %broadcast_in_dim.182), calls=%async_computation.1 | async-start | bytes 7340032 | tf_op jit(solution)/shard_map/all_to_all | solution.py:129
  67.5 5.3 %copy-start.7 = (s32[64,8]{1,0:T(8,128)}, s32[64,8]{1,0:T(8,128)S(1)}, u32[]{:S(2)}) copy-start(s32[64,8]{1,0:T(8,128)S(1)} %copy.96) | copy-start | bytes 6148
  68.1 3.3 copy-start.27
  68.2 4.6 %copy-start.20 = (s32[256]{0:T(256)}, s32[256]{0:T(256)S(1)}, u32[]{:S(2)}) copy-start(s32[256]{0:T(256)S(1)} %iota_add_fusion) | copy-start | bytes 3076
  68.9 1.8 copy-start.16
  69.3 48.3 %copy-start.25 = (f32[256]{0:T(256)}, f32[256]{0:T(256)S(1)}, u32[]{:S(2)}) copy-start(f32[256]{0:T(256)S(1)} %add_rsqrt_fusion) | copy-start | bytes 3076
  69.5 0.6 copy-start.12
  69.5 0.6 copy-start.13
  113.3 0.9 copy-start.2
  121.9 3.0 slice-start
  123.2 3.4 copy-start.5
  123.2 3.4 copy-start.26
  123.2 3.5 copy-start.29
  123.2 3.5 copy-start.31
  123.2 4.0 copy-start.14
  127.1 5.8 %copy-start.15 = (s32[2048]{0:T(1024)S(1)}, s32[2048]{0:T(1024)}, u32[]{:S(2)}) copy-start(s32[2048]{0:T(1024)} %convert_reduce_fusion) | copy-start | bytes 24580
  127.1 5.8 %copy-start.17 = (s32[256]{0:T(256)S(1)}, s32[256]{0:T(256)}, u32[]{:S(2)}) copy-start(s32[256]{0:T(256)} %copy-done.16) | copy-start | bytes 3076
  127.2 5.8 %copy-start.21 = (s32[256]{0:T(256)S(1)}, s32[256]{0:T(256)}, u32[]{:S(2)}) copy-start(s32[256]{0:T(256)} %copy-done.20) | copy-start | bytes 3076
  128.3 19.6 %all-to-all-start.2 = ((bf16[8,256,256]{1,2,0:T(8,128)(2,1)}), bf16[8,256,256]{1,2,0:T(8,128)(2,1)S(1)}, u32[]{:S(2)}, u32[]{:S(2)}) async-start(bf16[8,256,256]{1,2,0:T(8,128)(2,1)} %broadcast_in_dim.184), calls=%async_computation.2 | async-start | bytes 2097152 | tf_op jit(solution)/shard_map/all_to_all | solution.py:176
  154.7 3.2 copy-start.9
  157.9 3.7 copy-start.6
  161.5 5.9 %copy-start.19 = (s32[4,128]{1,0:T(4,128)S(1)}, s32[4,128]{1,0:T(4,128)}, u32[]{:S(2)}) copy-start(s32[4,128]{1,0:T(4,128)} %eq.130) | copy-start | bytes 6148
  161.5 5.9 %copy-start.8 = (s32[64,8]{1,0:T(8,128)S(1)}, s32[64,8]{1,0:T(8,128)}, u32[]{:S(2)}) copy-start(s32[64,8]{1,0:T(8,128)} %copy-done.7) | copy-start | bytes 6148
  163.0 15.7 %copy-start.18 = (f32[1536]{0:T(1024)S(1)}, f32[1536]{0:T(1024)}, u32[]{:S(2)}) copy-start(f32[1536]{0:T(1024)} %param.32) | copy-start | bytes 18436
  163.0 14.4 %all-to-all-start.3 = ((bf16[4,64,1536]{2,1,0:T(8,128)(2,1)}), bf16[4,64,1536]{2,1,0:T(8,128)(2,1)S(1)}, u32[]{:S(2)}, u32[]{:S(2)}) async-start(bf16[4,64,1536]{2,1,0:T(8,128)(2,1)} %bitcast.31), calls=%async_computation.3 | async-start | bytes 1572864 | tf_op jit(solution)/shard_map/all_to_all | solution.py:211
  169.2 0.6 copy-start.10
  177.5 4.3 %copy-start.3 = (bf16[64,1536]{1,0:T(8,128)(2,1)}, bf16[64,1536]{1,0:T(8,128)(2,1)S(1)}, u32[]{:S(2)}) copy-start(bf16[64,1536]{1,0:T(8,128)(2,1)S(1)} %reduce_sum.126) | copy-start | bytes 589828
  186.2 55.7 %all-to-all-start.4 = ((bf16[8,160,1536]{2,0,1:T(8,128)(2,1)}), bf16[8,160,1536]{2,0,1:T(8,128)(2,1)}, u32[]{:S(2)}, u32[]{:S(2)}) async-start(bf16[8,160,1536]{2,0,1:T(8,128)(2,1)} %bitcast.211), calls=%async_computation.4 | async-start | bytes 7864320 | tf_op jit(solution)/shard_map/all_to_all | solution.py:246
  245.3 53.2 %all-to-all-start.6 = ((bf16[8,160,1536]{2,0,1:T(8,128)(2,1)}), bf16[8,160,1536]{2,0,1:T(8,128)(2,1)}, u32[]{:S(2)}, u32[]{:S(2)}) async-start(bf16[8,160,1536]{2,0,1:T(8,128)(2,1)} %bitcast.210), calls=%async_computation.6 | async-start | bytes 7864320 | tf_op jit(solution)/shard_map/all_to_all | solution.py:246
  298.6 53.1 %all-to-all-start.5 = ((bf16[8,160,1536]{2,0,1:T(8,128)(2,1)}), bf16[8,160,1536]{2,0,1:T(8,128)(2,1)}, u32[]{:S(2)}, u32[]{:S(2)}) async-start(bf16[8,160,1536]{2,0,1:T(8,128)(2,1)} %bitcast.209), calls=%async_computation.5 | async-start | bytes 7864320 | tf_op jit(solution)/shard_map/all_to_all | solution.py:253
  351.6 5.7 %copy-start.23 = (f32[64,8]{0,1:T(8,128)S(1)}, f32[64,8]{0,1:T(8,128)}, u32[]{:S(2)}) copy-start(f32[64,8]{0,1:T(8,128)} %param.34) | copy-start | bytes 6148
  351.6 5.8 %copy-start.11 = (s32[64,8]{1,0:T(8,128)S(1)}, s32[64,8]{1,0:T(8,128)}, u32[]{:S(2)}) copy-start(s32[64,8]{1,0:T(8,128)} %copy-done.10) | copy-start | bytes 6148
  351.6 53.5 %all-to-all-start.7 = ((bf16[8,160,1536]{2,0,1:T(8,128)(2,1)}), bf16[8,160,1536]{2,0,1:T(8,128)(2,1)}, u32[]{:S(2)}, u32[]{:S(2)}) async-start(bf16[8,160,1536]{2,0,1:T(8,128)(2,1)} %bitcast.208), calls=%async_computation.7 | async-start | bytes 7864320 | tf_op jit(solution)/shard_map/all_to_all | solution.py:253
  411.9 2.0 copy-start.1

commit v10 on v6

--- a/solution.py
+++ b/solution.py
@@ -165,8 +165,17 @@
     ) + low_rank_term(va_sel, vb_sel, kv_cols, hid_index * kv_cols)
     values_own = values_own.astype(jnp.bfloat16)
     running_max = jnp.full((kv_local, group_share, query_rows), neg_large, jnp.float32)
-    key_piece = lax.all_gather(keys_own, "exp", axis=0, tiled=True)
-    value_piece = lax.all_gather(values_own, "exp", axis=0, tiled=True)
+    def exchange(own):
+        return lax.all_to_all(
+            jnp.broadcast_to(own[None], (exp_count,) + own.shape),
+            "exp",
+            split_axis=0,
+            concat_axis=0,
+            tiled=True,
+        ).reshape(exp_count * query_rows, own.shape[1])
+
+    key_piece = exchange(keys_own)
+    value_piece = exchange(values_own)
     piece_len = key_piece.shape[0]
     key_ids = jnp.arange(piece_len, dtype=jnp.int32)
     key_request = request_of(key_ids, group_len)

time: 416 us -> 413 us (level)
  blocking collectives: 92.8 us -> 28 us
  waiting for transfers between devices: 159 us -> 198 us
  starting transfers between devices: 36.4 us -> 47.9 us
  matrix products: 47.9 us -> 53.2 us
    all_gather x2 -> x0, blocking collectives: 64.3 us -> none  [the longest x1 51 us: per_device(): key_piece = lax.all_gather(keys_own, 'exp', axis=0, tiled=True)]
    all_to_all x1, waiting for transfers between devices: 0.01 us -> 37 us  [per_device(): lax.all_to_all(jnp.broadcast_to(rows_pick[None], (exp_count,) + rows_pick...]
    all_to_all x0 -> x2, starting transfers between devices: none -> 9.71 us  [exchange(): lax.all_to_all(jnp.broadcast_to(own[None], (exp_count,) + own.shape), 'ex...]
  transfers between devices with their start and end apart: 6 -> 8, of which waited for: 5 -> 7; matrix products, arithmetic and copies ran while one was open for 12% -> 16% of each run, Pallas kernels for 0% -> 0%
where the time goes in v10:
time: 413 us; the launch traced here: 407 us
  waiting for transfers between devices  198 us (48%)
  matrix products  53.2 us (13%)
  local copies, waits for them, and re-layouts  52.1 us (13%)
  starting transfers between devices  47.9 us (12%)
  blocking collectives  28 us (7%)
  other arithmetic  26.2 us (6%)
    all_to_all x2, waiting for transfers between devices, per_device(): lax.all_to_all(copies, ('exp', 'hid'), split_axis=1, concat_axis=0, tiled...  77.6 us
    all_to_all x2, waiting for transfers between devices, per_device(): lax.all_to_all(partials, ('exp', 'hid'), split_axis=1, concat_axis=1, til...  72.6 us
    all_to_all x1, waiting for transfers between devices, per_device(): lax.all_to_all(jnp.broadcast_to(rows_pick[None], (exp_count,) + rows_pick...  37 us
    all_gather x1, blocking collectives, per_device(): along_req = lax.all_gather(bank, 'req', axis=0, tiled=True)  28 us
    dot_general x2, matrix products, expert_rows(): jnp.einsum('ref,efd->red', hidden, expert_down_weight, preferred_element_...  13.7 us
    all_to_all x2, starting transfers between devices, per_device(): lax.all_to_all(copies, ('exp', 'hid'), split_axis=1, concat_axis=0, tiled...  13 us
    broadcast_in_dim x6, local copies, waits for them, and re-layouts, per_device(): jnp.broadcast_to(part_out.reshape(cap_part, exp_count, 1, local_exp, widt...  10.9 us
    all_to_all x2, starting transfers between devices, per_device(): lax.all_to_all(partials, ('exp', 'hid'), split_axis=1, concat_axis=1, til...  10.8 us
  transfers between devices with their start and end apart: 8, of which 7 were waited for; matrix products, arithmetic and copies ran while one was open for 16% of the time, Pallas kernels for 0%

profile of v10, /device:TPU:3, one launch (start us, length us, event | category | flops | bytes accessed | tf_op | source)
XLA Modules:
  0.0 406.5 jit_solution(9743208635775034771)
XLA Ops:
  0.7 1.5 fusion.22
  4.1 1.8 fusion.115
  6.8 5.1 %all-to-all-start = ((bf16[8,256,128]{1,2,0:T(8,128)(2,1)}), bf16[8,256,128]{1,2,0:T(8,128)(2,1)S(1)}, u32[]{:S(2)}, u32[]{:S(2)}) async-start(bf16[8,256,128]{1,2,0:T(8,128)(2,1)} %broadcast_in_dim.170), calls=%async_computation | async-start | bytes 1048576 | tf_op jit(solution)/shard_map/all_to_all | solution.py:169
  15.1 28.0 %all-gather = bf16[8,1,57344]{2,1,0:T(2,128)(2,1)S(1)} all-gather(bf16[1,1,57344]{2,1,0:T(2,128)(2,1)S(1)} %maximum_bitcast_fusion), channel_id=1, replica_groups=mesh['req'=8,'exp'=8,'hid'=4] {'req'}, dimensions={0}, use_global_device_ids=true | all-gather | bytes 1032192 | tf_op jit(solution)/shard_map/all_gather | solution.py:116
  43.1 1.0 copy.160
  44.1 1.7 gather_fusion
  45.9 1.3 select_select_fusion
  47.2 2.8 broadcast_in_dim.178
  50.0 10.0 %all-to-all-start.1 = ((bf16[8,4,57344]{2,1,0:T(4,128)(2,1)}), bf16[8,4,57344]{2,1,0:T(4,128)(2,1)}, u32[]{:S(2)}, u32[]{:S(2)}) async-start(bf16[8,4,57344]{2,1,0:T(4,128)(2,1)} %broadcast_in_dim.178), calls=%async_computation.1 | async-start | bytes 7340032 | tf_op jit(solution)/shard_map/all_to_all | solution.py:122
  60.9 2.6 fusion.113
  63.5 1.2 fusion.21
  65.0 1.1 reshape.451
  66.1 37.0 %all-to-all-done.1 = bf16[8,4,57344]{2,1,0:T(4,128)(2,1)} async-done(((bf16[8,4,57344]{2,1,0:T(4,128)(2,1)}), bf16[8,4,57344]{2,1,0:T(4,128)(2,1)}, u32[]{:S(2)}, u32[]{:S(2)}) %all-to-all-start.1) | async-done | bytes 3670048 | tf_op jit(solution)/shard_map/all_to_all | solution.py:122
  103.1 2.9 gather_fusion.1
  106.0 0.9 fusion.118
  107.5 2.1 reshape.417
  109.6 1.3 copy.95
  110.9 2.2 fusion.111
  113.1 2.1 reshape.419
  115.2 1.3 copy.97
  116.5 1.7 fusion.108
  119.0 0.9 select_convert_fusion
  120.4 7.7 %fusion = (f32[2,3,256]{2,1,0:T(4,128)S(1)}, f32[2,2048,256,3]{2,1,3,0:T(8,128)}) fusion(pred[256,2048]{0,1:T(8,128)(4,1)S(1)} %copy-done.2, bf16[256,2,3,32]{0,3,2,1:T(8,128)(2,1)S(1)} %bitcast.223, bf16[256,2,3,32]{0,3,2,1:T(8,128)(2,1)S(1)} %bitcast.222, bf16[2048,2,64,1]{0,2,1,3:T(8,128)(2,1)} %reshape.451), kind=kOutput, calls=%fused_computation.4 | convolution fusion | flops 412482048 | bytes 13834240 | tf_op jit(solution)/shard_map/qkgh,nkh->kgqn/dot_general | solution.py:186
  128.4 1.4 fusion.53
  129.9 0.9 broadcast_in_dim.183
  130.8 4.6 %all-to-all-start.2 = ((bf16[8,256,128]{1,2,0:T(8,128)(2,1)}), bf16[8,256,128]{1,2,0:T(8,128)(2,1)S(1)}, u32[]{:S(2)}, u32[]{:S(2)}) async-start(bf16[8,256,128]{1,2,0:T(8,128)(2,1)} %broadcast_in_dim.183), calls=%async_computation.2 | async-start | bytes 1048576 | tf_op jit(solution)/shard_map/all_to_all | solution.py:169
  135.4 6.5 %fusion.1 = f32[2,3,256]{2,1,0:T(4,128)S(1)} fusion(f32[2,2048,256,3]{2,1,3,0:T(8,128)} %get-tuple-element.19, f32[2,3,256]{2,1,0:T(4,128)S(1)} %broadcast_maximum_fusion, pred[256,2048]{0,1:T(8,128)(4,1)S(1)} %copy-done.2), kind=kLoop, calls=%fused_computation.5 | loop fusion | flops 15727104 | bytes 13119488 | tf_op jit(solution)/shard_map/reduce_sum | solution.py:192
  141.9 2.8 all-to-all-done.2
  145.3 6.4 %fusion.57 = bf16[256,2,3,64]{0,3,2,1:T(8,128)(2,1)S(1)} fusion(f32[2,2048,256,3]{2,1,3,0:T(8,128)} %get-tuple-element.19, f32[2,3,256]{2,1,0:T(4,128)S(1)} %broadcast_maximum_fusion, pred[256,2048]{0,1:T(8,128)(4,1)S(1)} %copy-done.2, bf16[2048,2,64,1]{0,2,1,3:T(8,128)(2,1)S(1)} %reshape.454, f32[256,2,3]{0,2,1:T(4,128)S(1)} %bitcast.227), kind=kOutput, calls=%fused_computation.53 | convolution fusion | flops 418578432 | bytes 13840384 | tf_op jit(solution)/shard_map/kgqn,nkh->kgqh/dot_general | solution.py:193
  151.7 1.5 convolution_convert_fusion.3
  153.1 4.4 %all-to-all-start.3 = ((bf16[4,64,1536]{2,1,0:T(8,128)(2,1)}), bf16[4,64,1536]{2,1,0:T(8,128)(2,1)S(1)}, u32[]{:S(2)}, u32[]{:S(2)}) async-start(bf16[4,64,1536]{2,1,0:T(8,128)(2,1)} %bitcast.27), calls=%async_computation.3 | async-start | bytes 1572864 | tf_op jit(solution)/shard_map/all_to_all | solution.py:205
  157.6 1.2 reduce-window.11
  159.9 7.5 %all-to-all-done.3 = bf16[4,64,1536]{2,1,0:T(8,128)(2,1)S(1)} async-done(((bf16[4,64,1536]{2,1,0:T(8,128)(2,1)}), bf16[4,64,1536]{2,1,0:T(8,128)(2,1)S(1)}, u32[]{:S(2)}, u32[]{:S(2)}) %all-to-all-start.3) | async-done | bytes 786464 | tf_op jit(solution)/shard_map/all_to_all | solution.py:205
  167.6 1.2 multiply_reduce_fusion
  168.8 1.7 convolution_convert_fusion.2
  170.5 1.5 fusion.117
  172.0 1.4 broadcast_in_dim.188
  174.1 2.2 broadcast_in_dim.189
  176.3 7.6 %all-to-all-start.6 = ((bf16[8,160,1536]{2,0,1:T(8,128)(2,1)}), bf16[8,160,1536]{2,0,1:T(8,128)(2,1)}, u32[]{:S(2)}, u32[]{:S(2)}) async-start(bf16[8,160,1536]{2,0,1:T(8,128)(2,1)} %bitcast.212), calls=%async_computation.6 | async-start | bytes 7864320 | tf_op jit(solution)/shard_map/all_to_all | solution.py:240
  183.9 1.4 broadcast_in_dim.186
  185.4 1.7 copy.106
  187.1 44.9 %all-to-all-done.6 = bf16[8,160,1536]{2,0,1:T(8,128)(2,1)} async-done(((bf16[8,160,1536]{2,0,1:T(8,128)(2,1)}), bf16[8,160,1536]{2,0,1:T(8,128)(2,1)}, u32[]{:S(2)}, u32[]{:S(2)}) %all-to-all-start.6) | async-done | bytes 3932192 | tf_op jit(solution)/shard_map/all_to_all | solution.py:240
  232.0 3.5 broadcast_in_dim.187
  235.5 5.4 %all-to-all-start.4 = ((bf16[8,160,1536]{2,0,1:T(8,128)(2,1)}), bf16[8,160,1536]{2,0,1:T(8,128)(2,1)}, u32[]{:S(2)}, u32[]{:S(2)}) async-start(bf16[8,160,1536]{2,0,1:T(8,128)(2,1)} %bitcast.211), calls=%async_computation.4 | async-start | bytes 7864320 | tf_op jit(solution)/shard_map/all_to_all | solution.py:240
  240.9 3.9 fusion.32
  244.8 6.8 %fusion.15 = bf16[32,8,5,1536]{3,1,0,2:T(8,128)(2,1)} fusion(bf16[5,128,1536]{2,1,0:T(8,128)(2,1)S(1)} %copy-done, bf16[5,1536,128]{2,1,0:T(8,128)(2,1)} %param.36, bf16[32,8,5,1536]{3,1,2,0:T(8,128)(2,1)} %bitcast.42, f32[256,5,128]{2,0,1:T(8,128)S(1)} %fusion.32), kind=kOutput, calls=%fused_computation.20 | convolution fusion | flops 1009582080 | bytes 12451840 | tf_op jit(solution)/shard_map/ref,efd->red/dot_general | solution.py:61
  251.7 4.3 %copy.112 = bf16[32,8,5,1536]{3,1,2,0:T(8,128)(2,1)} copy(bf16[32,8,5,1536]{3,1,0,2:T(8,128)(2,1)} %fusion.15) | data formatting | bytes 7864320 | tf_op jit(solution)/shard_map/reshape | solution.py:245
  256.0 32.6 %all-to-all-done.4 = bf16[8,160,1536]{2,0,1:T(8,128)(2,1)} async-done(((bf16[8,160,1536]{2,0,1:T(8,128)(2,1)}), bf16[8,160,1536]{2,0,1:T(8,128)(2,1)}, u32[]{:S(2)}, u32[]{:S(2)}) %all-to-all-start.4) | async-done | bytes 3932192 | tf_op jit(solution)/shard_map/all_to_all | solution.py:240
  288.7 5.1 %all-to-all-start.7 = ((bf16[8,160,1536]{2,0,1:T(8,128)(2,1)}), bf16[8,160,1536]{2,0,1:T(8,128)(2,1)}, u32[]{:S(2)}, u32[]{:S(2)}) async-start(bf16[8,160,1536]{2,0,1:T(8,128)(2,1)} %bitcast.210), calls=%async_computation.7 | async-start | bytes 7864320 | tf_op jit(solution)/shard_map/all_to_all | solution.py:247
  293.8 3.9 fusion.26
  297.7 6.9 %fusion.14 = bf16[32,8,5,1536]{3,1,0,2:T(8,128)(2,1)} fusion(bf16[5,128,1536]{2,1,0:T(8,128)(2,1)S(1)} %copy-done, bf16[5,1536,128]{2,1,0:T(8,128)(2,1)} %param.36, bf16[32,8,5,1536]{3,1,2,0:T(8,128)(2,1)} %bitcast.31, f32[256,5,128]{2,0,1:T(8,128)S(1)} %fusion.26), kind=kOutput, calls=%fused_computation.19 | convolution fusion | flops 1009582080 | bytes 12451840 | tf_op jit(solution)/shard_map/ref,efd->red/dot_general | solution.py:61
  304.6 4.3 %copy.108 = bf16[32,8,5,1536]{3,1,2,0:T(8,128)(2,1)} copy(bf16[32,8,5,1536]{3,1,0,2:T(8,128)(2,1)} %fusion.14) | data formatting | bytes 7864320 | tf_op jit(solution)/shard_map/reshape | solution.py:245
  308.9 32.9 %all-to-all-done.7 = bf16[8,160,1536]{2,0,1:T(8,128)(2,1)} async-done(((bf16[8,160,1536]{2,0,1:T(8,128)(2,1)}), bf16[8,160,1536]{2,0,1:T(8,128)(2,1)}, u32[]{:S(2)}, u32[]{:S(2)}) %all-to-all-start.7) | async-done | bytes 3932192 | tf_op jit(solution)/shard_map/all_to_all | solution.py:247
  341.8 5.7 %all-to-all-start.5 = ((bf16[8,160,1536]{2,0,1:T(8,128)(2,1)}), bf16[8,160,1536]{2,0,1:T(8,128)(2,1)}, u32[]{:S(2)}, u32[]{:S(2)}) async-start(bf16[8,160,1536]{2,0,1:T(8,128)(2,1)} %bitcast.209), calls=%async_computation.5 | async-start | bytes 7864320 | tf_op jit(solution)/shard_map/all_to_all | solution.py:247
  347.5 1.1 select_reduce_fusion
  348.7 4.0 reduce_sum.131
  352.6 1.6 copy.113
  354.2 1.2 reshape.432
  355.4 39.7 %all-to-all-done.5 = bf16[8,160,1536]{2,0,1:T(8,128)(2,1)} async-done(((bf16[8,160,1536]{2,0,1:T(8,128)(2,1)}), bf16[8,160,1536]{2,0,1:T(8,128)(2,1)}, u32[]{:S(2)}, u32[]{:S(2)}) %all-to-all-start.5) | async-done | bytes 3932192 | tf_op jit(solution)/shard_map/all_to_all | solution.py:247
  395.2 4.0 reduce_sum.130
  399.2 1.6 copy.109
  400.7 1.2 reshape.427
  401.9 2.0 fusion.87
  404.0 2.3 fusion.20
  (113 shorter events, 11.9 us)
Async XLA Ops:
  0.6 244.2 %copy-start = (bf16[5,128,1536]{2,1,0:T(8,128)(2,1)S(1)}, bf16[5,128,1536]{2,1,0:T(8,128)(2,1)}, u32[]{:S(2)}) copy-start(bf16[5,128,1536]{2,1,0:T(8,128)(2,1)} %param.37) | copy-start | bytes 5898244
  2.2 9.8 %copy-start.23 = (s32[8,4]{0,1:T(4,128)S(1)}, s32[8,4]{0,1:T(4,128)}, u32[]{:S(2)}) copy-start(s32[8,4]{0,1:T(4,128)} %param.30) | copy-start | bytes 388
  2.2 9.9 %copy-start.26 = (s32[64]{0:T(128)S(1)}, s32[64]{0:T(128)}, u32[]{:S(2)}) copy-start(s32[64]{0:T(128)} %param.31) | copy-start | bytes 772
  2.2 11.6 %copy-start.17 = (bf16[1,1536,16]{1,2,0:T(8,128)(2,1)S(1)}, bf16[1,1536,16]{1,2,0:T(8,128)(2,1)}, u32[]{:S(2)}) copy-start(bf16[1,1536,16]{1,2,0:T(8,128)(2,1)} %param.25) | copy-start | bytes 147460
  4.1 1.8 copy-start.13
  4.1 1.8 copy-start.15
  4.1 10.2 %copy-start.18 = (bf16[1,1536,16]{1,2,0:T(8,128)(2,1)S(1)}, bf16[1,1536,16]{1,2,0:T(8,128)(2,1)}, u32[]{:S(2)}) copy-start(bf16[1,1536,16]{1,2,0:T(8,128)(2,1)} %param.27) | copy-start | bytes 147460
  6.8 40.4 %all-to-all-start = ((bf16[8,256,128]{1,2,0:T(8,128)(2,1)}), bf16[8,256,128]{1,2,0:T(8,128)(2,1)S(1)}, u32[]{:S(2)}, u32[]{:S(2)}) async-start(bf16[8,256,128]{1,2,0:T(8,128)(2,1)} %broadcast_in_dim.170), calls=%async_computation | async-start | bytes 1048576 | tf_op jit(solution)/shard_map/all_to_all | solution.py:169
  50.0 10.0 %copy-start.21 = (s32[64,8]{0,1:T(8,128)S(1)}, s32[64,8]{0,1:T(8,128)}, u32[]{:S(2)}) copy-start(s32[64,8]{0,1:T(8,128)} %param.33) | copy-start | bytes 6148
  50.0 10.9 %copy-start.5 = (bf16[256,1536]{1,0:T(8,128)(2,1)S(1)}, bf16[256,1536]{1,0:T(8,128)(2,1)}, u32[]{:S(2)}) copy-start(bf16[256,1536]{1,0:T(8,128)(2,1)} %param.19) | copy-start | bytes 2359300
  50.0 10.9 %copy-start.24 = (f32[1536]{0:T(1024)S(1)}, f32[1536]{0:T(1024)}, u32[]{:S(2)}) copy-start(f32[1536]{0:T(1024)} %param.20) | copy-start | bytes 18436
  50.0 53.1 %all-to-all-start.1 = ((bf16[8,4,57344]{2,1,0:T(4,128)(2,1)}), bf16[8,4,57344]{2,1,0:T(4,128)(2,1)}, u32[]{:S(2)}, u32[]{:S(2)}) async-start(bf16[8,4,57344]{2,1,0:T(4,128)(2,1)} %broadcast_in_dim.178), calls=%async_computation.1 | async-start | bytes 7340032 | tf_op jit(solution)/shard_map/all_to_all | solution.py:122
  60.1 4.9 %copy-start.8 = (s32[64,8]{1,0:T(8,128)}, s32[64,8]{1,0:T(8,128)S(1)}, u32[]{:S(2)}) copy-start(s32[64,8]{1,0:T(8,128)S(1)} %copy.101) | copy-start | bytes 6148
  106.0 1.5 copy-start.3
  116.5 3.4 copy-start.10
  116.5 3.8 copy-start.14
  116.5 3.8 copy-start.16
  116.5 3.9 copy-start.2
  120.4 7.8 %slice-start = ((bf16[4,57344]{1,0:T(4,128)(2,1)}), bf16[4,2048]{1,0:T(4,128)(2,1)S(1)}, s32[]{:S(2)}) async-start(bf16[4,57344]{1,0:T(4,128)(2,1)} %copy-done.3), calls=%async_computation.8 | async-start | bytes 32768 | tf_op jit(solution)/shard_map/slice | solution.py:133
  120.4 8.0 %copy-start.6 = (bf16[256,1536]{1,0:T(8,128)(2,1)S(1)}, bf16[256,1536]{1,0:T(8,128)(2,1)}, u32[]{:S(2)}) copy-start(bf16[256,1536]{1,0:T(8,128)(2,1)} %param.19) | copy-start | bytes 2359300
  120.4 8.0 %copy-start.25 = (f32[1536]{0:T(1024)S(1)}, f32[1536]{0:T(1024)}, u32[]{:S(2)}) copy-start(f32[1536]{0:T(1024)} %param.20) | copy-start | bytes 18436
  130.8 13.9 %all-to-all-start.2 = ((bf16[8,256,128]{1,2,0:T(8,128)(2,1)}), bf16[8,256,128]{1,2,0:T(8,128)(2,1)S(1)}, u32[]{:S(2)}, u32[]{:S(2)}) async-start(bf16[8,256,128]{1,2,0:T(8,128)(2,1)} %broadcast_in_dim.183), calls=%async_computation.2 | async-start | bytes 1048576 | tf_op jit(solution)/shard_map/all_to_all | solution.py:169
  145.2 6.4 %copy-start.7 = (bf16[384,1536]{1,0:T(8,128)(2,1)S(1)}, bf16[384,1536]{1,0:T(8,128)(2,1)}, u32[]{:S(2)}) copy-start(bf16[384,1536]{1,0:T(8,128)(2,1)} %param.24) | copy-start | bytes 3538948
  151.6 5.9 %copy-start.20 = (s32[4,128]{1,0:T(4,128)S(1)}, s32[4,128]{1,0:T(4,128)}, u32[]{:S(2)}) copy-start(s32[4,128]{1,0:T(4,128)} %eq.130) | copy-start | bytes 6148
  151.6 5.9 %copy-start.9 = (s32[64,8]{1,0:T(8,128)S(1)}, s32[64,8]{1,0:T(8,128)}, u32[]{:S(2)}) copy-start(s32[64,8]{1,0:T(8,128)} %copy-done.8) | copy-start | bytes 6148
  153.1 15.7 %copy-start.19 = (f32[1536]{0:T(1024)S(1)}, f32[1536]{0:T(1024)}, u32[]{:S(2)}) copy-start(f32[1536]{0:T(1024)} %param.32) | copy-start | bytes 18436
  153.1 14.4 %all-to-all-start.3 = ((bf16[4,64,1536]{2,1,0:T(8,128)(2,1)}), bf16[4,64,1536]{2,1,0:T(8,128)(2,1)S(1)}, u32[]{:S(2)}, u32[]{:S(2)}) async-start(bf16[4,64,1536]{2,1,0:T(8,128)(2,1)} %bitcast.27), calls=%async_computation.3 | async-start | bytes 1572864 | tf_op jit(solution)/shard_map/all_to_all | solution.py:205
  159.3 0.6 copy-start.11
  167.6 4.4 %copy-start.4 = (bf16[64,1536]{1,0:T(8,128)(2,1)}, bf16[64,1536]{1,0:T(8,128)(2,1)S(1)}, u32[]{:S(2)}) copy-start(bf16[64,1536]{1,0:T(8,128)(2,1)S(1)} %reduce_sum.126) | copy-start | bytes 589828
  176.3 55.7 %all-to-all-start.6 = ((bf16[8,160,1536]{2,0,1:T(8,128)(2,1)}), bf16[8,160,1536]{2,0,1:T(8,128)(2,1)}, u32[]{:S(2)}, u32[]{:S(2)}) async-start(bf16[8,160,1536]{2,0,1:T(8,128)(2,1)} %bitcast.212), calls=%async_computation.6 | async-start | bytes 7864320 | tf_op jit(solution)/shard_map/all_to_all | solution.py:240
  235.5 53.2 %all-to-all-start.4 = ((bf16[8,160,1536]{2,0,1:T(8,128)(2,1)}), bf16[8,160,1536]{2,0,1:T(8,128)(2,1)}, u32[]{:S(2)}, u32[]{:S(2)}) async-start(bf16[8,160,1536]{2,0,1:T(8,128)(2,1)} %bitcast.211), calls=%async_computation.4 | async-start | bytes 7864320 | tf_op jit(solution)/shard_map/all_to_all | solution.py:240
  288.7 53.1 %all-to-all-start.7 = ((bf16[8,160,1536]{2,0,1:T(8,128)(2,1)}), bf16[8,160,1536]{2,0,1:T(8,128)(2,1)}, u32[]{:S(2)}, u32[]{:S(2)}) async-start(bf16[8,160,1536]{2,0,1:T(8,128)(2,1)} %bitcast.210), calls=%async_computation.7 | async-start | bytes 7864320 | tf_op jit(solution)/shard_map/all_to_all | solution.py:247
  341.7 5.7 %copy-start.22 = (f32[64,8]{0,1:T(8,128)S(1)}, f32[64,8]{0,1:T(8,128)}, u32[]{:S(2)}) copy-start(f32[64,8]{0,1:T(8,128)} %param.34) | copy-start | bytes 6148
  341.7 5.8 %copy-start.12 = (s32[64,8]{1,0:T(8,128)S(1)}, s32[64,8]{1,0:T(8,128)}, u32[]{:S(2)}) copy-start(s32[64,8]{1,0:T(8,128)} %copy-done.11) | copy-start | bytes 6148
  341.8 53.4 %all-to-all-start.5 = ((bf16[8,160,1536]{2,0,1:T(8,128)(2,1)}), bf16[8,160,1536]{2,0,1:T(8,128)(2,1)}, u32[]{:S(2)}, u32[]{:S(2)}) async-start(bf16[8,160,1536]{2,0,1:T(8,128)(2,1)} %bitcast.209), calls=%async_computation.5 | async-start | bytes 7864320 | tf_op jit(solution)/shard_map/all_to_all | solution.py:247
  401.9 2.0 copy-start.1
